TPU v7x, 256 devices: a whole 4x4x8 slice. The times are simulated.
256 devices in a mesh: wide: 32 (over x, y, core), blk: 8 (over z).
Axes of the slice: x: 4, y: 4, z: 8, core: 2. Of those that a mesh axis runs over, the one named last changes fastest.
Arguments:
- tokens: bfloat16 [1024, 8192], P('wide', 'blk'), may hold values from -6 to 6
- target: bfloat16 [1024, 8192], P('wide', 'blk'), may hold values from -3 to 3
- probe_vector: float32 [8192], P('blk'), may hold values from -12 to 12
- weight_in: bfloat16 [256, 8, 2, 128, 128], P('wide', 'blk'), may hold values from -0.375 to 0.375
- weight_out: bfloat16 [256, 8, 2, 128, 128], P('wide', 'blk'), may hold values from -0.09375 to 0.09375
- slot_rows: int32 [256, 8, 2], P('wide', 'blk'), may hold values from 0 to 7, as said below
- slot_count: int32 [256, 8], P('wide', 'blk'), may hold values from 0 to 2, as said below
Outputs:
- outputs: bfloat16 [1024, 8192], P('wide', 'blk')
- token_grad: bfloat16 [1024, 8192], P('wide', 'blk')
- grad_in: float32 [256, 8, 2, 128, 128], P('wide', 'blk')
- grad_out: float32 [256, 8, 2, 128, 128], P('wide', 'blk')
Inputs may be any that keep to these rules, and one draw needn't show every extreme that they name: `slot_rows`: the 2 entries of one (j, g) are distinct feature blocks of the row group. `slot_count`: every hidden block column has 2 used slots in at least one row group.
All inputs are finite; a program needn't handle non-finite values.
Results may differ from a plain program's by a relative error of at most 0.033.
Values may be sent and summed in bfloat16 or wider, within the bound.
No kernel may reach another device: no remote copies, remote signals or barrier semaphores. Data moves between devices by JAX's collectives and lax.ppermute only.
A program may use at most 64 MiB of HBM per device.

v0:
```python
import math

import jax
import jax.numpy as jnp
from jax import lax
from jax.sharding import PartitionSpec as P


def activate(value):
    return jax.nn.gelu(value, approximate=True)


def activate_slope(value):
    return jax.jvp(activate, (value,), (jnp.ones_like(value),))[1]


def row_stride(count, limit):
    return math.gcd(count, limit)


def by_blocks(blockfn, row_count, limit):
    stride = row_stride(row_count, limit)
    pieces = lax.map(
        lambda index: blockfn(index * stride, stride),
        jnp.arange(row_count // stride, dtype=jnp.int32),
    )
    return pieces.reshape((row_count,) + pieces.shape[2:])


def pick_rows(activity, row_index, block):
    row_total = activity.shape[0]
    columns, slots = row_index.shape
    blocks = activity.reshape(row_total, activity.shape[1] // block, block)
    return jnp.take(blocks, row_index.reshape(-1), axis=1).reshape(row_total, columns, slots, block)


def body(tokens, target, probe_vector, weight_in, weight_out, slot_rows, slot_count):
    columns, unit, slots, block, width_two = weight_in.shape
    features = tokens.shape[1]
    feature_blocks = features // block
    row_index = slot_rows[:, 0]
    in_use = lax.broadcasted_iota(jnp.int32, (columns, slots), 1) < slot_count[:, 0][:, None]
    mask_low = in_use.astype(jnp.bfloat16)[:, :, None, None]
    mask_full = in_use.astype(jnp.float32)[:, :, None, None]
    tiles_in = weight_in[:, 0] * mask_low
    tiles_out = weight_out[:, 0] * mask_low
    onehot = (
        row_index[:, :, None]
        == lax.broadcasted_iota(jnp.int32, (columns, slots, feature_blocks), 2)
    ).astype(jnp.float32)
    chosen = jnp.take(
        probe_vector.reshape(feature_blocks, block), row_index.reshape(-1), axis=0
    ).reshape(columns, slots, block)
    image_part = jnp.einsum(
        "jsk,jskn->jn", chosen, tiles_in.astype(jnp.float32), precision=lax.Precision.HIGHEST
    )
    image, norm_probe = lax.psum((image_part, jnp.sum(probe_vector * probe_vector)), "blk")
    norm_image = lax.psum(jnp.sum(image * image), "wide")
    spectral = jnp.sqrt(norm_image / norm_probe)
    x_full = lax.all_gather(tokens, "wide", axis=0, tiled=True)
    all_rows = x_full.shape[0]
    block_rows = all_rows // lax.axis_size("blk")
    owned = tokens.shape[0]

    def hidden_block_term(start_row, count):
        picked = pick_rows(lax.dynamic_slice_in_dim(x_full, start_row, count, 0), row_index, block)
        product = jnp.einsum("tjsk,jskn->tjn", picked, tiles_in, preferred_element_type=jnp.float32)
        return product.reshape(count, columns * block)

    hidden_own = (
        lax.psum_scatter(
            by_blocks(hidden_block_term, block_rows * lax.axis_size("blk"), 512).astype(
                jnp.bfloat16
            ),
            "blk",
            scatter_dimension=0,
            tiled=True,
        ).astype(jnp.float32)
        / spectral
    )
    active_own = activate(hidden_own).astype(jnp.bfloat16)
    active_full = lax.all_gather(active_own, "blk", axis=0, tiled=True)

    def output_block_term(start_row, count):
        active = lax.dynamic_slice_in_dim(active_full, start_row, count, 0).reshape(
            count, columns, block
        )
        contrib = jnp.einsum(
            "tjk,jskn->tjsn", active, tiles_out, preferred_element_type=jnp.float32
        )
        return jnp.einsum("tjsn,jsr->trn", contrib, onehot).reshape(count, features)

    outputs = lax.psum_scatter(
        by_blocks(output_block_term, owned * lax.axis_size("wide"), 256).astype(jnp.bfloat16),
        "wide",
        scatter_dimension=0,
        tiled=True,
    )
    residual = (outputs.astype(jnp.float32) - target.astype(jnp.float32)).astype(jnp.bfloat16)
    error_full = lax.all_gather(residual, "wide", axis=0, tiled=True)

    def back_block_term(start_row, count):
        picked = pick_rows(
            lax.dynamic_slice_in_dim(error_full, start_row, count, 0), row_index, block
        )
        product = jnp.einsum(
            "tjsn,jskn->tjk", picked, tiles_out, preferred_element_type=jnp.float32
        )
        return product.reshape(count, columns * block)

    back_own = lax.psum_scatter(
        by_blocks(back_block_term, block_rows * lax.axis_size("blk"), 512).astype(jnp.bfloat16),
        "blk",
        scatter_dimension=0,
        tiled=True,
    ).astype(jnp.float32)
    slope_own = (back_own * activate_slope(hidden_own)).astype(jnp.bfloat16)
    slope_full = lax.all_gather(slope_own, "blk", axis=0, tiled=True)
    stride = row_stride(all_rows, 256)

    def grads_block(index, totals):
        start_row = index * stride
        picked_in = pick_rows(
            lax.dynamic_slice_in_dim(x_full, start_row, stride, 0), row_index, block
        )
        picked_err = pick_rows(
            lax.dynamic_slice_in_dim(error_full, start_row, stride, 0), row_index, block
        )
        slope = lax.dynamic_slice_in_dim(slope_full, start_row, stride, 0).reshape(
            stride, columns, block
        )
        active = lax.dynamic_slice_in_dim(active_full, start_row, stride, 0).reshape(
            stride, columns, block
        )
        part_in = jnp.einsum("tjsk,tjn->jskn", picked_in, slope, preferred_element_type=jnp.float32)
        part_out = jnp.einsum(
            "tjk,tjsn->jskn", active, picked_err, preferred_element_type=jnp.float32
        )
        return (totals[0] + part_in, totals[1] + part_out)

    empty = jnp.zeros((columns, slots, block, block), jnp.float32)
    raw_in, raw_out = lax.fori_loop(0, all_rows // stride, grads_block, (empty, empty))
    raw_in = raw_in * mask_full
    grad_out = raw_out * mask_full
    curvature = lax.psum(jnp.sum(raw_in * tiles_in.astype(jnp.float32)), ("wide", "blk"))
    outer = jnp.einsum("jsk,jn->jskn", chosen, image) * mask_full
    grad_in = raw_in / spectral - curvature / (spectral**3 * norm_probe) * outer

    def input_block_term(start_row, count):
        slope = lax.dynamic_slice_in_dim(slope_full, start_row, count, 0).reshape(
            count, columns, block
        )
        contrib = jnp.einsum("tjn,jskn->tjsk", slope, tiles_in, preferred_element_type=jnp.float32)
        return jnp.einsum("tjsk,jsr->trk", contrib, onehot).reshape(count, features)

    token_grad = (
        lax.psum_scatter(
            by_blocks(input_block_term, owned * lax.axis_size("wide"), 256).astype(jnp.bfloat16),
            "wide",
            scatter_dimension=0,
            tiled=True,
        ).astype(jnp.float32)
        / spectral
    ).astype(jnp.bfloat16)
    return (outputs, token_grad, grad_in[:, None], grad_out[:, None])


def solution(mesh):
    in_specs = (
        P("wide", "blk"),
        P("wide", "blk"),
        P("blk"),
        P("wide", "blk", None, None, None),
        P("wide", "blk", None, None, None),
        P("wide", "blk", None),
        P("wide", "blk"),
    )
    out_specs = (
        P("wide", "blk"),
        P("wide", "blk"),
        P("wide", "blk", None, None, None),
        P("wide", "blk", None, None, None),
    )
    return jax.shard_map(body, mesh=mesh, in_specs=in_specs, out_specs=out_specs, check_vma=False)
```

profile of v0, /device:TPU:32, one launch (start us, length us, event | category | flops | bytes accessed | tf_op | source)
XLA Modules:
  0.0 650.4 jit_solution(13190907771488800029)
XLA Ops:
  9.5 2.1 bitcast_multiply_fusion
  12.7 49.4 %all-gather.5.cloned.1.call-done = bf16[1024,1024]{1,0:T(8,128)(2,1)} async-done(((bf16[32,1024]{1,0:T(8,128)(2,1)}), bf16[1024,1024]{1,0:T(8,128)(2,1)}) %all-gather.5.cloned.1.call-update) | async-done | bytes 2097168 | tf_op jit(solution)/shard_map/all_gather | solution.py:60
  62.0 3.9 copy.95
  67.5 15.2 %while.63 = (s32[]{:T(128)}, bf16[2,512,1024]{1,2,0:T(8,128)(2,1)}, s32[2]{0:T(128)S(1)}, bf16[1024,1024]{0,1:T(8,128)(2,1)}, s32[8,1,2]{2,0,1:T(8,128)}, /*inde...) while((s32[]{:T(128)}, bf16[2,512,1024]{1,2,0:T(8,128)(2,1)}, ...), condition=%wide.wide.region_1.3_spmd, body=%wide.wide.region_0.0_spmd.sunk | while | flops 269485216 | bytes 37229152 | solution.py:23
  82.7 3.9 copy.132
  89.1 17.2 %all-reduce = (f32[8,128]{1,0:T(8,128)S(1)}, f32[]{:T(128)}) all-reduce(f32[8,128]{1,0:T(8,128)S(1)} %bitcast.244, f32[]{:T(128)} %multiply_reduce_fusion.1), channel_id=1, replica_groups=mesh['wide'=32,'blk'=8] {'blk'}, use_global_device_ids=true, to_apply=%region_3.5 | all-reduce | flops 1025 | bytes 8200 | tf_op jit(solution)/shard_map/psum | solution.py:57
  106.9 63.3 %psum.29 = f32[]{:T(128)} all-reduce(f32[]{:T(128)} %multiply_reduce_fusion.2), channel_id=1, replica_groups=mesh['wide'=32,'blk'=8] {'wide'}, use_global_device_ids=true, to_apply=%region_5.7 | all-reduce | flops 1 | bytes 8 | tf_op jit(solution)/shard_map/psum | solution.py:58
  173.6 42.4 %all-gather.7.cloned.1.call-done = bf16[1024,1024]{0,1:T(8,128)(2,1)} async-done(((bf16[128,1024]{0,1:T(8,128)(2,1)}), bf16[1024,1024]{0,1:T(8,128)(2,1)}) %all-gather.7.cloned.1.call-update) | async-done | bytes 2097168 | tf_op jit(solution)/shard_map/all_gather | solution.py:82
  217.7 18.3 %while.61 = (s32[]{:T(128)}, bf16[4,256,1024]{2,1,0:T(8,128)(2,1)}, s32[4]{0:T(128)S(1)}, bf16[1024,1024]{0,1:T(8,128)(2,1)}, bf16[8,2,128,128]{3,2,1,0:T(8,128)...) while((s32[]{:T(128)}, bf16[4,256,1024]{2,1,0:T(8,128)(2,1)}, ...), condition=%wide.region_9.11_spmd.clone, body=%wide.region_8.10_spmd.clone.sunk | while | flops 142606592 | bytes 6816483 | solution.py:23
  236.0 85.6 %reduce-scatter.9.cloned.1.call-done = bf16[32,1024]{1,0:T(8,128)(2,1)} async-done(((bf16[1024,1024]{1,0:T(8,128)(2,1)}), bf16[32,1024]{1,0:T(8,128)(2,1)}) %reduce-scatter.9.cloned.1.call-update) | async-done | bytes 65552 | tf_op jit(solution)/shard_map/reduce_scatter | solution.py:93
  323.3 49.6 %all-gather.9.cloned.1.call-done = bf16[1024,1024]{1,0:T(8,128)(2,1)} async-done(((bf16[32,1024]{1,0:T(8,128)(2,1)}), bf16[1024,1024]{1,0:T(8,128)(2,1)}) %all-gather.9.cloned.1.call-update) | async-done | bytes 2097168 | tf_op jit(solution)/shard_map/all_gather | solution.py:100
  372.9 3.9 copy.101
  378.4 15.5 %while.64 = (s32[]{:T(128)}, bf16[2,512,1024]{1,2,0:T(8,128)(2,1)}, s32[2]{0:T(128)S(1)}, bf16[1024,1024]{0,1:T(8,128)(2,1)}, s32[8,1,2]{2,0,1:T(8,128)}, /*inde...) while((s32[]{:T(128)}, bf16[2,512,1024]{1,2,0:T(8,128)(2,1)}, ...), condition=%wide.wide.region_12.14_spmd, body=%wide.wide.region_11.13_spmd.sunk | while | flops 269485216 | bytes 39326336 | solution.py:23
  393.9 4.0 copy.133
  397.9 41.1 %reduce-scatter.15.cloned.1.call-done = bf16[128,1024]{1,0:T(8,128)(2,1)} async-done(((bf16[1024,1024]{1,0:T(8,128)(2,1)}), bf16[128,1024]{1,0:T(8,128)(2,1)}) %reduce-scatter.15.cloned.1.call-update) | async-done | bytes 262160
  441.6 46.5 %all-gather.11.cloned.1.call-done = bf16[1024,1024]{0,1:T(8,128)(2,1)} async-done(((bf16[128,1024]{0,1:T(8,128)(2,1)}), bf16[1024,1024]{0,1:T(8,128)(2,1)}) %all-gather.11.cloned.1.call-update) | async-done | bytes 2097168 | tf_op jit(solution)/shard_map/all_gather | solution.py:118
  489.7 18.8 %while.62 = (s32[]{:T(128)}, bf16[4,256,1024]{2,1,0:T(8,128)(2,1)}, s32[4]{0:T(128)S(1)}, bf16[1024,1024]{0,1:T(8,128)(2,1)}, bf16[8,2,128,128]{3,2,1,0:T(8,128)...) while((s32[]{:T(128)}, bf16[4,256,1024]{2,1,0:T(8,128)(2,1)}, ...), condition=%wide.region_15.17_spmd.clone, body=%wide.region_14.16_spmd.clone.sunk | while | flops 142606592 | bytes 6816483 | solution.py:23
  508.6 51.7 %while.65 = (s32[]{:T(128)}, f32[8,2,128,128]{3,2,1,0:T(8,128)}, f32[8,2,128,128]{2,3,1,0:T(8,128)}, bf16[1024,1024]{0,1:T(8,128)(2,1)}, s32[8,1,2]{2,0,1:T(8,12...) while((s32[]{:T(128)}, f32[8,2,128,128]{3,2,1,0:T(8,128)}, ...), condition=%wide.wide.region_18.21_spmd.clone, body=%wide.wide.region_17.20_spmd.clone.sunk | while | flops 270533760 | bytes 28316308 | solution.py:142
  508.6 2.1 constant_dynamic-slice_fusion.22
  516.1 2.6 fusion.105
  520.3 2.1 constant_dynamic-slice_fusion.22
  527.9 3.0 fusion.105
  530.9 2.7 convolution_add_fusion.3
  533.6 2.1 constant_dynamic-slice_fusion.22
  541.2 3.0 fusion.105
  544.2 2.7 convolution_add_fusion.3
  546.9 2.1 constant_dynamic-slice_fusion.22
  554.4 3.0 fusion.105
  557.4 2.8 convolution_add_fusion.3
  560.2 2.4 multiply_reduce_fusion
  563.2 74.9 %psum.31 = f32[]{:T(128)} all-reduce(f32[]{:T(128)} %multiply_reduce_fusion), channel_id=1, replica_groups=mesh['wide'=32,'blk'=8] {'wide','blk'}, use_global_device_ids=true, to_apply=%region_20.23 | all-reduce | flops 1 | bytes 8 | tf_op jit(solution)/shard_map/psum | solution.py:145
  639.1 2.9 multiply_bitcast_fusion
  (242 shorter events, 103.2 us)
Async XLA Ops:
  7.2 54.9 %all-gather.5.cloned.1.call-start = ((), (), s32[]{:S(2)}) async-start(), calls=%async_computation.4 | async-start | bytes 2162688 | tf_op jit(solution)/shard_map/all_gather | solution.py:60
  7.9 163.6 %reduce-scatter.13.cloned.1.call-start = ((), (), s32[]{:S(2)}) async-start(), calls=%async_computation.10 | async-start | bytes 2359296
  8.7 57.3 %copy-start.16 = (s32[8,1,2]{2,0,1:T(8,128)}, s32[8,1,2]{2,0,1:T(8,128)S(1)}, u32[]{:S(2)}) copy-start(s32[8,1,2]{2,0,1:T(8,128)S(1)} %copy.96) | copy-start | bytes 196
  11.6 55.8 %copy-start.5 = (bf16[8,2,128,128]{3,2,1,0:T(8,128)(2,1)}, bf16[8,2,128,128]{3,2,1,0:T(8,128)(2,1)S(1)}, u32[]{:S(2)}) copy-start(bf16[8,2,128,128]{3,2,1,0:T(8,128)(2,1)S(1)} %get-tuple-element.952) | copy-start | bytes 1572868
  72.0 1.6 copy-start.10
  79.6 1.6 copy-start.10
  86.6 2.1 copy-start.6
  86.6 131.0 %copy-start.1 = (bf16[8,2,128,128]{3,2,1,0:T(8,128)(2,1)S(1)}, bf16[8,2,128,128]{3,2,1,0:T(8,128)(2,1)}, u32[]{:S(2)}) copy-start(bf16[8,2,128,128]{3,2,1,0:T(8,128)(2,1)} %get-tuple-element.920) | copy-start | bytes 1572868
  86.7 129.4 %all-gather.7.cloned.1.call-start = ((), (), s32[]{:S(2)}) async-start(), calls=%async_computation.5 | async-start | bytes 2359296 | tf_op jit(solution)/shard_map/all_gather | solution.py:82
  173.6 148.0 %reduce-scatter.9.cloned.1.call-start = ((), (), s32[]{:S(2)}) async-start(), calls=%async_computation.6 | async-start | bytes 2162688 | tf_op jit(solution)/shard_map/reduce_scatter | solution.py:93
  235.9 85.7 %copy-start.19 = (bf16[32,1024]{1,0:T(8,128)(2,1)S(1)}, bf16[32,1024]{1,0:T(8,128)(2,1)}, u32[]{:S(2)}) copy-start(bf16[32,1024]{1,0:T(8,128)(2,1)} %param.22) | copy-start | bytes 196612
  236.0 136.9 %all-gather.9.cloned.1.call-start = ((), (), s32[]{:S(2)}) async-start(), calls=%async_computation.7 | async-start | bytes 2162688 | tf_op jit(solution)/shard_map/all_gather | solution.py:100
  323.1 115.9 %reduce-scatter.15.cloned.1.call-start = ((), (), s32[]{:S(2)}) async-start(), calls=%async_computation.11 | async-start | bytes 2359296
  378.4 2.6 copy-start.2
  383.0 1.6 copy-start.12
  384.7 1.4 copy-start.13
  386.1 2.6 copy-start.2
  390.7 1.6 copy-start.12
  392.5 1.4 copy-start.13
  397.8 43.6 %copy-start.18 = (s32[8,1,2]{2,0,1:T(8,128)S(1)}, s32[8,1,2]{2,0,1:T(8,128)}, u32[]{:S(2)}) copy-start(s32[8,1,2]{2,0,1:T(8,128)} %get-tuple-element.1050) | copy-start | bytes 196
  397.9 91.9 %copy-start.7 = (bf16[8,2,128,128]{3,2,1,0:T(8,128)(2,1)S(1)}, bf16[8,2,128,128]{3,2,1,0:T(8,128)(2,1)}, u32[]{:S(2)}) copy-start(bf16[8,2,128,128]{3,2,1,0:T(8,128)(2,1)} %copy-done.5) | copy-start | bytes 1572868
  397.9 90.2 %all-gather.11.cloned.1.call-start = ((), (), s32[]{:S(2)}) async-start(), calls=%async_computation.8 | async-start | bytes 2359296 | tf_op jit(solution)/shard_map/all_gather | solution.py:118
  441.2 200.8 %reduce-scatter.11.cloned.1.call-start = ((), (), s32[]{:S(2)}) async-start(), calls=%async_computation.9 | async-start | bytes 2162688 | tf_op jit(solution)/shard_map/reduce_scatter | solution.py:157
  516.1 2.6 copy-start
  516.1 2.6 copy-start.4
  527.9 3.0 copy-start
  527.9 3.0 copy-start.4
  541.2 3.0 copy-start
  541.2 3.0 copy-start.4
  554.4 3.0 copy-start
  554.4 3.0 copy-start.4
  560.2 77.9 %copy-start.8 = (f32[8,2,128,128]{2,3,1,0:T(8,128)S(1)}, f32[8,2,128,128]{2,3,1,0:T(8,128)}, u32[]{:S(2)}) copy-start(f32[8,2,128,128]{2,3,1,0:T(8,128)} %get-tuple-element.279) | copy-start | bytes 3145732
  (9 other events, 9.2 us)
Sparse Core Ops, SparseCore 0:
  10.6 51.4 all-gather.4
  86.8 41.2 reduce-scatter.12
  173.7 42.2 all-gather.6
  236.1 85.4 reduce-scatter.8
  324.6 48.2 all-gather.8
  398.0 40.9 reduce-scatter.14
  441.4 46.6 all-gather.10
  508.7 85.4 reduce-scatter.10
where the time goes:
time: 654 us; the launch traced here: 650 us
  waiting for transfers between devices  315 us (48%)
  blocking collectives  155 us (24%)
  local copies, waits for them, and re-layouts  98.7 us (15%)
  matrix products  34.1 us (5%)
  other arithmetic  20.6 us (3%)
  between operations  16.8 us (3%)
  loops' own time  8.79 us (1%)
    reduce_scatter x1, waiting for transfers between devices, body(): lax.psum_scatter(by_blocks(output_block_term, owned * lax.axis_size('wide...  85.6 us
    psum x1, blocking collectives, body(): lax.psum(jnp.sum(raw_in * tiles_in.astype(jnp.float32)), ('wide', 'blk'))  74.9 us
    psum x1, blocking collectives, body(): norm_image = lax.psum(jnp.sum(image * image), 'wide')  63.3 us
    all_gather x1, waiting for transfers between devices, body(): error_full = lax.all_gather(residual, 'wide', axis=0, tiled=True)  49.6 us
    all_gather x1, waiting for transfers between devices, body(): x_full = lax.all_gather(tokens, 'wide', axis=0, tiled=True)  49.4 us
    all_gather x1, waiting for transfers between devices, body(): slope_full = lax.all_gather(slope_own, 'blk', axis=0, tiled=True)  46.5 us
    all_gather x1, waiting for transfers between devices, body(): active_full = lax.all_gather(active_own, 'blk', axis=0, tiled=True)  42.4 us
    unnamed x10, waiting for transfers between devices  41.9 us
  transfers between devices with their start and end apart: 8, of which 6 were waited for; matrix products, arithmetic and copies ran while one was open for 10% of the time, Pallas kernels for 0%

commit v1 on v0

v1 whole, which is shorter than its diff:
```python
import jax
import jax.numpy as jnp
from jax import lax
from jax.sharding import PartitionSpec as P


def activate(value):
    return jax.nn.gelu(value, approximate=True)


def activate_slope(value):
    return jax.jvp(activate, (value,), (jnp.ones_like(value),))[1]


def spread_tiles(tiles, row_index, feature_blocks):
    rows = lax.broadcasted_iota(jnp.int32, (feature_blocks,) + row_index.shape, 0)
    hit = rows == row_index[None]
    zero = jnp.zeros((), tiles.dtype)
    dense = jnp.where(hit[:, :, 0, None, None], tiles[None, :, 0], zero)
    for slot in range(1, row_index.shape[1]):
        dense = dense + jnp.where(hit[:, :, slot, None, None], tiles[None, :, slot], zero)
    return jnp.transpose(dense, (0, 2, 1, 3))


def pick_tiles(dense, row_index):
    feature_blocks = dense.shape[0]
    rows = lax.broadcasted_iota(jnp.int32, (feature_blocks,) + row_index.shape, 0)
    hit = rows == row_index[None]
    by_col = jnp.transpose(dense, (0, 2, 1, 3))
    picked = jnp.zeros(row_index.shape + dense.shape[1:2] + dense.shape[3:4], dense.dtype)
    for r in range(feature_blocks):
        picked = picked + jnp.where(hit[r][:, :, None, None], by_col[r][:, None], 0.0)
    return picked


def body(tokens, target, probe_vector, weight_in, weight_out, slot_rows, slot_count):
    columns, unit, slots, block, width_two = weight_in.shape
    features = tokens.shape[1]
    feature_blocks = features // block
    hidden_width = columns * block
    row_index = slot_rows[:, 0]
    in_use = lax.broadcasted_iota(jnp.int32, (columns, slots), 1) < slot_count[:, 0][:, None]
    mask_low = in_use.astype(jnp.bfloat16)[:, :, None, None]
    mask_full = in_use.astype(jnp.float32)[:, :, None, None]
    tiles_in = weight_in[:, 0] * mask_low
    tiles_out = weight_out[:, 0] * mask_low
    chosen = jnp.take(
        probe_vector.reshape(feature_blocks, block), row_index.reshape(-1), axis=0
    ).reshape(columns, slots, block)
    image_part = jnp.einsum(
        "jsk,jskn->jn", chosen, tiles_in.astype(jnp.float32), precision=lax.Precision.HIGHEST
    )
    image, norm_probe = lax.psum((image_part, jnp.sum(probe_vector * probe_vector)), "blk")
    norm_image = lax.psum(jnp.sum(image * image), "wide")
    spectral = jnp.sqrt(norm_image / norm_probe)

    w1 = spread_tiles(tiles_in, row_index, feature_blocks).reshape(features, hidden_width)
    w2 = jnp.transpose(
        spread_tiles(tiles_out, row_index, feature_blocks), (2, 1, 0, 3)
    ).reshape(hidden_width, features)

    x_full = lax.all_gather(tokens, "wide", axis=0, tiled=True)
    x_full, spectral = lax.optimization_barrier((x_full, spectral))

    pre_part = jnp.dot(x_full, w1, preferred_element_type=jnp.float32)
    pre_own = lax.psum_scatter(
        pre_part.astype(jnp.bfloat16), "blk", scatter_dimension=0, tiled=True
    ).astype(jnp.float32)
    hidden_own = pre_own / spectral
    active_own = activate(hidden_own).astype(jnp.bfloat16)
    active_full = lax.all_gather(active_own, "blk", axis=0, tiled=True)

    out_part = jnp.dot(active_full, w2, preferred_element_type=jnp.float32)
    outputs = lax.psum_scatter(
        out_part.astype(jnp.bfloat16), "wide", scatter_dimension=0, tiled=True
    )
    residual = (outputs.astype(jnp.float32) - target.astype(jnp.float32)).astype(jnp.bfloat16)
    error_full = lax.all_gather(residual, "wide", axis=0, tiled=True)

    back_part = lax.dot_general(
        error_full, w2, (((1,), (1,)), ((), ())), preferred_element_type=jnp.float32
    )
    back_own = lax.psum_scatter(
        back_part.astype(jnp.bfloat16), "blk", scatter_dimension=0, tiled=True
    ).astype(jnp.float32)
    slope_own = (back_own * activate_slope(hidden_own)).astype(jnp.bfloat16)
    curvature = lax.psum(jnp.sum(slope_own.astype(jnp.float32) * pre_own), ("wide", "blk"))
    slope_full = lax.all_gather(slope_own, "blk", axis=0, tiled=True)

    in_part = lax.dot_general(
        slope_full, w1, (((1,), (1,)), ((), ())), preferred_element_type=jnp.float32
    )
    token_grad = (
        lax.psum_scatter(in_part.astype(jnp.bfloat16), "wide", scatter_dimension=0, tiled=True)
        .astype(jnp.float32)
        / spectral
    ).astype(jnp.bfloat16)

    g1 = lax.dot_general(
        x_full, slope_full, (((0,), (0,)), ((), ())), preferred_element_type=jnp.float32
    )
    raw_in = pick_tiles(g1.reshape(feature_blocks, block, columns, block), row_index) * mask_full
    g2 = lax.dot_general(
        error_full, active_full, (((0,), (0,)), ((), ())), preferred_element_type=jnp.float32
    )
    grad_out = pick_tiles(g2.reshape(feature_blocks, block, columns, block), row_index) * mask_full
    grad_out = jnp.transpose(grad_out, (0, 1, 3, 2))

    outer = jnp.einsum("jsk,jn->jskn", chosen, image) * mask_full
    grad_in = raw_in / spectral - curvature / (spectral**3 * norm_probe) * outer
    return (outputs, token_grad, grad_in[:, None], grad_out[:, None])


def solution(mesh):
    in_specs = (
        P("wide", "blk"),
        P("wide", "blk"),
        P("blk"),
        P("wide", "blk", None, None, None),
        P("wide", "blk", None, None, None),
        P("wide", "blk", None),
        P("wide", "blk"),
    )
    out_specs = (
        P("wide", "blk"),
        P("wide", "blk"),
        P("wide", "blk", None, None, None),
        P("wide", "blk", None, None, None),
    )
    return jax.shard_map(body, mesh=mesh, in_specs=in_specs, out_specs=out_specs, check_vma=False)
```

time: 654 us -> 537 us (0.82)
  local copies, waits for them, and re-layouts: 98.7 us -> 18.2 us
  waiting for transfers between devices: 315 us -> 290 us
  loops' own time: 8.79 us -> 0 us
    reduce_scatter x2 -> x4, waiting for transfers between devices: 85.6 us -> 163 us  [the longest x1 85.4 us: body(): lax.psum_scatter(out_part.astype(jnp.bfloat16), 'wide', scatter_dimension...]
    all_gather x1, waiting for transfers between devices: 49.4 us -> 0.02 us  [body(): x_full = lax.all_gather(tokens, 'wide', axis=0, tiled=True)]
    unnamed x10 -> x8, waiting for transfers between devices: 41.9 us -> 0.8 us
    dynamic_slice x32 -> x0, local copies, waits for them, and re-layouts: 38.2 us -> none  [the longest x4 8.53 us: grads_block(): lax.dynamic_slice_in_dim(active_full, start_row, stride, 0)]
    while x49 -> x0, local copies, waits for them, and re-layouts: 18.7 us -> none  [the longest x4 9.64 us: by_blocks(): lax.map(lambda index: blockfn(index * stride, stride), jnp.arange(row_cou...]
    broadcast_in_dim x8 -> x32, local copies, waits for them, and re-layouts: 1.82 us -> 11.9 us  [the longest x26 11.2 us: pick_tiles(): jnp.where(hit[r][:, :, None, None], by_col[r][:, None], 0.0)]
    gather x12 -> x0, local copies, waits for them, and re-layouts: 9.81 us -> none  [pick_rows(): jnp.take(blocks, row_index.reshape(-1), axis=1)]
    another operation x5 -> x0, loops' own time: 8.79 us -> none  [the longest x4 8.56 us: by_blocks(): lax.map(lambda index: blockfn(index * stride, stride), jnp.arange(row_cou...]
  transfers between devices with their start and end apart: 8 -> 8, of which waited for: 6 -> 6; matrix products, arithmetic and copies ran while one was open for 10% -> 7% of each run, Pallas kernels for 0% -> 0%
where the time goes in v1:
time: 537 us; the launch traced here: 535 us
  waiting for transfers between devices  290 us (54%)
  blocking collectives  158 us (29%)
  matrix products  31.3 us (6%)
  other arithmetic  19.8 us (4%)
  local copies, waits for them, and re-layouts  18.2 us (3%)
  between operations  17.1 us (3%)
    reduce_scatter x1, waiting for transfers between devices, body(): lax.psum_scatter(out_part.astype(jnp.bfloat16), 'wide', scatter_dimension...  85.4 us
    psum x1, blocking collectives, body(): lax.psum(jnp.sum(slope_own.astype(jnp.float32) * pre_own), ('wide', 'blk'))  75 us
    psum x1, blocking collectives, body(): norm_image = lax.psum(jnp.sum(image * image), 'wide')  64.7 us
    all_gather x1, waiting for transfers between devices, body(): error_full = lax.all_gather(residual, 'wide', axis=0, tiled=True)  49.7 us
    reduce_scatter x1, waiting for transfers between devices, body(): lax.psum_scatter(back_part.astype(jnp.bfloat16), 'blk', scatter_dimension...  41.2 us
    all_gather x1, waiting for transfers between devices, body(): active_full = lax.all_gather(active_own, 'blk', axis=0, tiled=True)  38.3 us
    all_gather x1, waiting for transfers between devices, body(): slope_full = lax.all_gather(slope_own, 'blk', axis=0, tiled=True)  38.3 us
    reduce_scatter x1, waiting for transfers between devices, body(): lax.psum_scatter(pre_part.astype(jnp.bfloat16), 'blk', scatter_dimension=...  36.2 us
  transfers between devices with their start and end apart: 8, of which 6 were waited for; matrix products, arithmetic and copies ran while one was open for 7% of the time, Pallas kernels for 0%

profile of v1, /device:TPU:32, one launch (start us, length us, event | category | flops | bytes accessed | tf_op | source)
XLA Modules:
  0.0 535.2 jit_solution(15255143224916321714)
XLA Ops:
  9.6 1.2 gather_fusion
  10.8 1.3 multiply_reduce_fusion
  12.9 1.3 bitcast_multiply_fusion
  14.6 18.8 %all-reduce = (f32[8,128]{1,0:T(8,128)S(1)}, f32[]{:T(128)}) all-reduce(f32[8,128]{1,0:T(8,128)S(1)} %bitcast.156, f32[]{:T(128)} %multiply_reduce_fusion), channel_id=1, replica_groups=mesh['wide'=32,'blk'=8] {'blk'}, use_global_device_ids=true, to_apply=%region_0.1 | all-reduce | flops 1025 | bytes 8200 | tf_op jit(solution)/shard_map/psum | solution.py:53
  34.0 64.7 %psum.29 = f32[]{:T(128)} all-reduce(f32[]{:T(128)} %multiply_reduce_fusion.1), channel_id=1, replica_groups=mesh['wide'=32,'blk'=8] {'wide'}, use_global_device_ids=true, to_apply=%region_2.3 | all-reduce | flops 1 | bytes 8 | tf_op jit(solution)/shard_map/psum | solution.py:54
  101.0 5.2 fusion.8
  106.3 36.2 %reduce-scatter.5.cloned.1.call-done = bf16[128,1024]{1,0:T(8,128)(2,1)} async-done(((bf16[1024,1024]{1,0:T(8,128)(2,1)}), bf16[128,1024]{1,0:T(8,128)(2,1)}) %reduce-scatter.5.cloned.1.call-update) | async-done | bytes 262160 | tf_op jit(solution)/shard_map/reduce_scatter | solution.py:66
  142.4 1.9 multiply_convert_fusion
  144.5 1.9 select_add_fusion
  146.5 38.3 %all-gather.7.cloned.1.call-done = bf16[1024,1024]{1,0:T(8,128)(2,1)} async-done(((bf16[128,1024]{1,0:T(8,128)(2,1)}), bf16[1024,1024]{1,0:T(8,128)(2,1)}) %all-gather.7.cloned.1.call-update) | async-done | bytes 2097168 | tf_op jit(solution)/shard_map/all_gather | solution.py:71
  184.8 5.9 %fusion.14 = bf16[1024,1024]{1,0:T(8,128)(2,1)} fusion(bf16[1024,1024]{1,0:T(8,128)(2,1)} %all-gather.7.cloned.1.call-done, bf16[128,8,8,128]{3,2,1,0:T(8,128)(2,1)} %bitcast.151), kind=kOutput, calls=%fused_computation.17 | convolution fusion | flops 2148532224 | bytes 6291456 | tf_op jit(solution)/shard_map/dot_general | solution.py:73
  190.8 85.4 %reduce-scatter.7.cloned.1.call-done = bf16[32,1024]{1,0:T(8,128)(2,1)} async-done(((bf16[1024,1024]{1,0:T(8,128)(2,1)}), bf16[32,1024]{1,0:T(8,128)(2,1)}) %reduce-scatter.7.cloned.1.call-update) | async-done | bytes 65552 | tf_op jit(solution)/shard_map/reduce_scatter | solution.py:74
  276.2 1.5 subtract_convert_fusion
  277.7 49.7 %all-gather.9.cloned.1.call-done = bf16[1024,1024]{1,0:T(8,128)(2,1)} async-done(((bf16[32,1024]{1,0:T(8,128)(2,1)}), bf16[1024,1024]{1,0:T(8,128)(2,1)}) %all-gather.9.cloned.1.call-update) | async-done | bytes 2097168 | tf_op jit(solution)/shard_map/all_gather | solution.py:78
  327.5 5.9 %fusion.17 = bf16[1024,1024]{1,0:T(8,128)(2,1)} fusion(bf16[1024,1024]{1,0:T(8,128)(2,1)} %all-gather.9.cloned.1.call-done, bf16[128,8,8,128]{3,2,1,0:T(8,128)(2,1)} %bitcast.152), kind=kOutput, calls=%fused_computation.18 | convolution fusion | flops 2148532224 | bytes 6291456 | tf_op jit(solution)/shard_map/dot_general | solution.py:80
  333.5 41.2 %reduce-scatter.9.cloned.1.call-done = bf16[128,1024]{1,0:T(8,128)(2,1)} async-done(((bf16[1024,1024]{1,0:T(8,128)(2,1)}), bf16[128,1024]{1,0:T(8,128)(2,1)}) %reduce-scatter.9.cloned.1.call-update) | async-done | bytes 262160 | tf_op jit(solution)/shard_map/reduce_scatter | solution.py:83
  374.7 2.7 fusion.24
  379.0 38.3 %all-gather.11.cloned.1.call-done = bf16[1024,1024]{1,0:T(8,128)(2,1)} async-done(((bf16[128,1024]{1,0:T(8,128)(2,1)}), bf16[1024,1024]{1,0:T(8,128)(2,1)}) %all-gather.11.cloned.1.call-update) | async-done | bytes 2097168 | tf_op jit(solution)/shard_map/all_gather | solution.py:88
  417.3 5.3 fusion.11
  422.7 1.6 copy-done.4
  424.2 4.0 convolution_bitcast_fusion
  429.5 1.3 slice_bitcast_fusion.7
  431.3 1.2 copy.82
  432.5 2.0 copy.80
  434.5 2.0 copy.78
  436.6 1.0 copy.76
  437.6 1.0 copy.74
  438.9 3.1 add_multiply_fusion
  442.0 75.0 %psum.31 = f32[]{:T(128)} all-reduce(f32[]{:T(128)} %get-tuple-element.10), channel_id=1, replica_groups=mesh['wide'=32,'blk'=8] {'wide','blk'}, use_global_device_ids=true, to_apply=%region_10.11 | all-reduce | flops 1 | bytes 8 | tf_op jit(solution)/shard_map/psum | solution.py:87
  517.6 4.6 convolution_bitcast_fusion.1
  524.7 2.1 subtract_bitcast_fusion
  526.8 1.5 divide_convert_fusion
  (70 shorter events, 10.8 us)
Async XLA Ops:
  7.2 93.8 %all-gather.5.cloned.1.call-start = ((), (), s32[]{:S(2)}) async-start(), calls=%async_computation.4 | async-start | bytes 2162688 | tf_op jit(solution)/shard_map/all_gather | solution.py:62
  7.9 134.5 %reduce-scatter.5.cloned.1.call-start = ((), (), s32[]{:S(2)}) async-start(), calls=%async_computation.5 | async-start | bytes 2359296 | tf_op jit(solution)/shard_map/reduce_scatter | solution.py:66
  14.3 86.2 %copy-start.3 = (s32[8,1,2]{0,2,1:T(2,128)S(1)}, s32[8,1,2]{0,2,1:T(2,128)}, u32[]{:S(2)}) copy-start(s32[8,1,2]{0,2,1:T(2,128)} %param.12) | copy-start | bytes 196
  106.2 78.6 %all-gather.7.cloned.1.call-start = ((), (), s32[]{:S(2)}) async-start(), calls=%async_computation.6 | async-start | bytes 2359296 | tf_op jit(solution)/shard_map/all_gather | solution.py:71
  144.3 131.9 %reduce-scatter.7.cloned.1.call-start = ((), (), s32[]{:S(2)}) async-start(), calls=%async_computation.7 | async-start | bytes 2162688 | tf_op jit(solution)/shard_map/reduce_scatter | solution.py:74
  190.7 85.4 %copy-start.2 = (bf16[32,1024]{1,0:T(8,128)(2,1)S(1)}, bf16[32,1024]{1,0:T(8,128)(2,1)}, u32[]{:S(2)}) copy-start(bf16[32,1024]{1,0:T(8,128)(2,1)} %param.8) | copy-start | bytes 196612
  190.7 136.7 %all-gather.9.cloned.1.call-start = ((), (), s32[]{:S(2)}) async-start(), calls=%async_computation.8 | async-start | bytes 2162688 | tf_op jit(solution)/shard_map/all_gather | solution.py:78
  277.7 97.0 %reduce-scatter.9.cloned.1.call-start = ((), (), s32[]{:S(2)}) async-start(), calls=%async_computation.9 | async-start | bytes 2359296 | tf_op jit(solution)/shard_map/reduce_scatter | solution.py:83
  333.4 41.2 %copy-start.1 = (bf16[128,1024]{1,0:T(8,128)(2,1)S(1)}, bf16[128,1024]{1,0:T(8,128)(2,1)}, u32[]{:S(2)}) copy-start(bf16[128,1024]{1,0:T(8,128)(2,1)} %reduce-scatter.5.cloned.1.call-done) | copy-start | bytes 786436
  333.4 83.9 %all-gather.11.cloned.1.call-start = ((), (), s32[]{:S(2)}) async-start(), calls=%async_computation.10 | async-start | bytes 2359296 | tf_op jit(solution)/shard_map/all_gather | solution.py:88
  377.3 149.5 %reduce-scatter.11.cloned.1.call-start = ((), (), s32[]{:S(2)}) async-start(), calls=%async_computation.11 | async-start | bytes 2162688 | tf_op jit(solution)/shard_map/reduce_scatter | solution.py:94
  422.6 1.6 copy-start.4
  437.6 1.3 copy-start
Sparse Core Ops, SparseCore 0:
  10.6 51.4 all-gather.4
  106.3 36.0 reduce-scatter.4
  144.8 39.9 all-gather.6
  190.9 85.2 reduce-scatter.6
  279.1 48.2 all-gather.8
  333.6 41.0 reduce-scatter.8
  377.5 39.8 all-gather.10
  422.8 85.2 reduce-scatter.10

commit v2 on v1

--- a/solution.py
+++ b/solution.py
@@ -33,6 +33,15 @@
     return picked
 
 
+def butterfly_sum(value, axis):
+    size = lax.axis_size(axis)
+    step = 1
+    while step < size:
+        value = value + lax.ppermute(value, axis, [(i, i ^ step) for i in range(size)])
+        step *= 2
+    return value
+
+
 def body(tokens, target, probe_vector, weight_in, weight_out, slot_rows, slot_count):
     columns, unit, slots, block, width_two = weight_in.shape
     features = tokens.shape[1]
@@ -50,8 +59,12 @@
     image_part = jnp.einsum(
         "jsk,jskn->jn", chosen, tiles_in.astype(jnp.float32), precision=lax.Precision.HIGHEST
     )
-    image, norm_probe = lax.psum((image_part, jnp.sum(probe_vector * probe_vector)), "blk")
-    norm_image = lax.psum(jnp.sum(image * image), "wide")
+    image_and_norm = butterfly_sum(
+        jnp.concatenate([image_part.reshape(-1), jnp.sum(probe_vector * probe_vector)[None]]), "blk"
+    )
+    image = image_and_norm[:-1].reshape(image_part.shape)
+    norm_probe = image_and_norm[-1]
+    norm_image = butterfly_sum(jnp.sum(image * image)[None], "wide")[0]
     spectral = jnp.sqrt(norm_image / norm_probe)
 
     w1 = spread_tiles(tiles_in, row_index, feature_blocks).reshape(features, hidden_width)
@@ -84,7 +97,9 @@
         back_part.astype(jnp.bfloat16), "blk", scatter_dimension=0, tiled=True
     ).astype(jnp.float32)
     slope_own = (back_own * activate_slope(hidden_own)).astype(jnp.bfloat16)
-    curvature = lax.psum(jnp.sum(slope_own.astype(jnp.float32) * pre_own), ("wide", "blk"))
+    curvature = butterfly_sum(
+        butterfly_sum(jnp.sum(slope_own.astype(jnp.float32) * pre_own)[None], "blk"), "wide"
+    )[0]
     slope_full = lax.all_gather(slope_own, "blk", axis=0, tiled=True)
 
     in_part = lax.dot_general(

time: 537 us -> 484 us (0.901)
  blocking collectives: 158 us -> 0 us
  starting transfers between devices: 0.51 us -> 50.7 us
  waiting for transfers between devices: 290 us -> 336 us
  between operations: 17.1 us -> 25 us
    psum x3 -> x0, blocking collectives: 158 us -> none  [the longest x1 75 us: body(): lax.psum(jnp.sum(slope_own.astype(jnp.float32) * pre_own), ('wide', 'blk'))]
    ppermute x0 -> x16, starting transfers between devices: none -> 50.2 us  [butterfly_sum(): lax.ppermute(value, axis, [(i, i ^ step) for i in range(size)])]
    ppermute x0 -> x16, waiting for transfers between devices: none -> 18.9 us  [butterfly_sum(): lax.ppermute(value, axis, [(i, i ^ step) for i in range(size)])]
    reduce_scatter x1, waiting for transfers between devices: 0.01 us -> 16.9 us  [body(): lax.psum_scatter(in_part.astype(jnp.bfloat16), 'wide', scatter_dimension=...]
  transfers between devices with their start and end apart: 8 -> 24, of which waited for: 6 -> 24; matrix products, arithmetic and copies ran while one was open for 7% -> 8% of each run, Pallas kernels for 0% -> 0%
where the time goes in v2:
time: 484 us; the launch traced here: 483 us
  waiting for transfers between devices  336 us (69%)
  starting transfers between devices  50.7 us (10%)
  matrix products  31.4 us (6%)
  between operations  25 us (5%)
  other arithmetic  21.1 us (4%)
  local copies, waits for them, and re-layouts  18.7 us (4%)
    reduce_scatter x1, waiting for transfers between devices, body(): lax.psum_scatter(out_part.astype(jnp.bfloat16), 'wide', scatter_dimension...  85.4 us
    ppermute x16, starting transfers between devices, butterfly_sum(): lax.ppermute(value, axis, [(i, i ^ step) for i in range(size)])  50.2 us
    all_gather x1, waiting for transfers between devices, body(): error_full = lax.all_gather(residual, 'wide', axis=0, tiled=True)  49.5 us
    reduce_scatter x1, waiting for transfers between devices, body(): lax.psum_scatter(pre_part.astype(jnp.bfloat16), 'blk', scatter_dimension=...  41.1 us
    reduce_scatter x1, waiting for transfers between devices, body(): lax.psum_scatter(back_part.astype(jnp.bfloat16), 'blk', scatter_dimension...  40.8 us
    all_gather x1, waiting for transfers between devices, body(): slope_full = lax.all_gather(slope_own, 'blk', axis=0, tiled=True)  39 us
    all_gather x1, waiting for transfers between devices, body(): active_full = lax.all_gather(active_own, 'blk', axis=0, tiled=True)  38.4 us
    ppermute x16, waiting for transfers between devices, butterfly_sum(): lax.ppermute(value, axis, [(i, i ^ step) for i in range(size)])  18.9 us
  transfers between devices with their start and end apart: 24, of which 24 were waited for; matrix products, arithmetic and copies ran while one was open for 8% of the time, Pallas kernels for 0%

profile of v2, /device:TPU:32, one launch (start us, length us, event | category | flops | bytes accessed | tf_op | source)
XLA Modules:
  0.0 482.8 jit_solution(7220642685689882648)
XLA Ops:
  19.7 3.4 collective-permute-start.1
  24.7 5.9 %collective-permute-start.2 = (f32[1025]{0:T(1024)S(1)}, f32[1025]{0:T(1024)S(1)}, u32[]{:S(2)}, u32[]{:S(2)}) collective-permute-start(f32[1025]{0:T(1024)S(1)} %add.198), channel_id=1, source_target_pairs={{0,4},{1,5},{2,6},{3,7},{4,0},{5,1},{6,2},{7,3},{8,12},{9,13},{10,... | collective-permute-start | bytes 12308 | tf_op jit(solution)/shard_map/ppermute | solution.py:40
  35.9 3.0 collective-permute-start.4
  40.2 4.6 collective-permute-start.5
  46.0 2.9 collective-permute-start.6
  50.3 4.4 collective-permute-start.7
  56.9 5.2 %all-gather.5.cloned.1.call-done = bf16[1024,1024]{1,0:T(8,128)(2,1)} async-done(((bf16[32,1024]{1,0:T(8,128)(2,1)}), bf16[1024,1024]{1,0:T(8,128)(2,1)}) %all-gather.5.cloned.1.call-update) | async-done | bytes 2097168 | tf_op jit(solution)/shard_map/all_gather | solution.py:75
  62.1 5.2 %fusion.8 = bf16[1024,1024]{1,0:T(8,128)(2,1)} fusion(bf16[1024,1024]{1,0:T(8,128)(2,1)} %all-gather.5.cloned.1.call-done, bf16[128,8,8,128]{3,2,1,0:T(8,128)(2,1)S(1)} %bitcast.159), kind=kOutput, calls=%fused_computation.15 | convolution fusion | flops 2148532224 | bytes 6291456 | tf_op jit(solution)/shard_map/dot_general | solution.py:78
  67.4 41.1 %reduce-scatter.5.cloned.1.call-done = bf16[128,1024]{1,0:T(8,128)(2,1)} async-done(((bf16[1024,1024]{1,0:T(8,128)(2,1)}), bf16[128,1024]{1,0:T(8,128)(2,1)}) %reduce-scatter.5.cloned.1.call-update) | async-done | bytes 262160 | tf_op jit(solution)/shard_map/reduce_scatter | solution.py:79
  112.5 38.4 %all-gather.7.cloned.1.call-done = bf16[1024,1024]{1,0:T(8,128)(2,1)} async-done(((bf16[128,1024]{1,0:T(8,128)(2,1)}), bf16[1024,1024]{1,0:T(8,128)(2,1)}) %all-gather.7.cloned.1.call-update) | async-done | bytes 2097168 | tf_op jit(solution)/shard_map/all_gather | solution.py:84
  150.9 5.9 %fusion.14 = bf16[1024,1024]{1,0:T(8,128)(2,1)} fusion(bf16[1024,1024]{1,0:T(8,128)(2,1)} %all-gather.7.cloned.1.call-done, bf16[128,8,8,128]{3,2,1,0:T(8,128)(2,1)} %bitcast.161), kind=kOutput, calls=%fused_computation.17 | convolution fusion | flops 2148532224 | bytes 6291456 | tf_op jit(solution)/shard_map/dot_general | solution.py:86
  156.9 85.4 %reduce-scatter.7.cloned.1.call-done = bf16[32,1024]{1,0:T(8,128)(2,1)} async-done(((bf16[1024,1024]{1,0:T(8,128)(2,1)}), bf16[32,1024]{1,0:T(8,128)(2,1)}) %reduce-scatter.7.cloned.1.call-update) | async-done | bytes 65552 | tf_op jit(solution)/shard_map/reduce_scatter | solution.py:87
  244.0 49.5 %all-gather.9.cloned.1.call-done = bf16[1024,1024]{1,0:T(8,128)(2,1)} async-done(((bf16[32,1024]{1,0:T(8,128)(2,1)}), bf16[1024,1024]{1,0:T(8,128)(2,1)}) %all-gather.9.cloned.1.call-update) | async-done | bytes 2097168 | tf_op jit(solution)/shard_map/all_gather | solution.py:91
  293.6 6.0 %fusion.17 = bf16[1024,1024]{1,0:T(8,128)(2,1)} fusion(bf16[1024,1024]{1,0:T(8,128)(2,1)} %all-gather.9.cloned.1.call-done, bf16[128,8,8,128]{3,2,1,0:T(8,128)(2,1)} %bitcast.162), kind=kOutput, calls=%fused_computation.18 | convolution fusion | flops 2148532224 | bytes 6291456 | tf_op jit(solution)/shard_map/dot_general | solution.py:93
  299.6 40.8 %reduce-scatter.9.cloned.1.call-done = bf16[128,1024]{1,0:T(8,128)(2,1)} async-done(((bf16[1024,1024]{1,0:T(8,128)(2,1)}), bf16[128,1024]{1,0:T(8,128)(2,1)}) %reduce-scatter.9.cloned.1.call-update) | async-done | bytes 262160 | tf_op jit(solution)/shard_map/reduce_scatter | solution.py:96
  340.5 2.7 fusion.24
  344.6 39.0 %all-gather.11.cloned.1.call-done = bf16[1024,1024]{1,0:T(8,128)(2,1)} async-done(((bf16[128,1024]{1,0:T(8,128)(2,1)}), bf16[1024,1024]{1,0:T(8,128)(2,1)}) %all-gather.11.cloned.1.call-update) | async-done | bytes 2097168 | tf_op jit(solution)/shard_map/all_gather | solution.py:103
  383.6 5.3 %fusion.11 = bf16[1024,1024]{1,0:T(8,128)(2,1)} fusion(bf16[1024,1024]{1,0:T(8,128)(2,1)} %all-gather.11.cloned.1.call-done, bf16[128,8,8,128]{3,2,1,0:T(8,128)(2,1)S(1)} %bitcast.160), kind=kOutput, calls=%fused_computation.16 | convolution fusion | flops 2148532224 | bytes 6291456 | tf_op jit(solution)/shard_map/dot_general | solution.py:105
  390.5 4.0 convolution_bitcast_fusion
  400.9 2.0 copy.78
  405.2 3.1 add_multiply_fusion
  409.1 2.9 collective-permute-done.8
  413.2 3.5 collective-permute-start.9
  418.3 4.5 collective-permute-start.10
  422.8 3.2 collective-permute-done.10
  428.4 2.9 collective-permute-start.12
  432.6 4.4 collective-permute-start.13
  438.4 2.9 collective-permute-start.14
  442.6 4.4 collective-permute-start.15
  448.3 4.6 convolution_bitcast_fusion.1
  455.4 2.1 subtract_bitcast_fusion
  457.6 16.9 %reduce-scatter.11.cloned.1.call-done = bf16[32,1024]{1,0:T(8,128)(2,1)} async-done(((bf16[1024,1024]{1,0:T(8,128)(2,1)}), bf16[32,1024]{1,0:T(8,128)(2,1)}) %reduce-scatter.11.cloned.1.call-update) | async-done | bytes 65552 | tf_op jit(solution)/shard_map/reduce_scatter | solution.py:109
  (104 shorter events, 47.9 us)
Async XLA Ops:
  7.2 54.9 %all-gather.5.cloned.1.call-start = ((), (), s32[]{:S(2)}) async-start(), calls=%async_computation.4 | async-start | bytes 2162688 | tf_op jit(solution)/shard_map/all_gather | solution.py:75
  7.9 100.6 %reduce-scatter.5.cloned.1.call-start = ((), (), s32[]{:S(2)}) async-start(), calls=%async_computation.5 | async-start | bytes 2359296 | tf_op jit(solution)/shard_map/reduce_scatter | solution.py:79
  12.9 4.4 copy-start.3
  15.3 3.7 collective-permute-start
  19.7 5.0 %collective-permute-start.1 = (f32[1025]{0:T(1024)S(1)}, f32[1025]{0:T(1024)S(1)}, u32[]{:S(2)}, u32[]{:S(2)}) collective-permute-start(f32[1025]{0:T(1024)S(1)} %fusion.40), channel_id=1, source_target_pairs={{0,2},{1,3},{2,0},{3,1},{4,6},{5,7},{6,4},{7,5},{8,10},{9,11},{10,... | collective-permute-start | bytes 12308 | tf_op jit(solution)/shard_map/ppermute | solution.py:40
  24.7 7.6 %collective-permute-start.2 = (f32[1025]{0:T(1024)S(1)}, f32[1025]{0:T(1024)S(1)}, u32[]{:S(2)}, u32[]{:S(2)}) collective-permute-start(f32[1025]{0:T(1024)S(1)} %add.198), channel_id=1, source_target_pairs={{0,4},{1,5},{2,6},{3,7},{4,0},{5,1},{6,2},{7,3},{8,12},{9,13},{10,... | collective-permute-start | bytes 12308 | tf_op jit(solution)/shard_map/ppermute | solution.py:40
  33.3 1.4 collective-permute-start.3
  35.9 3.7 collective-permute-start.4
  40.2 5.2 %collective-permute-start.5 = (f32[1]{0:T(128)}, f32[1]{0:T(128)}, u32[]{:S(2)}, u32[]{:S(2)}) collective-permute-start(f32[1]{0:T(128)} %add.201), channel_id=1, source_target_pairs={{0,32},{8,40},{16,48},{24,56},{32,0},{40,8},{48,16},{56,24},{64,96... | collective-permute-start | bytes 20 | tf_op jit(solution)/shard_map/ppermute | solution.py:40
  46.0 3.7 collective-permute-start.6
  50.3 5.2 %collective-permute-start.7 = (f32[1]{0:T(128)}, f32[1]{0:T(128)}, u32[]{:S(2)}, u32[]{:S(2)}) collective-permute-start(f32[1]{0:T(128)} %add.203), channel_id=1, source_target_pairs={{0,128},{8,136},{16,144},{24,152},{32,160},{40,168},{48,176},{56,1... | collective-permute-start | bytes 20 | tf_op jit(solution)/shard_map/ppermute | solution.py:40
  67.3 83.6 %all-gather.7.cloned.1.call-start = ((), (), s32[]{:S(2)}) async-start(), calls=%async_computation.6 | async-start | bytes 2359296 | tf_op jit(solution)/shard_map/all_gather | solution.py:84
  110.3 132.0 %reduce-scatter.7.cloned.1.call-start = ((), (), s32[]{:S(2)}) async-start(), calls=%async_computation.7 | async-start | bytes 2162688 | tf_op jit(solution)/shard_map/reduce_scatter | solution.py:87
  156.8 85.5 %copy-start.2 = (bf16[32,1024]{1,0:T(8,128)(2,1)S(1)}, bf16[32,1024]{1,0:T(8,128)(2,1)}, u32[]{:S(2)}) copy-start(bf16[32,1024]{1,0:T(8,128)(2,1)} %param.8) | copy-start | bytes 196612
  156.8 136.8 %all-gather.9.cloned.1.call-start = ((), (), s32[]{:S(2)}) async-start(), calls=%async_computation.8 | async-start | bytes 2162688 | tf_op jit(solution)/shard_map/all_gather | solution.py:91
  243.8 96.7 %reduce-scatter.9.cloned.1.call-start = ((), (), s32[]{:S(2)}) async-start(), calls=%async_computation.9 | async-start | bytes 2359296 | tf_op jit(solution)/shard_map/reduce_scatter | solution.py:96
  299.6 40.9 %copy-start.1 = (bf16[128,1024]{1,0:T(8,128)(2,1)S(1)}, bf16[128,1024]{1,0:T(8,128)(2,1)}, u32[]{:S(2)}) copy-start(bf16[128,1024]{1,0:T(8,128)(2,1)} %reduce-scatter.5.cloned.1.call-done) | copy-start | bytes 786436
  299.6 84.0 %all-gather.11.cloned.1.call-start = ((), (), s32[]{:S(2)}) async-start(), calls=%async_computation.10 | async-start | bytes 2359296 | tf_op jit(solution)/shard_map/all_gather | solution.py:103
  343.2 131.3 %reduce-scatter.11.cloned.1.call-start = ((), (), s32[]{:S(2)}) async-start(), calls=%async_computation.11 | async-start | bytes 2162688 | tf_op jit(solution)/shard_map/reduce_scatter | solution.py:109
  389.0 1.6 copy-start.4
  403.9 1.3 copy-start
  408.3 3.6 collective-permute-start.8
  413.2 4.5 collective-permute-start.9
  418.3 7.7 %collective-permute-start.10 = (f32[1]{0:T(128)}, f32[1]{0:T(128)}, u32[]{:S(2)}, u32[]{:S(2)}) collective-permute-start(f32[1]{0:T(128)} %add.219), channel_id=1, source_target_pairs={{0,4},{1,5},{2,6},{3,7},{4,0},{5,1},{6,2},{7,3},{8,12},{9,13},{10,... | collective-permute-start | bytes 20 | tf_op jit(solution)/shard_map/ppermute | solution.py:40
  426.6 1.2 collective-permute-start.11
  428.4 3.6 collective-permute-start.12
  432.6 5.1 %collective-permute-start.13 = (f32[1]{0:T(128)}, f32[1]{0:T(128)}, u32[]{:S(2)}, u32[]{:S(2)}) collective-permute-start(f32[1]{0:T(128)} %add.222), channel_id=1, source_target_pairs={{0,32},{8,40},{16,48},{24,56},{32,0},{40,8},{48,16},{56,24},{64,96... | collective-permute-start | bytes 20 | tf_op jit(solution)/shard_map/ppermute | solution.py:40
  438.4 3.6 collective-permute-start.14
  442.6 5.1 %collective-permute-start.15 = (f32[1]{0:T(128)}, f32[1]{0:T(128)}, u32[]{:S(2)}, u32[]{:S(2)}) collective-permute-start(f32[1]{0:T(128)} %add.224), channel_id=1, source_target_pairs={{0,128},{8,136},{16,144},{24,152},{32,160},{40,168},{48,176},{56,1... | collective-permute-start | bytes 20 | tf_op jit(solution)/shard_map/ppermute | solution.py:40
Sparse Core Ops, SparseCore 0:
  10.6 51.4 all-gather.4
  67.4 40.9 reduce-scatter.4
  110.8 40.0 all-gather.6
  157.0 85.2 reduce-scatter.6
  245.3 48.2 all-gather.8
  299.7 40.7 reduce-scatter.8
  343.3 40.2 all-gather.10
  389.1 85.3 reduce-scatter.10

commit v3 on v2

--- a/solution.py
+++ b/solution.py
@@ -42,6 +42,20 @@
     return value
 
 
+def gather_rows(value, axis):
+    size = lax.axis_size(axis)
+    spread = jnp.broadcast_to(value[None], (size,) + value.shape)
+    gathered = lax.all_to_all(spread, axis, 0, 0, tiled=False)
+    return gathered.reshape((size * value.shape[0],) + value.shape[1:])
+
+
+def sum_rows(value, axis):
+    size = lax.axis_size(axis)
+    parts = value.reshape((size, value.shape[0] // size) + value.shape[1:])
+    received = lax.all_to_all(parts, axis, 0, 0, tiled=False)
+    return jnp.sum(received.astype(jnp.float32), axis=0)
+
+
 def body(tokens, target, probe_vector, weight_in, weight_out, slot_rows, slot_count):
     columns, unit, slots, block, width_two = weight_in.shape
     features = tokens.shape[1]
@@ -72,7 +86,7 @@
         spread_tiles(tiles_out, row_index, feature_blocks), (2, 1, 0, 3)
     ).reshape(hidden_width, features)
 
-    x_full = lax.all_gather(tokens, "wide", axis=0, tiled=True)
+    x_full = gather_rows(tokens, "wide")
     x_full, spectral = lax.optimization_barrier((x_full, spectral))
 
     pre_part = jnp.dot(x_full, w1, preferred_element_type=jnp.float32)
@@ -84,11 +98,9 @@
     active_full = lax.all_gather(active_own, "blk", axis=0, tiled=True)
 
     out_part = jnp.dot(active_full, w2, preferred_element_type=jnp.float32)
-    outputs = lax.psum_scatter(
-        out_part.astype(jnp.bfloat16), "wide", scatter_dimension=0, tiled=True
-    )
+    outputs = sum_rows(out_part.astype(jnp.bfloat16), "wide").astype(jnp.bfloat16)
     residual = (outputs.astype(jnp.float32) - target.astype(jnp.float32)).astype(jnp.bfloat16)
-    error_full = lax.all_gather(residual, "wide", axis=0, tiled=True)
+    error_full = gather_rows(residual, "wide")
 
     back_part = lax.dot_general(
         error_full, w2, (((1,), (1,)), ((), ())), preferred_element_type=jnp.float32
@@ -105,11 +117,7 @@
     in_part = lax.dot_general(
         slope_full, w1, (((1,), (1,)), ((), ())), preferred_element_type=jnp.float32
     )
-    token_grad = (
-        lax.psum_scatter(in_part.astype(jnp.bfloat16), "wide", scatter_dimension=0, tiled=True)
-        .astype(jnp.float32)
-        / spectral
-    ).astype(jnp.bfloat16)
+    token_grad = (sum_rows(in_part.astype(jnp.bfloat16), "wide") / spectral).astype(jnp.bfloat16)
 
     g1 = lax.dot_general(
         x_full, slope_full, (((0,), (0,)), ((), ())), preferred_element_type=jnp.float32

time: 484 us -> 388 us (0.80)
  waiting for transfers between devices: 336 us -> 154 us
  blocking collectives: 0 us -> 67 us
  starting transfers between devices: 50.7 us -> 65.3 us
  local copies, waits for them, and re-layouts: 18.7 us -> 26.6 us
    reduce_scatter x2 -> x0, waiting for transfers between devices: 102 us -> none  [the longest x1 85.4 us: body(): lax.psum_scatter(out_part.astype(jnp.bfloat16), 'wide', scatter_dimension...]
    all_to_all x0 -> x2, blocking collectives: none -> 67 us  [the longest x1 34.9 us: sum_rows(): received = lax.all_to_all(parts, axis, 0, 0, tiled=False)]
    all_gather x2 -> x0, waiting for transfers between devices: 54.7 us -> none  [the longest x1 49.5 us: body(): error_full = lax.all_gather(residual, 'wide', axis=0, tiled=True)]
    all_gather x1, waiting for transfers between devices: 39 us -> 16.6 us  [body(): slope_full = lax.all_gather(slope_own, 'blk', axis=0, tiled=True)]
    all_to_all x0 -> x2, starting transfers between devices: none -> 14.5 us  [the longest x1 7.45 us: gather_rows(): gathered = lax.all_to_all(spread, axis, 0, 0, tiled=False)]
    dot_general x0 -> x2, local copies, waits for them, and re-layouts: none -> 6.52 us  [body(): lax.dot_general(error_full, active_full, (((0,), (0,)), ((), ())), prefer...]
  transfers between devices with their start and end apart: 24 -> 22, of which waited for: 24 -> 19; matrix products, arithmetic and copies ran while one was open for 8% -> 12% of each run, Pallas kernels for 0% -> 0%
where the time goes in v3:
time: 388 us; the launch traced here: 385 us
  waiting for transfers between devices  154 us (40%)
  blocking collectives  67 us (17%)
  starting transfers between devices  65.3 us (17%)
  matrix products  29.1 us (8%)
  local copies, waits for them, and re-layouts  26.6 us (7%)
  between operations  25.1 us (6%)
  other arithmetic  17.9 us (5%)
    ppermute x16, starting transfers between devices, butterfly_sum(): lax.ppermute(value, axis, [(i, i ^ step) for i in range(size)])  50.6 us
    reduce_scatter x1, waiting for transfers between devices, body(): lax.psum_scatter(pre_part.astype(jnp.bfloat16), 'blk', scatter_dimension=...  44 us
    all_gather x1, waiting for transfers between devices, body(): active_full = lax.all_gather(active_own, 'blk', axis=0, tiled=True)  39.7 us
    reduce_scatter x1, waiting for transfers between devices, body(): lax.psum_scatter(back_part.astype(jnp.bfloat16), 'blk', scatter_dimension...  37.6 us
    all_to_all x1, blocking collectives, sum_rows(): received = lax.all_to_all(parts, axis, 0, 0, tiled=False)  34.9 us
    all_to_all x1, blocking collectives, gather_rows(): gathered = lax.all_to_all(spread, axis, 0, 0, tiled=False)  32 us
    all_gather x1, waiting for transfers between devices, body(): slope_full = lax.all_gather(slope_own, 'blk', axis=0, tiled=True)  16.6 us
    ppermute x16, waiting for transfers between devices, butterfly_sum(): lax.ppermute(value, axis, [(i, i ^ step) for i in range(size)])  16.5 us
  transfers between devices with their start and end apart: 22, of which 19 were waited for; matrix products, arithmetic and copies ran while one was open for 12% of the time, Pallas kernels for 0%

profile of v3, /device:TPU:32, one launch (start us, length us, event | category | flops | bytes accessed | tf_op | source)
XLA Modules:
  0.0 385.5 jit_solution(1736977316046464918)
XLA Ops:
  9.6 7.5 %all-to-all-start = ((bf16[32,32,1024]{2,1,0:T(8,128)(2,1)}), bf16[32,32,1024]{2,1,0:T(8,128)(2,1)S(1)}, u32[]{:S(2)}, u32[]{:S(2)}) async-start(bf16[32,32,1024]{2,1,0:T(8,128)(2,1)} %broadcast_in_dim.361), calls=%async_computation | async-start | bytes 4194304 | tf_op jit(solution)/shard_map/all_to_all | solution.py:48
  22.1 2.7 collective-permute-done
  25.5 3.4 collective-permute-start.1
  30.5 5.9 %collective-permute-start.2 = (f32[1025]{0:T(1024)S(1)}, f32[1025]{0:T(1024)S(1)}, u32[]{:S(2)}, u32[]{:S(2)}) collective-permute-start(f32[1025]{0:T(1024)S(1)} %add.201), channel_id=1, source_target_pairs={{0,4},{1,5},{2,6},{3,7},{4,0},{5,1},{6,2},{7,3},{8,12},{9,13},{10,... | collective-permute-start | bytes 12308 | tf_op jit(solution)/shard_map/ppermute | solution.py:40
  41.8 3.2 collective-permute-start.4
  46.1 4.7 %collective-permute-start.5 = (f32[1]{0:T(128)}, f32[1]{0:T(128)}, u32[]{:S(2)}, u32[]{:S(2)}) collective-permute-start(f32[1]{0:T(128)} %add.204), channel_id=1, source_target_pairs={{0,32},{8,40},{16,48},{24,56},{32,0},{40,8},{48,16},{56,24},{64,96... | collective-permute-start | bytes 20 | tf_op jit(solution)/shard_map/ppermute | solution.py:40
  51.9 3.2 collective-permute-start.6
  56.2 4.7 %collective-permute-start.7 = (f32[1]{0:T(128)}, f32[1]{0:T(128)}, u32[]{:S(2)}, u32[]{:S(2)}) collective-permute-start(f32[1]{0:T(128)} %add.206), channel_id=1, source_target_pairs={{0,128},{8,136},{16,144},{24,152},{32,160},{40,168},{48,176},{56,1... | collective-permute-start | bytes 20 | tf_op jit(solution)/shard_map/ppermute | solution.py:40
  62.7 6.0 %fusion.8 = bf16[1024,1024]{1,0:T(8,128)(2,1)} fusion(bf16[1024,1024]{1,0:T(8,128)(2,1)S(1)} %bitcast.169, bf16[128,8,8,128]{3,2,1,0:T(8,128)(2,1)} %bitcast.171), kind=kOutput, calls=%fused_computation.15 | convolution fusion | flops 2148532224 | bytes 6291456 | tf_op jit(solution)/shard_map/dot_general | solution.py:92
  68.8 44.0 %reduce-scatter.3.cloned.1.call-done = bf16[128,1024]{1,0:T(8,128)(2,1)} async-done(((bf16[1024,1024]{1,0:T(8,128)(2,1)}), bf16[128,1024]{1,0:T(8,128)(2,1)}) %reduce-scatter.3.cloned.1.call-update) | async-done | bytes 262160 | tf_op jit(solution)/shard_map/reduce_scatter | solution.py:93
  115.6 39.7 %all-gather.3.cloned.1.call-done = bf16[1024,1024]{1,0:T(8,128)(2,1)} async-done(((bf16[128,1024]{1,0:T(8,128)(2,1)}), bf16[1024,1024]{1,0:T(8,128)(2,1)}) %all-gather.3.cloned.1.call-update) | async-done | bytes 2097168 | tf_op jit(solution)/shard_map/all_gather | solution.py:98
  155.2 3.9 %fusion.14 = bf16[1024,1024]{1,0:T(8,128)(2,1)S(1)} fusion(bf16[1024,1024]{1,0:T(8,128)(2,1)} %all-gather.3.cloned.1.call-done, bf16[128,8,8,128]{3,2,1,0:T(8,128)(2,1)S(1)} %bitcast.175), kind=kOutput, calls=%fused_computation.17 | convolution fusion | flops 2148532224 | bytes 6291456 | tf_op jit(solution)/shard_map/dot_general | solution.py:100
  159.2 34.9 %all_to_all.20 = bf16[32,32,1024]{2,1,0:T(8,128)(2,1)S(1)} all-to-all(bf16[32,32,1024]{2,1,0:T(8,128)(2,1)S(1)} %bitcast.179), channel_id=1, replica_groups=mesh['wide'=32,'blk'=8] {'wide'}, dimensions={0} | all-to-all | bytes 4194304 | tf_op jit(solution)/shard_map/all_to_all | solution.py:55
  195.2 32.0 %all_to_all.21 = bf16[32,32,1024]{2,1,0:T(8,128)(2,1)S(1)} all-to-all(bf16[32,32,1024]{2,1,0:T(8,128)(2,1)S(1)} %broadcast_in_dim.385), channel_id=1, replica_groups=mesh['wide'=32,'blk'=8] {'wide'}, dimensions={0} | all-to-all | bytes 4194304 | tf_op jit(solution)/shard_map/all_to_all | solution.py:48
  227.3 3.7 fusion.17
  231.0 37.6 %reduce-scatter.5.cloned.1.call-done = bf16[128,1024]{1,0:T(8,128)(2,1)} async-done(((bf16[1024,1024]{1,0:T(8,128)(2,1)}), bf16[128,1024]{1,0:T(8,128)(2,1)}) %reduce-scatter.5.cloned.1.call-update) | async-done | bytes 262160 | tf_op jit(solution)/shard_map/reduce_scatter | solution.py:108
  268.7 2.7 fusion.24
  272.8 3.9 %copy.94 = bf16[1024,1024]{1,0:T(8,128)(2,1)} copy(bf16[1024,1024]{0,1:T(8,128)(2,1)} %bitcast.174) | data formatting | bytes 4194304 | tf_op jit(solution)/shard_map/dot_general | solution.py:126
  279.3 4.6 %convolution_bitcast_fusion = f32[8,8,128,128]{3,2,1,0:T(8,128)S(1)} fusion(bf16[8,128,1024,1]{2,1,3,0:T(8,128)(2,1)} %bitcast.178, bf16[8,128,1024,1]{2,1,0,3:T(8,128)(2,1)} %bitcast.177), kind=kOutput, calls=%fused_computation.3 | convolution fusion | flops 2147483648 | bytes 8388608 | tf_op jit(solution)/shard_map/dot_general | solution.py:126
  295.0 16.6 %all-gather.5.cloned.1.call-done = bf16[1024,1024]{1,0:T(8,128)(2,1)} async-done(((bf16[128,1024]{1,0:T(8,128)(2,1)}), bf16[1024,1024]{1,0:T(8,128)(2,1)}) %all-gather.5.cloned.1.call-update) | async-done | bytes 2097168 | tf_op jit(solution)/shard_map/all_gather | solution.py:115
  311.5 6.0 %fusion.11 = bf16[1024,1024]{1,0:T(8,128)(2,1)} fusion(bf16[1024,1024]{1,0:T(8,128)(2,1)} %all-gather.5.cloned.1.call-done, bf16[128,8,8,128]{3,2,1,0:T(8,128)(2,1)} %bitcast.172), kind=kOutput, calls=%fused_computation.16 | convolution fusion | flops 2148532224 | bytes 6291456 | tf_op jit(solution)/shard_map/dot_general | solution.py:117
  317.5 7.1 %all-to-all-start.3 = ((bf16[32,32,1024]{2,1,0:T(8,128)(2,1)}), bf16[32,32,1024]{2,1,0:T(8,128)(2,1)S(1)}, u32[]{:S(2)}, u32[]{:S(2)}) async-start(bf16[32,32,1024]{2,1,0:T(8,128)(2,1)} %bitcast.173), calls=%async_computation.5 | async-start | bytes 4194304 | tf_op jit(solution)/shard_map/all_to_all | solution.py:55
  324.6 3.5 add_multiply_fusion
  329.0 2.8 collective-permute-done.8
  333.1 3.4 collective-permute-start.9
  338.3 4.6 %collective-permute-start.10 = (f32[1]{0:T(128)}, f32[1]{0:T(128)}, u32[]{:S(2)}, u32[]{:S(2)}) collective-permute-start(f32[1]{0:T(128)} %add.222), channel_id=1, source_target_pairs={{0,4},{1,5},{2,6},{3,7},{4,0},{5,1},{6,2},{7,3},{8,12},{9,13},{10,... | collective-permute-start | bytes 20 | tf_op jit(solution)/shard_map/ppermute | solution.py:40
  342.9 3.2 collective-permute-done.10
  348.6 3.2 collective-permute-start.12
  352.9 4.7 %collective-permute-start.13 = (f32[1]{0:T(128)}, f32[1]{0:T(128)}, u32[]{:S(2)}, u32[]{:S(2)}) collective-permute-start(f32[1]{0:T(128)} %add.225), channel_id=1, source_target_pairs={{0,32},{8,40},{16,48},{24,56},{32,0},{40,8},{48,16},{56,24},{64,96... | collective-permute-start | bytes 20 | tf_op jit(solution)/shard_map/ppermute | solution.py:40
  358.6 3.2 collective-permute-start.14
  362.9 4.7 %collective-permute-start.15 = (f32[1]{0:T(128)}, f32[1]{0:T(128)}, u32[]{:S(2)}, u32[]{:S(2)}) collective-permute-start(f32[1]{0:T(128)} %add.227), channel_id=1, source_target_pairs={{0,128},{8,136},{16,144},{24,152},{32,160},{40,168},{48,176},{56,1... | collective-permute-start | bytes 20 | tf_op jit(solution)/shard_map/ppermute | solution.py:40
  368.7 4.6 %convolution_bitcast_fusion.1 = f32[128,8,8,128]{3,1,2,0:T(8,128)S(1)} fusion(bf16[1024,1024]{1,0:T(8,128)(2,1)} %bitcast.170, bf16[1024,1024]{1,0:T(8,128)(2,1)} %all-gather.5.cloned.1.call-done), kind=kOutput, calls=%fused_computation.4 | convolution fusion | flops 2147483648 | bytes 8388608 | tf_op jit(solution)/shard_map/dot_general | solution.py:122
  (112 shorter events, 44.6 us)
Async XLA Ops:
  9.6 7.5 %copy-start.8 = (s32[8,1,2]{0,2,1:T(2,128)S(1)}, s32[8,1,2]{0,2,1:T(2,128)}, u32[]{:S(2)}) copy-start(s32[8,1,2]{0,2,1:T(2,128)} %param.12) | copy-start | bytes 196
  9.6 7.6 %copy-start.3 = (f32[1024]{0:T(1024)S(1)}, f32[1024]{0:T(1024)}, u32[]{:S(2)}) copy-start(f32[1024]{0:T(1024)} %param.9) | copy-start | bytes 12292
  9.6 8.3 %copy-start.9 = (s32[8,1]{0,1:T(1,128)S(1)}, s32[8,1]{0,1:T(1,128)}, u32[]{:S(2)}) copy-start(s32[8,1]{0,1:T(1,128)} %param.13) | copy-start | bytes 100
  9.6 53.1 %all-to-all-start = ((bf16[32,32,1024]{2,1,0:T(8,128)(2,1)}), bf16[32,32,1024]{2,1,0:T(8,128)(2,1)S(1)}, u32[]{:S(2)}, u32[]{:S(2)}) async-start(bf16[32,32,1024]{2,1,0:T(8,128)(2,1)} %broadcast_in_dim.361), calls=%async_computation | async-start | bytes 4194304 | tf_op jit(solution)/shard_map/all_to_all | solution.py:48
  17.1 95.8 %reduce-scatter.3.cloned.1.call-start = ((), (), s32[]{:S(2)}) async-start(), calls=%async_computation.6 | async-start | bytes 2359296 | tf_op jit(solution)/shard_map/reduce_scatter | solution.py:93
  21.1 3.7 collective-permute-start
  25.5 5.0 %collective-permute-start.1 = (f32[1025]{0:T(1024)S(1)}, f32[1025]{0:T(1024)S(1)}, u32[]{:S(2)}, u32[]{:S(2)}) collective-permute-start(f32[1025]{0:T(1024)S(1)} %fusion.40), channel_id=1, source_target_pairs={{0,2},{1,3},{2,0},{3,1},{4,6},{5,7},{6,4},{7,5},{8,10},{9,11},{10,... | collective-permute-start | bytes 12308 | tf_op jit(solution)/shard_map/ppermute | solution.py:40
  30.5 7.6 %collective-permute-start.2 = (f32[1025]{0:T(1024)S(1)}, f32[1025]{0:T(1024)S(1)}, u32[]{:S(2)}, u32[]{:S(2)}) collective-permute-start(f32[1025]{0:T(1024)S(1)} %add.201), channel_id=1, source_target_pairs={{0,4},{1,5},{2,6},{3,7},{4,0},{5,1},{6,2},{7,3},{8,12},{9,13},{10,... | collective-permute-start | bytes 12308 | tf_op jit(solution)/shard_map/ppermute | solution.py:40
  39.2 1.4 collective-permute-start.3
  41.8 3.7 collective-permute-start.4
  46.1 5.2 %collective-permute-start.5 = (f32[1]{0:T(128)}, f32[1]{0:T(128)}, u32[]{:S(2)}, u32[]{:S(2)}) collective-permute-start(f32[1]{0:T(128)} %add.204), channel_id=1, source_target_pairs={{0,32},{8,40},{16,48},{24,56},{32,0},{40,8},{48,16},{56,24},{64,96... | collective-permute-start | bytes 20 | tf_op jit(solution)/shard_map/ppermute | solution.py:40
  51.9 3.7 collective-permute-start.6
  56.2 5.2 %collective-permute-start.7 = (f32[1]{0:T(128)}, f32[1]{0:T(128)}, u32[]{:S(2)}, u32[]{:S(2)}) collective-permute-start(f32[1]{0:T(128)} %add.206), channel_id=1, source_target_pairs={{0,128},{8,136},{16,144},{24,152},{32,160},{40,168},{48,176},{56,1... | collective-permute-start | bytes 20 | tf_op jit(solution)/shard_map/ppermute | solution.py:40
  62.7 6.0 %copy-start = (bf16[32,32,1024]{2,1,0:T(8,128)(2,1)}, bf16[32,32,1024]{2,1,0:T(8,128)(2,1)S(1)}, u32[]{:S(2)}) copy-start(bf16[32,32,1024]{2,1,0:T(8,128)(2,1)S(1)} %all-to-all-done) | copy-start | bytes 6291460
  68.8 46.2 %copy-start.5 = (bf16[8,128,128]{2,1,0:T(8,128)(2,1)S(1)}, bf16[8,128,128]{2,1,0:T(8,128)(2,1)}, u32[]{:S(2)}) copy-start(bf16[8,128,128]{2,1,0:T(8,128)(2,1)} %get-tuple-element.27) | copy-start | bytes 786436
  68.8 86.4 %all-gather.3.cloned.1.call-start = ((), (), s32[]{:S(2)}) async-start(), calls=%async_computation.7 | async-start | bytes 2359296 | tf_op jit(solution)/shard_map/all_gather | solution.py:98
  114.7 154.0 %reduce-scatter.5.cloned.1.call-start = ((), (), s32[]{:S(2)}) async-start(), calls=%async_computation.8 | async-start | bytes 2359296 | tf_op jit(solution)/shard_map/reduce_scatter | solution.py:108
  115.6 43.6 %copy-start.1 = (bf16[8,128,8,128]{3,2,1,0:T(8,128)(2,1)}, bf16[8,128,8,128]{3,2,1,0:T(8,128)(2,1)S(1)}, u32[]{:S(2)}) copy-start(bf16[8,128,8,128]{3,2,1,0:T(8,128)(2,1)S(1)} %select_add_fusion) | copy-start | bytes 6291460
  194.1 0.8 copy-start.7
  194.9 32.3 %copy-start.6 = (bf16[32,1024]{1,0:T(8,128)(2,1)}, bf16[32,1024]{1,0:T(8,128)(2,1)S(1)}, u32[]{:S(2)}) copy-start(bf16[32,1024]{1,0:T(8,128)(2,1)S(1)} %reduce_sum.50) | copy-start | bytes 196612
  195.2 32.0 %copy-start.2 = (bf16[8,128,8,128]{3,2,1,0:T(8,128)(2,1)S(1)}, bf16[8,128,8,128]{3,2,1,0:T(8,128)(2,1)}, u32[]{:S(2)}) copy-start(bf16[8,128,8,128]{3,2,1,0:T(8,128)(2,1)} %copy-done.1) | copy-start | bytes 6291460
  231.0 37.7 %copy-start.4 = (bf16[128,1024]{1,0:T(8,128)(2,1)S(1)}, bf16[128,1024]{1,0:T(8,128)(2,1)}, u32[]{:S(2)}) copy-start(bf16[128,1024]{1,0:T(8,128)(2,1)} %reduce-scatter.3.cloned.1.call-done) | copy-start | bytes 786436
  231.0 80.6 %all-gather.5.cloned.1.call-start = ((), (), s32[]{:S(2)}) async-start(), calls=%async_computation.9 | async-start | bytes 2359296 | tf_op jit(solution)/shard_map/all_gather | solution.py:115
  317.5 60.4 %all-to-all-start.3 = ((bf16[32,32,1024]{2,1,0:T(8,128)(2,1)}), bf16[32,32,1024]{2,1,0:T(8,128)(2,1)S(1)}, u32[]{:S(2)}, u32[]{:S(2)}) async-start(bf16[32,32,1024]{2,1,0:T(8,128)(2,1)} %bitcast.173), calls=%async_computation.5 | async-start | bytes 4194304 | tf_op jit(solution)/shard_map/all_to_all | solution.py:55
  328.2 3.6 collective-permute-start.8
  333.1 4.5 %collective-permute-start.9 = (f32[1]{0:T(128)}, f32[1]{0:T(128)}, u32[]{:S(2)}, u32[]{:S(2)}) collective-permute-start(f32[1]{0:T(128)} %add.221), channel_id=1, source_target_pairs={{0,2},{1,3},{2,0},{3,1},{4,6},{5,7},{6,4},{7,5},{8,10},{9,11},{10,... | collective-permute-start | bytes 20 | tf_op jit(solution)/shard_map/ppermute | solution.py:40
  338.3 7.7 %collective-permute-start.10 = (f32[1]{0:T(128)}, f32[1]{0:T(128)}, u32[]{:S(2)}, u32[]{:S(2)}) collective-permute-start(f32[1]{0:T(128)} %add.222), channel_id=1, source_target_pairs={{0,4},{1,5},{2,6},{3,7},{4,0},{5,1},{6,2},{7,3},{8,12},{9,13},{10,... | collective-permute-start | bytes 20 | tf_op jit(solution)/shard_map/ppermute | solution.py:40
  346.7 1.2 collective-permute-start.11
  348.6 3.6 collective-permute-start.12
  352.9 5.1 %collective-permute-start.13 = (f32[1]{0:T(128)}, f32[1]{0:T(128)}, u32[]{:S(2)}, u32[]{:S(2)}) collective-permute-start(f32[1]{0:T(128)} %add.225), channel_id=1, source_target_pairs={{0,32},{8,40},{16,48},{24,56},{32,0},{40,8},{48,16},{56,24},{64,96... | collective-permute-start | bytes 20 | tf_op jit(solution)/shard_map/ppermute | solution.py:40
  358.6 3.6 collective-permute-start.14
  362.9 5.1 %collective-permute-start.15 = (f32[1]{0:T(128)}, f32[1]{0:T(128)}, u32[]{:S(2)}, u32[]{:S(2)}) collective-permute-start(f32[1]{0:T(128)} %add.227), channel_id=1, source_target_pairs={{0,128},{8,136},{16,144},{24,152},{32,160},{40,168},{48,176},{56,1... | collective-permute-start | bytes 20 | tf_op jit(solution)/shard_map/ppermute | solution.py:40
Sparse Core Ops, SparseCore 0:
  68.9 43.8 reduce-scatter.2
  115.2 39.9 all-gather.2
  231.1 37.5 reduce-scatter.4
  271.5 40.0 all-gather.4

commit v4 on v3

--- a/solution.py
+++ b/solution.py
@@ -87,12 +87,11 @@
     ).reshape(hidden_width, features)
 
     x_full = gather_rows(tokens, "wide")
-    x_full, spectral = lax.optimization_barrier((x_full, spectral))
-
     pre_part = jnp.dot(x_full, w1, preferred_element_type=jnp.float32)
     pre_own = lax.psum_scatter(
         pre_part.astype(jnp.bfloat16), "blk", scatter_dimension=0, tiled=True
     ).astype(jnp.float32)
+    pre_own, spectral = lax.optimization_barrier((pre_own, spectral))
     hidden_own = pre_own / spectral
     active_own = activate(hidden_own).astype(jnp.bfloat16)
     active_full = lax.all_gather(active_own, "blk", axis=0, tiled=True)
@@ -113,6 +112,7 @@
         butterfly_sum(jnp.sum(slope_own.astype(jnp.float32) * pre_own)[None], "blk"), "wide"
     )[0]
     slope_full = lax.all_gather(slope_own, "blk", axis=0, tiled=True)
+    slope_full, curvature = lax.optimization_barrier((slope_full, curvature))
 
     in_part = lax.dot_general(
         slope_full, w1, (((1,), (1,)), ((), ())), preferred_element_type=jnp.float32

time: 388 us -> 379 us (0.977)
  local copies, waits for them, and re-layouts: 26.6 us -> 44 us
  waiting for transfers between devices: 154 us -> 138 us
  starting transfers between devices: 65.3 us -> 56.5 us
    reduce_scatter x2 -> x0, waiting for transfers between devices: 81.6 us -> none  [the longest x1 44 us: body(): lax.psum_scatter(pre_part.astype(jnp.bfloat16), 'blk', scatter_dimension=...]
    unnamed x4 -> x6, waiting for transfers between devices: 0.07 us -> 38 us
    all_to_all x1, waiting for transfers between devices: 0.01 us -> 25.2 us  [gather_rows(): gathered = lax.all_to_all(spread, axis, 0, 0, tiled=False)]
    all_gather x1, waiting for transfers between devices: 16.6 us -> 0.02 us  [body(): slope_full = lax.all_gather(slope_own, 'blk', axis=0, tiled=True)]
    ppermute x16, waiting for transfers between devices: 16.5 us -> 29.1 us  [butterfly_sum(): lax.ppermute(value, axis, [(i, i ^ step) for i in range(size)])]
    broadcast_in_dim x26 -> x25, local copies, waits for them, and re-layouts: 12.9 us -> 23.8 us  [pick_tiles(): jnp.where(hit[r][:, :, None, None], by_col[r][:, None], 0.0)]
    ppermute x16, starting transfers between devices: 50.6 us -> 41.3 us  [butterfly_sum(): lax.ppermute(value, axis, [(i, i ^ step) for i in range(size)])]
    unnamed x22 -> x25, local copies, waits for them, and re-layouts: 1.59 us -> 8.3 us
  transfers between devices with their start and end apart: 22 -> 22, of which waited for: 19 -> 20; matrix products, arithmetic and copies ran while one was open for 12% -> 15% of each run, Pallas kernels for 0% -> 0%
where the time goes in v4:
time: 379 us; the launch traced here: 377 us
  waiting for transfers between devices  138 us (36%)
  blocking collectives  67 us (18%)
  starting transfers between devices  56.5 us (15%)
  local copies, waits for them, and re-layouts  44 us (12%)
  matrix products  29.3 us (8%)
  between operations  25.2 us (7%)
  other arithmetic  16.8 us (4%)
    all_gather x1, waiting for transfers between devices, body(): active_full = lax.all_gather(active_own, 'blk', axis=0, tiled=True)  44.5 us
    ppermute x16, starting transfers between devices, butterfly_sum(): lax.ppermute(value, axis, [(i, i ^ step) for i in range(size)])  41.3 us
    unnamed x6, waiting for transfers between devices  38 us
    all_to_all x1, blocking collectives, sum_rows(): received = lax.all_to_all(parts, axis, 0, 0, tiled=False)  34.9 us
    all_to_all x1, blocking collectives, gather_rows(): gathered = lax.all_to_all(spread, axis, 0, 0, tiled=False)  32 us
    ppermute x16, waiting for transfers between devices, butterfly_sum(): lax.ppermute(value, axis, [(i, i ^ step) for i in range(size)])  29.1 us
    all_to_all x1, waiting for transfers between devices, gather_rows(): gathered = lax.all_to_all(spread, axis, 0, 0, tiled=False)  25.2 us
    broadcast_in_dim x25, local copies, waits for them, and re-layouts, pick_tiles(): jnp.where(hit[r][:, :, None, None], by_col[r][:, None], 0.0)  23.8 us
  transfers between devices with their start and end apart: 22, of which 20 were waited for; matrix products, arithmetic and copies ran while one was open for 15% of the time, Pallas kernels for 0%

profile of v4, /device:TPU:32, one launch (start us, length us, event | category | flops | bytes accessed | tf_op | source)
XLA Modules:
  0.0 376.7 jit_solution(18395437612279440039)
XLA Ops:
  7.2 2.4 broadcast_in_dim.372
  9.6 7.5 %all-to-all-start = ((bf16[32,32,1024]{2,1,0:T(8,128)(2,1)}), bf16[32,32,1024]{2,1,0:T(8,128)(2,1)S(1)}, u32[]{:S(2)}, u32[]{:S(2)}) async-start(bf16[32,32,1024]{2,1,0:T(8,128)(2,1)} %broadcast_in_dim.372), calls=%async_computation | async-start | bytes 4194304 | tf_op jit(solution)/shard_map/all_to_all | solution.py:48
  20.8 25.2 %all-to-all-done = bf16[32,32,1024]{2,1,0:T(8,128)(2,1)S(1)} async-done(((bf16[32,32,1024]{2,1,0:T(8,128)(2,1)}), bf16[32,32,1024]{2,1,0:T(8,128)(2,1)S(1)}, u32[]{:S(2)}, u32[]{:S(2)}) %all-to-all-start) | async-done | bytes 2097184 | tf_op jit(solution)/shard_map/all_to_all | solution.py:48
  46.0 6.1 %convert_bitcast_fusion = bf16[1024,1024]{0,1:T(8,128)(2,1)} fusion(bf16[1024,1024]{1,0:T(8,128)(2,1)S(1)} %bitcast.175, bf16[128,8,8,128]{3,2,1,0:T(8,128)(2,1)} %bitcast.177), kind=kOutput, calls=%fused_computation.13 | convolution fusion | flops 2148532224 | bytes 6291456 | tf_op jit(solution)/shard_map/dot_general | solution.py:90
  52.1 3.9 %copy.134 = bf16[1024,1024]{1,0:T(8,128)(2,1)} copy(bf16[1024,1024]{0,1:T(8,128)(2,1)} %convert_bitcast_fusion) | data formatting | bytes 4194304
  59.1 3.5 collective-permute-done
  63.3 3.4 collective-permute-start.1
  68.4 6.0 %collective-permute-start.2 = (f32[1025]{0:T(1024)S(1)}, f32[1025]{0:T(1024)S(1)}, u32[]{:S(2)}, u32[]{:S(2)}) collective-permute-start(f32[1025]{0:T(1024)S(1)} %add.210), channel_id=1, source_target_pairs={{0,4},{1,5},{2,6},{3,7},{4,0},{5,1},{6,2},{7,3},{8,12},{9,13},{10,... | collective-permute-start | bytes 12308 | tf_op jit(solution)/shard_map/ppermute | solution.py:40
  86.4 2.8 collective-permute-done.5
  95.8 3.5 collective-permute-done.7
  103.8 44.5 %all-gather.3.cloned.1.call-done = bf16[1024,1024]{0,1:T(8,128)(2,1)} async-done(((bf16[128,1024]{0,1:T(8,128)(2,1)}), bf16[1024,1024]{0,1:T(8,128)(2,1)}) %all-gather.3.cloned.1.call-update) | async-done | bytes 2097168 | tf_op jit(solution)/shard_map/all_gather | solution.py:97
  148.3 4.0 %fusion.13 = bf16[1024,1024]{1,0:T(8,128)(2,1)S(1)} fusion(bf16[1024,1024]{0,1:T(8,128)(2,1)} %all-gather.3.cloned.1.call-done, bf16[128,8,8,128]{3,2,1,0:T(8,128)(2,1)S(1)} %bitcast.180), kind=kOutput, calls=%fused_computation.16 | convolution fusion | flops 2148532224 | bytes 6291456 | tf_op jit(solution)/shard_map/dot_general | solution.py:99
  152.3 34.9 %all_to_all.20 = bf16[32,32,1024]{2,1,0:T(8,128)(2,1)S(1)} all-to-all(bf16[32,32,1024]{2,1,0:T(8,128)(2,1)S(1)} %bitcast.183), channel_id=1, replica_groups=mesh['wide'=32,'blk'=8] {'wide'}, dimensions={0} | all-to-all | bytes 4194304 | tf_op jit(solution)/shard_map/all_to_all | solution.py:55
  188.4 32.0 %all_to_all.21 = bf16[32,32,1024]{2,1,0:T(8,128)(2,1)S(1)} all-to-all(bf16[32,32,1024]{2,1,0:T(8,128)(2,1)S(1)} %broadcast_in_dim.385), channel_id=1, replica_groups=mesh['wide'=32,'blk'=8] {'wide'}, dimensions={0} | all-to-all | bytes 4194304 | tf_op jit(solution)/shard_map/all_to_all | solution.py:48
  220.4 3.7 fusion.16
  224.2 37.9 %reduce-scatter.9.cloned.1.call-done = bf16[128,1024]{1,0:T(8,128)(2,1)} async-done(((bf16[1024,1024]{1,0:T(8,128)(2,1)}), bf16[128,1024]{1,0:T(8,128)(2,1)}) %reduce-scatter.9.cloned.1.call-update) | async-done | bytes 262160
  266.4 2.7 copy.115
  269.1 4.6 %convolution_bitcast_fusion = f32[8,8,128,128]{3,2,1,0:T(8,128)S(1)} fusion(bf16[8,128,1024,1]{2,1,3,0:T(8,128)(2,1)} %bitcast.182, bf16[8,128,1024,1]{2,1,0,3:T(8,128)(2,1)} %bitcast.207), kind=kOutput, calls=%fused_computation.2 | convolution fusion | flops 2147483648 | bytes 8388608 | tf_op jit(solution)/shard_map/dot_general | solution.py:126
  283.1 3.1 add_multiply_fusion
  286.9 3.0 collective-permute-done.8
  291.2 4.1 %collective-permute-start.9 = (f32[1]{0:T(128)}, f32[1]{0:T(128)}, u32[]{:S(2)}, u32[]{:S(2)}) collective-permute-start(f32[1]{0:T(128)} %add.221), channel_id=1, source_target_pairs={{0,2},{1,3},{2,0},{3,1},{4,6},{5,7},{6,4},{7,5},{8,10},{9,11},{10,... | collective-permute-start | bytes 20 | tf_op jit(solution)/shard_map/ppermute | solution.py:40
  296.4 4.9 %collective-permute-start.10 = (f32[1]{0:T(128)}, f32[1]{0:T(128)}, u32[]{:S(2)}, u32[]{:S(2)}) collective-permute-start(f32[1]{0:T(128)} %add.222), channel_id=1, source_target_pairs={{0,4},{1,5},{2,6},{3,7},{4,0},{5,1},{6,2},{7,3},{8,12},{9,13},{10,... | collective-permute-start | bytes 20 | tf_op jit(solution)/shard_map/ppermute | solution.py:40
  301.4 2.7 collective-permute-done.10
  306.7 2.8 collective-permute-start.12
  311.0 4.4 %collective-permute-start.13 = (f32[1]{0:T(128)}, f32[1]{0:T(128)}, u32[]{:S(2)}, u32[]{:S(2)}) collective-permute-start(f32[1]{0:T(128)} %add.225), channel_id=1, source_target_pairs={{0,32},{8,40},{16,48},{24,56},{32,0},{40,8},{48,16},{56,24},{64,96... | collective-permute-start | bytes 20 | tf_op jit(solution)/shard_map/ppermute | solution.py:40
  316.9 2.7 collective-permute-start.14
  321.2 4.4 %collective-permute-start.15 = (f32[1]{0:T(128)}, f32[1]{0:T(128)}, u32[]{:S(2)}, u32[]{:S(2)}) collective-permute-start(f32[1]{0:T(128)} %add.227), channel_id=1, source_target_pairs={{0,128},{8,136},{16,144},{24,152},{32,160},{40,168},{48,176},{56,1... | collective-permute-start | bytes 20 | tf_op jit(solution)/shard_map/ppermute | solution.py:40
  327.1 6.0 %fusion.10 = bf16[1024,1024]{1,0:T(8,128)(2,1)} fusion(bf16[1024,1024]{0,1:T(8,128)(2,1)} %all-gather.5.cloned.1.call-done, bf16[128,8,8,128]{3,2,1,0:T(8,128)(2,1)} %bitcast.178), kind=kOutput, calls=%fused_computation.15 | convolution fusion | flops 2148532224 | bytes 6291456 | tf_op jit(solution)/shard_map/dot_general | solution.py:117
  333.1 7.4 %all-to-all-start.3 = ((bf16[32,32,1024]{2,1,0:T(8,128)(2,1)}), bf16[32,32,1024]{2,1,0:T(8,128)(2,1)S(1)}, u32[]{:S(2)}, u32[]{:S(2)}) async-start(bf16[32,32,1024]{2,1,0:T(8,128)(2,1)} %bitcast.179), calls=%async_computation.3 | async-start | bytes 4194304 | tf_op jit(solution)/shard_map/all_to_all | solution.py:55
  340.5 4.5 %convolution_bitcast_fusion.1 = f32[128,8,8,128]{3,1,2,0:T(8,128)S(1)} fusion(bf16[1024,1024]{0,1:T(8,128)(2,1)} %all-gather.5.cloned.1.call-done, bf16[1024,1024]{1,0:T(8,128)(2,1)} %bitcast.176), kind=kOutput, calls=%fused_computation.3 | convolution fusion | flops 2147483648 | bytes 8388608 | tf_op jit(solution)/shard_map/dot_general | solution.py:122
  346.1 4.7 %fusion.40 = (f32[1,8,128,128]{2,0,3,1:T(1,128)}, f32[1,8,128,128]{2,0,3,1:T(1,128)S(1)}, f32[1,8,128,128]{2,0,3,1:T(1,128)}, f32[1,8,128,128]{2,0,3,1:T(1,128)}...) fusion(f32[8,8,128,128]{2,0,3,1:T(8,128)S(1)} %bitcast.164), kind=kLoop, calls=%fused_computation.76 | loop fusion | bytes 8388608 | tf_op jit(solution)/shard_map/slice | solution.py:32
  364.6 3.4 subtract_bitcast_fusion
  (114 shorter events, 64.7 us)
Async XLA Ops:
  9.6 7.5 %copy-start.9 = (s32[8,1]{0,1:T(1,128)S(1)}, s32[8,1]{0,1:T(1,128)}, u32[]{:S(2)}) copy-start(s32[8,1]{0,1:T(1,128)} %param.13) | copy-start | bytes 100
  9.6 7.6 %copy-start.5 = (bf16[8,1,2,128,128]{4,3,2,1,0:T(8,128)(2,1)S(1)}, bf16[8,1,2,128,128]{4,3,2,1,0:T(8,128)(2,1)}, u32[]{:S(2)}) copy-start(bf16[8,1,2,128,128]{4,3,2,1,0:T(8,128)(2,1)} %param.11) | copy-start | bytes 1572868
  9.6 36.4 %all-to-all-start = ((bf16[32,32,1024]{2,1,0:T(8,128)(2,1)}), bf16[32,32,1024]{2,1,0:T(8,128)(2,1)S(1)}, u32[]{:S(2)}, u32[]{:S(2)}) async-start(bf16[32,32,1024]{2,1,0:T(8,128)(2,1)} %broadcast_in_dim.372), calls=%async_computation | async-start | bytes 4194304 | tf_op jit(solution)/shard_map/all_to_all | solution.py:48
  17.0 83.7 %reduce-scatter.7.cloned.1.call-start = ((), (), s32[]{:S(2)}) async-start(), calls=%async_computation.8 | async-start | bytes 2359296
  18.3 0.7 copy-start.8
  46.0 6.1 %copy-start.1 = (bf16[32,32,1024]{2,1,0:T(8,128)(2,1)}, bf16[32,32,1024]{2,1,0:T(8,128)(2,1)S(1)}, u32[]{:S(2)}) copy-start(bf16[32,32,1024]{2,1,0:T(8,128)(2,1)S(1)} %all-to-all-done) | copy-start | bytes 6291460
  56.0 0.7 copy-start.4
  56.1 92.3 %all-gather.3.cloned.1.call-start = ((), (), s32[]{:S(2)}) async-start(), calls=%async_computation.6 | async-start | bytes 2359296 | tf_op jit(solution)/shard_map/all_gather | solution.py:97
  58.9 3.7 collective-permute-start
  63.3 5.1 %collective-permute-start.1 = (f32[1025]{0:T(1024)S(1)}, f32[1025]{0:T(1024)S(1)}, u32[]{:S(2)}, u32[]{:S(2)}) collective-permute-start(f32[1025]{0:T(1024)S(1)} %fusion.38), channel_id=1, source_target_pairs={{0,2},{1,3},{2,0},{3,1},{4,6},{5,7},{6,4},{7,5},{8,10},{9,11},{10,... | collective-permute-start | bytes 12308 | tf_op jit(solution)/shard_map/ppermute | solution.py:40
  68.4 7.7 %collective-permute-start.2 = (f32[1025]{0:T(1024)S(1)}, f32[1025]{0:T(1024)S(1)}, u32[]{:S(2)}, u32[]{:S(2)}) collective-permute-start(f32[1025]{0:T(1024)S(1)} %add.210), channel_id=1, source_target_pairs={{0,4},{1,5},{2,6},{3,7},{4,0},{5,1},{6,2},{7,3},{8,12},{9,13},{10,... | collective-permute-start | bytes 12308 | tf_op jit(solution)/shard_map/ppermute | solution.py:40
  77.3 1.2 collective-permute-start.3
  79.9 3.6 collective-permute-start.4
  84.1 5.1 %collective-permute-start.5 = (f32[1]{0:T(128)}, f32[1]{0:T(128)}, u32[]{:S(2)}, u32[]{:S(2)}) collective-permute-start(f32[1]{0:T(128)} %add.213), channel_id=1, source_target_pairs={{0,32},{8,40},{16,48},{24,56},{32,0},{40,8},{48,16},{56,24},{64,96... | collective-permute-start | bytes 20 | tf_op jit(solution)/shard_map/ppermute | solution.py:40
  89.9 3.6 collective-permute-start.6
  94.2 5.1 %collective-permute-start.7 = (f32[1]{0:T(128)}, f32[1]{0:T(128)}, u32[]{:S(2)}, u32[]{:S(2)}) collective-permute-start(f32[1]{0:T(128)} %add.215), channel_id=1, source_target_pairs={{0,128},{8,136},{16,144},{24,152},{32,160},{40,168},{48,176},{56,1... | collective-permute-start | bytes 20 | tf_op jit(solution)/shard_map/ppermute | solution.py:40
  102.8 159.3 %reduce-scatter.9.cloned.1.call-start = ((), (), s32[]{:S(2)}) async-start(), calls=%async_computation.9 | async-start | bytes 2359296
  103.8 48.5 %copy-start.2 = (bf16[8,128,8,128]{3,2,1,0:T(8,128)(2,1)}, bf16[8,128,8,128]{3,2,1,0:T(8,128)(2,1)S(1)}, u32[]{:S(2)}) copy-start(bf16[8,128,8,128]{3,2,1,0:T(8,128)(2,1)S(1)} %select_add_fusion) | copy-start | bytes 6291460
  187.3 0.8 copy-start.7
  188.1 32.3 %copy-start.6 = (bf16[32,1024]{1,0:T(8,128)(2,1)}, bf16[32,1024]{1,0:T(8,128)(2,1)S(1)}, u32[]{:S(2)}) copy-start(bf16[32,1024]{1,0:T(8,128)(2,1)S(1)} %reduce_sum.50) | copy-start | bytes 196612
  188.4 32.0 %copy-start.3 = (bf16[8,128,8,128]{3,2,1,0:T(8,128)(2,1)S(1)}, bf16[8,128,8,128]{3,2,1,0:T(8,128)(2,1)}, u32[]{:S(2)}) copy-start(bf16[8,128,8,128]{3,2,1,0:T(8,128)(2,1)} %copy-done.2) | copy-start | bytes 6291460
  224.2 103.0 %all-gather.5.cloned.1.call-start = ((), (), s32[]{:S(2)}) async-start(), calls=%async_computation.7 | async-start | bytes 2359296 | tf_op jit(solution)/shard_map/all_gather | solution.py:114
  281.9 1.2 copy-start
  286.1 3.8 %collective-permute-start.8 = (f32[1]{0:T(128)}, f32[1]{0:T(128)}, u32[]{:S(2)}, u32[]{:S(2)}) collective-permute-start(f32[1]{0:T(128)} %bitcast.30), channel_id=1, source_target_pairs={{0,1},{1,0},{2,3},{3,2},{4,5},{5,4},{6,7},{7,6},{8,9},{9,8},{10,11... | collective-permute-start | bytes 20 | tf_op jit(solution)/shard_map/ppermute | solution.py:40
  291.2 4.6 %collective-permute-start.9 = (f32[1]{0:T(128)}, f32[1]{0:T(128)}, u32[]{:S(2)}, u32[]{:S(2)}) collective-permute-start(f32[1]{0:T(128)} %add.221), channel_id=1, source_target_pairs={{0,2},{1,3},{2,0},{3,1},{4,6},{5,7},{6,4},{7,5},{8,10},{9,11},{10,... | collective-permute-start | bytes 20 | tf_op jit(solution)/shard_map/ppermute | solution.py:40
  296.4 7.6 %collective-permute-start.10 = (f32[1]{0:T(128)}, f32[1]{0:T(128)}, u32[]{:S(2)}, u32[]{:S(2)}) collective-permute-start(f32[1]{0:T(128)} %add.222), channel_id=1, source_target_pairs={{0,4},{1,5},{2,6},{3,7},{4,0},{5,1},{6,2},{7,3},{8,12},{9,13},{10,... | collective-permute-start | bytes 20 | tf_op jit(solution)/shard_map/ppermute | solution.py:40
  304.7 1.3 collective-permute-start.11
  306.7 3.7 collective-permute-start.12
  311.0 5.2 %collective-permute-start.13 = (f32[1]{0:T(128)}, f32[1]{0:T(128)}, u32[]{:S(2)}, u32[]{:S(2)}) collective-permute-start(f32[1]{0:T(128)} %add.225), channel_id=1, source_target_pairs={{0,32},{8,40},{16,48},{24,56},{32,0},{40,8},{48,16},{56,24},{64,96... | collective-permute-start | bytes 20 | tf_op jit(solution)/shard_map/ppermute | solution.py:40
  316.9 3.7 collective-permute-start.14
  321.2 5.2 %collective-permute-start.15 = (f32[1]{0:T(128)}, f32[1]{0:T(128)}, u32[]{:S(2)}, u32[]{:S(2)}) collective-permute-start(f32[1]{0:T(128)} %add.227), channel_id=1, source_target_pairs={{0,128},{8,136},{16,144},{24,152},{32,160},{40,168},{48,176},{56,1... | collective-permute-start | bytes 20 | tf_op jit(solution)/shard_map/ppermute | solution.py:40
  333.1 36.0 %all-to-all-start.3 = ((bf16[32,32,1024]{2,1,0:T(8,128)(2,1)}), bf16[32,32,1024]{2,1,0:T(8,128)(2,1)S(1)}, u32[]{:S(2)}, u32[]{:S(2)}) async-start(bf16[32,32,1024]{2,1,0:T(8,128)(2,1)} %bitcast.179), calls=%async_computation.3 | async-start | bytes 4194304 | tf_op jit(solution)/shard_map/all_to_all | solution.py:55
Sparse Core Ops, SparseCore 0:
  56.2 40.3 reduce-scatter.6
  102.9 45.3 all-gather.2
  224.3 37.7 reduce-scatter.8
  265.1 46.7 all-gather.4

commit v5 on v4

--- a/solution.py
+++ b/solution.py
@@ -56,6 +56,24 @@
     return jnp.sum(received.astype(jnp.float32), axis=0)
 
 
+def split_three(value):
+    high = value.astype(jnp.bfloat16)
+    rest = value - high.astype(jnp.float32)
+    middle = rest.astype(jnp.bfloat16)
+    low = (rest - middle.astype(jnp.float32)).astype(jnp.bfloat16)
+    return jnp.stack([high, middle, low])
+
+
+def join_three(pieces):
+    pieces = pieces.astype(jnp.float32)
+    return pieces[..., 0] + pieces[..., 1] + pieces[..., 2]
+
+
+def with_row(rows, pieces):
+    extra = jnp.zeros((1, rows.shape[1]), rows.dtype).at[0, : pieces.shape[0]].set(pieces)
+    return jnp.concatenate([rows, extra], axis=0)
+
+
 def body(tokens, target, probe_vector, weight_in, weight_out, slot_rows, slot_count):
     columns, unit, slots, block, width_two = weight_in.shape
     features = tokens.shape[1]
@@ -73,9 +91,11 @@
     image_part = jnp.einsum(
         "jsk,jskn->jn", chosen, tiles_in.astype(jnp.float32), precision=lax.Precision.HIGHEST
     )
+    x_full = gather_rows(tokens, "wide")
     image_and_norm = butterfly_sum(
         jnp.concatenate([image_part.reshape(-1), jnp.sum(probe_vector * probe_vector)[None]]), "blk"
     )
+    x_full, image_and_norm = lax.optimization_barrier((x_full, image_and_norm))
     image = image_and_norm[:-1].reshape(image_part.shape)
     norm_probe = image_and_norm[-1]
     norm_image = butterfly_sum(jnp.sum(image * image)[None], "wide")[0]
@@ -86,7 +106,6 @@
         spread_tiles(tiles_out, row_index, feature_blocks), (2, 1, 0, 3)
     ).reshape(hidden_width, features)
 
-    x_full = gather_rows(tokens, "wide")
     pre_part = jnp.dot(x_full, w1, preferred_element_type=jnp.float32)
     pre_own = lax.psum_scatter(
         pre_part.astype(jnp.bfloat16), "blk", scatter_dimension=0, tiled=True
@@ -108,16 +127,28 @@
         back_part.astype(jnp.bfloat16), "blk", scatter_dimension=0, tiled=True
     ).astype(jnp.float32)
     slope_own = (back_own * activate_slope(hidden_own)).astype(jnp.bfloat16)
-    curvature = butterfly_sum(
-        butterfly_sum(jnp.sum(slope_own.astype(jnp.float32) * pre_own)[None], "blk"), "wide"
-    )[0]
-    slope_full = lax.all_gather(slope_own, "blk", axis=0, tiled=True)
-    slope_full, curvature = lax.optimization_barrier((slope_full, curvature))
+    curvature_part = jnp.sum(slope_own.astype(jnp.float32) * pre_own)
+    slope_rows = lax.all_gather(
+        with_row(slope_own, split_three(curvature_part)), "blk", axis=0, tiled=False
+    )
+    slope_full = slope_rows[:, :-1].reshape(-1, slope_own.shape[1])
+    curvature_blk = jnp.sum(join_three(slope_rows[:, -1, :3]))
 
     in_part = lax.dot_general(
         slope_full, w1, (((1,), (1,)), ((), ())), preferred_element_type=jnp.float32
     )
-    token_grad = (sum_rows(in_part.astype(jnp.bfloat16), "wide") / spectral).astype(jnp.bfloat16)
+    size = lax.axis_size("wide")
+    in_rows = in_part.astype(jnp.bfloat16).reshape(size, -1, features)
+    extra = jnp.zeros((size, 1, features), jnp.bfloat16).at[:, 0, :3].set(
+        split_three(curvature_blk)[None]
+    )
+    received = lax.all_to_all(
+        jnp.concatenate([in_rows, extra], axis=1), "wide", 0, 0, tiled=False
+    )
+    token_grad = (
+        jnp.sum(received[:, :-1].astype(jnp.float32), axis=0) / spectral
+    ).astype(jnp.bfloat16)
+    curvature = jnp.sum(join_three(received[:, -1, :3]))
 
     g1 = lax.dot_general(
         x_full, slope_full, (((0,), (0,)), ((), ())), preferred_element_type=jnp.float32

time: 379 us -> 365 us (0.963)
  starting transfers between devices: 56.5 us -> 31.4 us
  waiting for transfers between devices: 138 us -> 147 us
  other arithmetic: 16.8 us -> 25.7 us
  matrix products: 29.3 us -> 25.4 us
    reduce_scatter x0 -> x2, waiting for transfers between devices: none -> 52.4 us  [the longest x1 36.9 us: body(): lax.psum_scatter(back_part.astype(jnp.bfloat16), 'blk', scatter_dimension...]
    unnamed x6 -> x4, waiting for transfers between devices: 38 us -> 0.07 us
    all_gather x1, waiting for transfers between devices: 0.02 us -> 29.8 us  [body(): lax.all_gather(with_row(slope_own, split_three(curvature_part)), 'blk', a...]
    ppermute x16 -> x8, starting transfers between devices: 41.3 us -> 16.4 us  [butterfly_sum(): lax.ppermute(value, axis, [(i, i ^ step) for i in range(size)])]
    all_to_all x1, waiting for transfers between devices: 25.2 us -> 9.12 us  [gather_rows(): gathered = lax.all_to_all(spread, axis, 0, 0, tiled=False)]
    ppermute x16 -> x8, waiting for transfers between devices: 29.1 us -> 17.1 us  [butterfly_sum(): lax.ppermute(value, axis, [(i, i ^ step) for i in range(size)])]
    unnamed x25 -> x29, local copies, waits for them, and re-layouts: 8.3 us -> 2.02 us
    all_gather x1, waiting for transfers between devices: 44.5 us -> 38.4 us  [body(): active_full = lax.all_gather(active_own, 'blk', axis=0, tiled=True)]
  transfers between devices with their start and end apart: 22 -> 14, of which waited for: 20 -> 12; matrix products, arithmetic and copies ran while one was open for 15% -> 15% of each run, Pallas kernels for 0% -> 0%
where the time goes in v5:
time: 365 us; the launch traced here: 361 us
  waiting for transfers between devices  147 us (40%)
  blocking collectives  67.1 us (18%)
  local copies, waits for them, and re-layouts  42.9 us (12%)
  starting transfers between devices  31.4 us (9%)
  other arithmetic  25.7 us (7%)
  matrix products  25.4 us (7%)
  between operations  22.2 us (6%)
    all_gather x1, waiting for transfers between devices, body(): active_full = lax.all_gather(active_own, 'blk', axis=0, tiled=True)  38.4 us
    reduce_scatter x1, waiting for transfers between devices, body(): lax.psum_scatter(back_part.astype(jnp.bfloat16), 'blk', scatter_dimension...  36.9 us
    all_to_all x1, blocking collectives, sum_rows(): received = lax.all_to_all(parts, axis, 0, 0, tiled=False)  35.1 us
    all_to_all x1, blocking collectives, gather_rows(): gathered = lax.all_to_all(spread, axis, 0, 0, tiled=False)  32 us
    all_gather x1, waiting for transfers between devices, body(): lax.all_gather(with_row(slope_own, split_three(curvature_part)), 'blk', a...  29.8 us
    broadcast_in_dim x18, local copies, waits for them, and re-layouts, pick_tiles(): jnp.where(hit[r][:, :, None, None], by_col[r][:, None], 0.0)  20.3 us
    ppermute x8, waiting for transfers between devices, butterfly_sum(): lax.ppermute(value, axis, [(i, i ^ step) for i in range(size)])  17.1 us
    ppermute x8, starting transfers between devices, butterfly_sum(): lax.ppermute(value, axis, [(i, i ^ step) for i in range(size)])  16.4 us
  transfers between devices with their start and end apart: 14, of which 12 were waited for; matrix products, arithmetic and copies ran while one was open for 15% of the time, Pallas kernels for 0%

profile of v5, /device:TPU:32, one launch (start us, length us, event | category | flops | bytes accessed | tf_op | source)
XLA Modules:
  0.0 361.5 jit_solution(12489624085435057459)
XLA Ops:
  7.2 2.4 broadcast_in_dim.364
  9.6 7.5 %all-to-all-start = ((bf16[32,32,1024]{2,1,0:T(8,128)(2,1)}), bf16[32,32,1024]{2,1,0:T(8,128)(2,1)S(1)}, u32[]{:S(2)}, u32[]{:S(2)}) async-start(bf16[32,32,1024]{2,1,0:T(8,128)(2,1)} %broadcast_in_dim.364), calls=%async_computation | async-start | bytes 4194304 | tf_op jit(solution)/shard_map/all_to_all | solution.py:48
  20.2 3.4 collective-permute-done
  24.3 3.4 collective-permute-start.1
  29.3 5.9 %collective-permute-start.2 = (f32[1025]{0:T(1024)S(1)}, f32[1025]{0:T(1024)S(1)}, u32[]{:S(2)}, u32[]{:S(2)}) collective-permute-start(f32[1025]{0:T(1024)S(1)} %add.208), channel_id=1, source_target_pairs={{0,4},{1,5},{2,6},{3,7},{4,0},{5,1},{6,2},{7,3},{8,12},{9,13},{10,... | collective-permute-start | bytes 12308 | tf_op jit(solution)/shard_map/ppermute | solution.py:40
  36.9 9.1 %all-to-all-done = bf16[32,32,1024]{2,1,0:T(8,128)(2,1)S(1)} async-done(((bf16[32,32,1024]{2,1,0:T(8,128)(2,1)}), bf16[32,32,1024]{2,1,0:T(8,128)(2,1)S(1)}, u32[]{:S(2)}, u32[]{:S(2)}) %all-to-all-start) | async-done | bytes 2097184 | tf_op jit(solution)/shard_map/all_to_all | solution.py:48
  46.0 5.3 %fusion.8 = bf16[1024,1024]{1,0:T(8,128)(2,1)} fusion(bf16[1024,1024]{1,0:T(8,128)(2,1)S(1)} %bitcast.184, bf16[128,8,8,128]{3,2,1,0:T(8,128)(2,1)} %bitcast.191), kind=kOutput, calls=%fused_computation.15 | convolution fusion | flops 2148532224 | bytes 6291456 | tf_op jit(solution)/shard_map/dot_general | solution.py:109
  56.5 2.3 collective-permute-done.4
  59.4 2.3 collective-permute-start.5
  61.7 2.9 collective-permute-done.5
  66.5 2.3 collective-permute-done.6
  71.3 3.4 collective-permute-done.7
  76.0 15.6 %reduce-scatter.3.cloned.1.call-done = bf16[128,1024]{1,0:T(8,128)(2,1)} async-done(((bf16[1024,1024]{1,0:T(8,128)(2,1)}), bf16[128,1024]{1,0:T(8,128)(2,1)}) %reduce-scatter.3.cloned.1.call-update) | async-done | bytes 262160 | tf_op jit(solution)/shard_map/reduce_scatter | solution.py:110
  95.6 38.4 %all-gather.5.cloned.1.call-done = bf16[1024,1024]{1,0:T(8,128)(2,1)} async-done(((bf16[128,1024]{1,0:T(8,128)(2,1)}), bf16[1024,1024]{1,0:T(8,128)(2,1)}) %all-gather.5.cloned.1.call-update) | async-done | bytes 2097168 | tf_op jit(solution)/shard_map/all_gather | solution.py:116
  134.1 4.5 %fusion.14 = bf16[1024,1024]{1,0:T(8,128)(2,1)S(1)} fusion(bf16[1024,1024]{1,0:T(8,128)(2,1)} %all-gather.5.cloned.1.call-done, bf16[128,8,8,128]{3,2,1,0:T(8,128)(2,1)} %bitcast.197), kind=kOutput, calls=%fused_computation.17 | convolution fusion | flops 2148532224 | bytes 6291456 | tf_op jit(solution)/shard_map/dot_general | solution.py:118
  138.6 35.1 %all_to_all.20 = bf16[32,32,1024]{2,1,0:T(8,128)(2,1)} all-to-all(bf16[32,32,1024]{2,1,0:T(8,128)(2,1)S(1)} %bitcast.200), channel_id=1, replica_groups=mesh['wide'=32,'blk'=8] {'wide'}, dimensions={0} | all-to-all | bytes 4194304 | tf_op jit(solution)/shard_map/all_to_all | solution.py:55
  176.0 32.0 %all_to_all.21 = bf16[32,32,1024]{2,1,0:T(8,128)(2,1)S(1)} all-to-all(bf16[32,32,1024]{2,1,0:T(8,128)(2,1)S(1)} %broadcast_in_dim.388), channel_id=1, replica_groups=mesh['wide'=32,'blk'=8] {'wide'}, dimensions={0} | all-to-all | bytes 4194304 | tf_op jit(solution)/shard_map/all_to_all | solution.py:48
  209.4 3.7 %fusion.17 = bf16[1024,1024]{1,0:T(8,128)(2,1)} fusion(bf16[1024,1024]{1,0:T(8,128)(2,1)S(1)} %bitcast.186, bf16[128,8,8,128]{3,2,1,0:T(8,128)(2,1)S(1)} %bitcast.198), kind=kOutput, calls=%fused_computation.18 | convolution fusion | flops 2148532224 | bytes 6291456 | tf_op jit(solution)/shard_map/dot_general | solution.py:123
  213.8 36.9 %reduce-scatter.5.cloned.1.call-done = bf16[128,1024]{1,0:T(8,128)(2,1)} async-done(((bf16[1024,1024]{1,0:T(8,128)(2,1)}), bf16[128,1024]{1,0:T(8,128)(2,1)}) %reduce-scatter.5.cloned.1.call-update) | async-done | bytes 262160 | tf_op jit(solution)/shard_map/reduce_scatter | solution.py:126
  256.2 2.6 copy.197
  259.5 4.1 %copy.198 = bf16[1024,1024]{1,0:T(8,128)(2,1)} copy(bf16[1024,1024]{0,1:T(8,128)(2,1)} %bitcast.193) | data formatting | bytes 4194304 | tf_op jit(solution)/shard_map/dot_general | solution.py:157
  263.6 2.7 copy.176
  266.2 29.8 %all-gather.7.cloned.1.call-done = bf16[8,129,1024]{2,1,0:T(8,128)(2,1)} async-done(((bf16[1,129,1024]{2,1,0:T(8,128)(2,1)}), bf16[8,129,1024]{2,1,0:T(8,128)(2,1)}) %all-gather.7.cloned.1.call-update) | async-done | bytes 2113552 | tf_op jit(solution)/shard_map/all_gather | solution.py:131
  301.0 2.4 fusion.11
  305.3 7.3 %all-to-all-start.3 = ((bf16[32,33,1024]{2,1,0:T(8,128)(2,1)}), bf16[32,33,1024]{2,1,0:T(8,128)(2,1)S(1)}, u32[]{:S(2)}, u32[]{:S(2)}) async-start(bf16[32,33,1024]{2,1,0:T(8,128)(2,1)} %pad_maximum_fusion), calls=%async_computation.5 | async-start | bytes 5242880 | tf_op jit(solution)/shard_map/all_to_all | solution.py:145
  312.6 4.6 %convolution_bitcast_fusion = f32[8,8,128,128]{3,2,1,0:T(8,128)S(1)} fusion(bf16[8,128,1024,1]{2,1,3,0:T(8,128)(2,1)} %bitcast.196, bf16[8,128,1024,1]{2,1,0,3:T(8,128)(2,1)} %bitcast.195), kind=kOutput, calls=%fused_computation.3 | convolution fusion | flops 2147483648 | bytes 8388608 | tf_op jit(solution)/shard_map/dot_general | solution.py:157
  317.2 2.1 slice_bitcast_fusion.7
  324.6 2.1 copy.186
  334.9 3.7 %add_multiply_fusion = f32[8,1,2,128,128]{4,3,2,1,0:T(8,128)} fusion(f32[8,2]{1,0:T(8,128)S(1)} %get-tuple-element.74, f32[8,128,128]{2,1,0:T(8,128)S(1)} %copy.192, f32[8,128,128]{2,1,0:T(8,128)} %copy.190, f32[8,128,128]{2,1,0:T(8,128)} %copy.188, f32[8,128,128]{2,1,0:T(8,128)} %copy.186, f32[8,128,128]{2,1,0:T(8,128)} %copy.184, ...), kind=kLoop, calls=%fused_computation.23 | loop fusion | flops 4194304 | bytes 5243072 | tf_op jit(solution)/shard_map/mul | solution.py:160
  338.6 4.0 %copy.165 = bf16[1024,1024]{0,1:T(8,128)(2,1)} copy(bf16[1024,1024]{1,0:T(8,128)(2,1)} %bitcast.189) | data formatting | bytes 4194304 | tf_op jit(solution)/shard_map/reshape | solution.py:134
  342.5 4.6 %convolution_bitcast_fusion.1 = f32[8,8,128,128]{3,2,1,0:T(8,128)S(1)} fusion(bf16[8,128,1024,1]{2,1,3,0:T(8,128)(2,1)} %bitcast.194, bf16[8,128,1024,1]{2,1,0,3:T(8,128)(2,1)} %bitcast.199), kind=kOutput, calls=%fused_computation.4 | convolution fusion | flops 2147483648 | bytes 8388608 | tf_op jit(solution)/shard_map/dot_general | solution.py:153
  351.5 3.5 subtract_bitcast_fusion
  (108 shorter events, 49.6 us)
Async XLA Ops:
  9.6 7.5 %copy-start.10 = (s32[8,1,2]{0,2,1:T(2,128)S(1)}, s32[8,1,2]{0,2,1:T(2,128)}, u32[]{:S(2)}) copy-start(s32[8,1,2]{0,2,1:T(2,128)} %param.16) | copy-start | bytes 196
  9.6 7.6 %copy-start.5 = (f32[1024]{0:T(1024)S(1)}, f32[1024]{0:T(1024)}, u32[]{:S(2)}) copy-start(f32[1024]{0:T(1024)} %param.13) | copy-start | bytes 12292
  9.6 9.1 %copy-start.11 = (s32[8,1]{0,1:T(1,128)S(1)}, s32[8,1]{0,1:T(1,128)}, u32[]{:S(2)}) copy-start(s32[8,1]{0,1:T(1,128)} %param.17) | copy-start | bytes 100
  9.6 9.2 %copy-start.6 = (bf16[8,1,2,128,128]{4,3,2,1,0:T(8,128)(2,1)S(1)}, bf16[8,1,2,128,128]{4,3,2,1,0:T(8,128)(2,1)}, u32[]{:S(2)}) copy-start(bf16[8,1,2,128,128]{4,3,2,1,0:T(8,128)(2,1)} %param.15) | copy-start | bytes 1572868
  9.6 9.2 %copy-start.7 = (bf16[8,1,2,128,128]{4,3,2,1,0:T(8,128)(2,1)S(1)}, bf16[8,1,2,128,128]{4,3,2,1,0:T(8,128)(2,1)}, u32[]{:S(2)}) copy-start(bf16[8,1,2,128,128]{4,3,2,1,0:T(8,128)(2,1)} %param.14) | copy-start | bytes 1572868
  9.6 36.4 %all-to-all-start = ((bf16[32,32,1024]{2,1,0:T(8,128)(2,1)}), bf16[32,32,1024]{2,1,0:T(8,128)(2,1)S(1)}, u32[]{:S(2)}, u32[]{:S(2)}) async-start(bf16[32,32,1024]{2,1,0:T(8,128)(2,1)} %broadcast_in_dim.364), calls=%async_computation | async-start | bytes 4194304 | tf_op jit(solution)/shard_map/all_to_all | solution.py:48
  17.1 74.4 %reduce-scatter.3.cloned.1.call-start = ((), (), s32[]{:S(2)}) async-start(), calls=%async_computation.6 | async-start | bytes 2359296 | tf_op jit(solution)/shard_map/reduce_scatter | solution.py:110
  19.9 3.7 %collective-permute-start = (f32[1025]{0:T(1024)S(1)}, f32[1025]{0:T(1024)S(1)}, u32[]{:S(2)}, u32[]{:S(2)}) collective-permute-start(f32[1025]{0:T(1024)S(1)} %pad_maximum_fusion.1), channel_id=1, source_target_pairs={{0,1},{1,0},{2,3},{3,2},{4,5},{5,4},{6,7},{7,6},{8,9},{9,8},{10,11... | collective-permute-start | bytes 12308 | tf_op jit(solution)/shard_map/ppermute | solution.py:40
  24.3 5.0 %collective-permute-start.1 = (f32[1025]{0:T(1024)S(1)}, f32[1025]{0:T(1024)S(1)}, u32[]{:S(2)}, u32[]{:S(2)}) collective-permute-start(f32[1025]{0:T(1024)S(1)} %fusion.47), channel_id=1, source_target_pairs={{0,2},{1,3},{2,0},{3,1},{4,6},{5,7},{6,4},{7,5},{8,10},{9,11},{10,... | collective-permute-start | bytes 12308 | tf_op jit(solution)/shard_map/ppermute | solution.py:40
  29.3 7.6 %collective-permute-start.2 = (f32[1025]{0:T(1024)S(1)}, f32[1025]{0:T(1024)S(1)}, u32[]{:S(2)}, u32[]{:S(2)}) collective-permute-start(f32[1025]{0:T(1024)S(1)} %add.208), channel_id=1, source_target_pairs={{0,4},{1,5},{2,6},{3,7},{4,0},{5,1},{6,2},{7,3},{8,12},{9,13},{10,... | collective-permute-start | bytes 12308 | tf_op jit(solution)/shard_map/ppermute | solution.py:40
  51.3 82.8 %all-gather.5.cloned.1.call-start = ((), (), s32[]{:S(2)}) async-start(), calls=%async_computation.7 | async-start | bytes 2359296 | tf_op jit(solution)/shard_map/all_gather | solution.py:116
  52.5 1.4 collective-permute-start.3
  55.1 3.7 %collective-permute-start.4 = (f32[1]{0:T(128)}, f32[1]{0:T(128)}, u32[]{:S(2)}, u32[]{:S(2)}) collective-permute-start(f32[1]{0:T(128)} %add.212), channel_id=1, source_target_pairs={{0,16},{8,24},{16,0},{24,8},{32,48},{40,56},{48,32},{56,40},{64,80... | collective-permute-start | bytes 20 | tf_op jit(solution)/shard_map/ppermute | solution.py:40
  59.4 5.2 %collective-permute-start.5 = (f32[1]{0:T(128)}, f32[1]{0:T(128)}, u32[]{:S(2)}, u32[]{:S(2)}) collective-permute-start(f32[1]{0:T(128)} %add.213), channel_id=1, source_target_pairs={{0,32},{8,40},{16,48},{24,56},{32,0},{40,8},{48,16},{56,24},{64,96... | collective-permute-start | bytes 20 | tf_op jit(solution)/shard_map/ppermute | solution.py:40
  65.2 3.7 %collective-permute-start.6 = (f32[1]{0:T(128)}, f32[1]{0:T(128)}, u32[]{:S(2)}, u32[]{:S(2)}) collective-permute-start(f32[1]{0:T(128)} %add.214), channel_id=1, source_target_pairs={{0,64},{8,72},{16,80},{24,88},{32,96},{40,104},{48,112},{56,120},{... | collective-permute-start | bytes 20 | tf_op jit(solution)/shard_map/ppermute | solution.py:40
  69.5 5.2 %collective-permute-start.7 = (f32[1]{0:T(128)}, f32[1]{0:T(128)}, u32[]{:S(2)}, u32[]{:S(2)}) collective-permute-start(f32[1]{0:T(128)} %add.215), channel_id=1, source_target_pairs={{0,128},{8,136},{16,144},{24,152},{32,160},{40,168},{48,176},{56,1... | collective-permute-start | bytes 20 | tf_op jit(solution)/shard_map/ppermute | solution.py:40
  93.5 157.2 %reduce-scatter.5.cloned.1.call-start = ((), (), s32[]{:S(2)}) async-start(), calls=%async_computation.8 | async-start | bytes 2359296 | tf_op jit(solution)/shard_map/reduce_scatter | solution.py:126
  173.7 2.0 copy-start.9
  175.7 32.3 %copy-start.8 = (bf16[32,1024]{1,0:T(8,128)(2,1)}, bf16[32,1024]{1,0:T(8,128)(2,1)S(1)}, u32[]{:S(2)}) copy-start(bf16[32,1024]{1,0:T(8,128)(2,1)S(1)} %reduce_sum.68) | copy-start | bytes 196612
  176.0 33.4 %copy-start.4 = (bf16[8,128,8,128]{3,2,1,0:T(8,128)(2,1)S(1)}, bf16[8,128,8,128]{3,2,1,0:T(8,128)(2,1)}, u32[]{:S(2)}) copy-start(bf16[8,128,8,128]{3,2,1,0:T(8,128)(2,1)} %select_add_fusion) | copy-start | bytes 6291460
  208.0 1.4 copy-start
  213.1 82.8 %all-gather.7.cloned.1.call-start = ((), (), s32[]{:S(2)}) async-start(), calls=%async_computation.9 | async-start | bytes 2506752 | tf_op jit(solution)/shard_map/all_gather | solution.py:131
  259.4 4.1 %copy-start.1 = (bf16[32,32,1024]{2,1,0:T(8,128)(2,1)S(1)}, bf16[32,32,1024]{2,1,0:T(8,128)(2,1)}, u32[]{:S(2)}) copy-start(bf16[32,32,1024]{2,1,0:T(8,128)(2,1)} %copy-done) | copy-start | bytes 6291460
  298.7 2.2 copy-start.3
  300.7 2.7 copy-start.2
  305.3 43.7 %all-to-all-start.3 = ((bf16[32,33,1024]{2,1,0:T(8,128)(2,1)}), bf16[32,33,1024]{2,1,0:T(8,128)(2,1)S(1)}, u32[]{:S(2)}, u32[]{:S(2)}) async-start(bf16[32,33,1024]{2,1,0:T(8,128)(2,1)} %pad_maximum_fusion), calls=%async_computation.5 | async-start | bytes 5242880 | tf_op jit(solution)/shard_map/all_to_all | solution.py:145
Sparse Core Ops, SparseCore 0:
  51.4 40.0 reduce-scatter.2
  93.9 40.1 all-gather.4
  213.3 37.3 reduce-scatter.4
  255.6 40.3 all-gather.6

commit v6 on v5

--- a/solution.py
+++ b/solution.py
@@ -126,6 +126,12 @@
     back_own = lax.psum_scatter(
         back_part.astype(jnp.bfloat16), "blk", scatter_dimension=0, tiled=True
     ).astype(jnp.float32)
+    g2 = lax.dot_general(
+        error_full, active_full, (((0,), (0,)), ((), ())), preferred_element_type=jnp.float32
+    )
+    grad_out = pick_tiles(g2.reshape(feature_blocks, block, columns, block), row_index) * mask_full
+    grad_out = jnp.transpose(grad_out, (0, 1, 3, 2))
+    back_own, grad_out = lax.optimization_barrier((back_own, grad_out))
     slope_own = (back_own * activate_slope(hidden_own)).astype(jnp.bfloat16)
     curvature_part = jnp.sum(slope_own.astype(jnp.float32) * pre_own)
     slope_rows = lax.all_gather(
@@ -154,11 +160,6 @@
         x_full, slope_full, (((0,), (0,)), ((), ())), preferred_element_type=jnp.float32
     )
     raw_in = pick_tiles(g1.reshape(feature_blocks, block, columns, block), row_index) * mask_full
-    g2 = lax.dot_general(
-        error_full, active_full, (((0,), (0,)), ((), ())), preferred_element_type=jnp.float32
-    )
-    grad_out = pick_tiles(g2.reshape(feature_blocks, block, columns, block), row_index) * mask_full
-    grad_out = jnp.transpose(grad_out, (0, 1, 3, 2))
 
     outer = jnp.einsum("jsk,jn->jskn", chosen, image) * mask_full
     grad_in = raw_in / spectral - curvature / (spectral**3 * norm_probe) * outer

time: 365 us -> 360 us (0.986)
  local copies, waits for them, and re-layouts: 42.9 us -> 36 us
  waiting for transfers between devices: 147 us -> 153 us
    reduce_scatter x1, waiting for transfers between devices: 36.9 us -> 11.3 us  [body(): lax.psum_scatter(back_part.astype(jnp.bfloat16), 'blk', scatter_dimension...]
    all_to_all x1, waiting for transfers between devices: 0.01 us -> 19.5 us  [body(): lax.all_to_all(jnp.concatenate([in_rows, extra], axis=1), 'wide', 0, 0, t...]
    all_gather x1, waiting for transfers between devices: 29.8 us -> 40.5 us  [body(): lax.all_gather(with_row(slope_own, split_three(curvature_part)), 'blk', a...]
    broadcast_in_dim x18, local copies, waits for them, and re-layouts: 20.3 us -> 13.1 us  [pick_tiles(): jnp.where(hit[r][:, :, None, None], by_col[r][:, None], 0.0)]
  transfers between devices with their start and end apart: 14 -> 14, of which waited for: 12 -> 13; matrix products, arithmetic and copies ran while one was open for 15% -> 13% of each run, Pallas kernels for 0% -> 0%
where the time goes in v6:
time: 360 us; the launch traced here: 357 us
  waiting for transfers between devices  153 us (42%)
  blocking collectives  67 us (19%)
  local copies, waits for them, and re-layouts  36 us (10%)
  starting transfers between devices  31.4 us (9%)
  matrix products  25.5 us (7%)
  other arithmetic  22.4 us (6%)
  between operations  22 us (6%)
    all_gather x1, waiting for transfers between devices, body(): lax.all_gather(with_row(slope_own, split_three(curvature_part)), 'blk', a...  40.5 us
    all_gather x1, waiting for transfers between devices, body(): active_full = lax.all_gather(active_own, 'blk', axis=0, tiled=True)  39.7 us
    all_to_all x1, blocking collectives, sum_rows(): received = lax.all_to_all(parts, axis, 0, 0, tiled=False)  34.9 us
    all_to_all x1, blocking collectives, gather_rows(): gathered = lax.all_to_all(spread, axis, 0, 0, tiled=False)  32 us
    all_to_all x1, waiting for transfers between devices, body(): lax.all_to_all(jnp.concatenate([in_rows, extra], axis=1), 'wide', 0, 0, t...  19.5 us
    ppermute x8, waiting for transfers between devices, butterfly_sum(): lax.ppermute(value, axis, [(i, i ^ step) for i in range(size)])  17.1 us
    ppermute x8, starting transfers between devices, butterfly_sum(): lax.ppermute(value, axis, [(i, i ^ step) for i in range(size)])  16.4 us
    reduce_scatter x1, waiting for transfers between devices, body(): lax.psum_scatter(pre_part.astype(jnp.bfloat16), 'blk', scatter_dimension=...  15.8 us
  transfers between devices with their start and end apart: 14, of which 13 were waited for; matrix products, arithmetic and copies ran while one was open for 13% of the time, Pallas kernels for 0%

profile of v6, /device:TPU:32, one launch (start us, length us, event | category | flops | bytes accessed | tf_op | source)
XLA Modules:
  0.0 357.3 jit_solution(2359451482114171299)
XLA Ops:
  7.2 2.4 broadcast_in_dim.348
  9.6 7.5 %all-to-all-start = ((bf16[32,32,1024]{2,1,0:T(8,128)(2,1)}), bf16[32,32,1024]{2,1,0:T(8,128)(2,1)S(1)}, u32[]{:S(2)}, u32[]{:S(2)}) async-start(bf16[32,32,1024]{2,1,0:T(8,128)(2,1)} %broadcast_in_dim.348), calls=%async_computation | async-start | bytes 4194304 | tf_op jit(solution)/shard_map/all_to_all | solution.py:48
  20.2 3.4 collective-permute-done
  24.3 3.4 collective-permute-start.1
  29.3 5.9 %collective-permute-start.2 = (f32[1025]{0:T(1024)S(1)}, f32[1025]{0:T(1024)S(1)}, u32[]{:S(2)}, u32[]{:S(2)}) collective-permute-start(f32[1025]{0:T(1024)S(1)} %add.159), channel_id=1, source_target_pairs={{0,4},{1,5},{2,6},{3,7},{4,0},{5,1},{6,2},{7,3},{8,12},{9,13},{10,... | collective-permute-start | bytes 12308 | tf_op jit(solution)/shard_map/ppermute | solution.py:40
  36.9 9.1 %all-to-all-done = bf16[32,32,1024]{2,1,0:T(8,128)(2,1)S(1)} async-done(((bf16[32,32,1024]{2,1,0:T(8,128)(2,1)}), bf16[32,32,1024]{2,1,0:T(8,128)(2,1)S(1)}, u32[]{:S(2)}, u32[]{:S(2)}) %all-to-all-start) | async-done | bytes 2097184 | tf_op jit(solution)/shard_map/all_to_all | solution.py:48
  46.0 6.0 %fusion.8 = bf16[1024,1024]{1,0:T(8,128)(2,1)} fusion(bf16[1024,1024]{1,0:T(8,128)(2,1)S(1)} %bitcast.185, bf16[128,8,8,128]{3,2,1,0:T(8,128)(2,1)} %bitcast.192), kind=kOutput, calls=%fused_computation.15 | convolution fusion | flops 2148532224 | bytes 6291456 | tf_op jit(solution)/shard_map/dot_general | solution.py:109
  57.2 2.3 collective-permute-done.4
  60.1 2.3 collective-permute-start.5
  62.4 2.9 collective-permute-done.5
  67.3 2.3 collective-permute-done.6
  72.1 3.4 collective-permute-done.7
  76.7 15.8 %reduce-scatter.3.cloned.1.call-done = bf16[128,1024]{1,0:T(8,128)(2,1)} async-done(((bf16[1024,1024]{1,0:T(8,128)(2,1)}), bf16[128,1024]{1,0:T(8,128)(2,1)}) %reduce-scatter.3.cloned.1.call-update) | async-done | bytes 262160 | tf_op jit(solution)/shard_map/reduce_scatter | solution.py:110
  95.2 39.7 %all-gather.5.cloned.1.call-done = bf16[1024,1024]{1,0:T(8,128)(2,1)} async-done(((bf16[128,1024]{1,0:T(8,128)(2,1)}), bf16[1024,1024]{1,0:T(8,128)(2,1)}) %all-gather.5.cloned.1.call-update) | async-done | bytes 2097168 | tf_op jit(solution)/shard_map/all_gather | solution.py:116
  134.9 3.9 %fusion.14 = bf16[1024,1024]{1,0:T(8,128)(2,1)S(1)} fusion(bf16[1024,1024]{1,0:T(8,128)(2,1)} %all-gather.5.cloned.1.call-done, bf16[128,8,8,128]{3,2,1,0:T(8,128)(2,1)S(1)} %bitcast.195), kind=kOutput, calls=%fused_computation.17 | convolution fusion | flops 2148532224 | bytes 6291456 | tf_op jit(solution)/shard_map/dot_general | solution.py:118
  138.8 34.9 %all_to_all.20 = bf16[32,32,1024]{2,1,0:T(8,128)(2,1)S(1)} all-to-all(bf16[32,32,1024]{2,1,0:T(8,128)(2,1)S(1)} %bitcast.201), channel_id=1, replica_groups=mesh['wide'=32,'blk'=8] {'wide'}, dimensions={0} | all-to-all | bytes 4194304 | tf_op jit(solution)/shard_map/all_to_all | solution.py:55
  174.9 32.0 %all_to_all.21 = bf16[32,32,1024]{2,1,0:T(8,128)(2,1)S(1)} all-to-all(bf16[32,32,1024]{2,1,0:T(8,128)(2,1)S(1)} %broadcast_in_dim.372), channel_id=1, replica_groups=mesh['wide'=32,'blk'=8] {'wide'}, dimensions={0} | all-to-all | bytes 4194304 | tf_op jit(solution)/shard_map/all_to_all | solution.py:48
  206.9 3.7 %fusion.17 = bf16[1024,1024]{1,0:T(8,128)(2,1)} fusion(bf16[1024,1024]{1,0:T(8,128)(2,1)S(1)} %bitcast.187, bf16[128,8,8,128]{3,2,1,0:T(8,128)(2,1)S(1)} %bitcast.196), kind=kOutput, calls=%fused_computation.18 | convolution fusion | flops 2148532224 | bytes 6291456 | tf_op jit(solution)/shard_map/dot_general | solution.py:123
  212.2 4.0 %copy.158 = bf16[1024,1024]{1,0:T(8,128)(2,1)} copy(bf16[1024,1024]{0,1:T(8,128)(2,1)} %bitcast.194) | data formatting | bytes 4194304 | tf_op jit(solution)/shard_map/dot_general | solution.py:129
  216.1 2.6 copy.132
  218.7 4.6 %convolution_bitcast_fusion.1 = f32[8,8,128,128]{3,2,1,0:T(8,128)S(1)} fusion(bf16[8,128,1024,1]{2,1,3,0:T(8,128)(2,1)} %bitcast.199, bf16[8,128,1024,1]{2,1,0,3:T(8,128)(2,1)} %bitcast.198), kind=kOutput, calls=%fused_computation.4 | convolution fusion | flops 2147483648 | bytes 8388608 | tf_op jit(solution)/shard_map/dot_general | solution.py:129
  230.6 2.1 copy.138
  233.9 3.2 add_multiply_fusion
  237.1 11.3 %reduce-scatter.5.cloned.1.call-done = bf16[128,1024]{1,0:T(8,128)(2,1)} async-done(((bf16[1024,1024]{1,0:T(8,128)(2,1)}), bf16[128,1024]{1,0:T(8,128)(2,1)}) %reduce-scatter.5.cloned.1.call-update) | async-done | bytes 262160 | tf_op jit(solution)/shard_map/reduce_scatter | solution.py:126
  253.2 40.5 %all-gather.7.cloned.1.call-done = bf16[8,129,1024]{2,1,0:T(8,128)(2,1)} async-done(((bf16[1,129,1024]{2,1,0:T(8,128)(2,1)}), bf16[8,129,1024]{2,1,0:T(8,128)(2,1)}) %all-gather.7.cloned.1.call-update) | async-done | bytes 2113552 | tf_op jit(solution)/shard_map/all_gather | solution.py:137
  298.7 2.4 fusion.11
  303.1 7.3 %all-to-all-start.3 = ((bf16[32,33,1024]{2,1,0:T(8,128)(2,1)}), bf16[32,33,1024]{2,1,0:T(8,128)(2,1)S(1)}, u32[]{:S(2)}, u32[]{:S(2)}) async-start(bf16[32,33,1024]{2,1,0:T(8,128)(2,1)} %pad_maximum_fusion), calls=%async_computation.5 | async-start | bytes 5242880 | tf_op jit(solution)/shard_map/all_to_all | solution.py:151
  310.4 3.9 %copy.166 = bf16[1024,1024]{1,0:T(8,128)(2,1)} copy(bf16[1024,1024]{0,1:T(8,128)(2,1)} %bitcast.186) | data formatting | bytes 4194304 | tf_op jit(solution)/shard_map/dot_general | solution.py:159
  314.9 4.0 %copy.150 = bf16[1024,1024]{0,1:T(8,128)(2,1)} copy(bf16[1024,1024]{1,0:T(8,128)(2,1)} %bitcast.190) | data formatting | bytes 4194304 | tf_op jit(solution)/shard_map/reshape | solution.py:140
  318.9 4.6 %convolution_bitcast_fusion = f32[8,8,128,128]{3,2,1,0:T(8,128)S(1)} fusion(bf16[8,128,1024,1]{2,1,3,0:T(8,128)(2,1)} %bitcast.197, bf16[8,128,1024,1]{2,1,0,3:T(8,128)(2,1)} %bitcast.200), kind=kOutput, calls=%fused_computation.3 | convolution fusion | flops 2147483648 | bytes 8388608 | tf_op jit(solution)/shard_map/dot_general | solution.py:159
  325.3 19.5 %all-to-all-done.3 = bf16[32,33,1024]{2,1,0:T(8,128)(2,1)S(1)} async-done(((bf16[32,33,1024]{2,1,0:T(8,128)(2,1)}), bf16[32,33,1024]{2,1,0:T(8,128)(2,1)S(1)}, u32[]{:S(2)}, u32[]{:S(2)}) %all-to-all-start.3) | async-done | bytes 2162720 | tf_op jit(solution)/shard_map/all_to_all | solution.py:151
  347.2 3.5 subtract_bitcast_fusion
  (109 shorter events, 40.6 us)
Async XLA Ops:
  9.6 7.5 %copy-start.10 = (s32[8,1,2]{0,2,1:T(2,128)S(1)}, s32[8,1,2]{0,2,1:T(2,128)}, u32[]{:S(2)}) copy-start(s32[8,1,2]{0,2,1:T(2,128)} %param.16) | copy-start | bytes 196
  9.6 7.6 %copy-start.5 = (f32[1024]{0:T(1024)S(1)}, f32[1024]{0:T(1024)}, u32[]{:S(2)}) copy-start(f32[1024]{0:T(1024)} %param.13) | copy-start | bytes 12292
  9.6 9.1 %copy-start.11 = (s32[8,1]{0,1:T(1,128)S(1)}, s32[8,1]{0,1:T(1,128)}, u32[]{:S(2)}) copy-start(s32[8,1]{0,1:T(1,128)} %param.17) | copy-start | bytes 100
  9.6 9.2 %copy-start.6 = (bf16[8,1,2,128,128]{4,3,2,1,0:T(8,128)(2,1)S(1)}, bf16[8,1,2,128,128]{4,3,2,1,0:T(8,128)(2,1)}, u32[]{:S(2)}) copy-start(bf16[8,1,2,128,128]{4,3,2,1,0:T(8,128)(2,1)} %param.15) | copy-start | bytes 1572868
  9.6 9.2 %copy-start.7 = (bf16[8,1,2,128,128]{4,3,2,1,0:T(8,128)(2,1)S(1)}, bf16[8,1,2,128,128]{4,3,2,1,0:T(8,128)(2,1)}, u32[]{:S(2)}) copy-start(bf16[8,1,2,128,128]{4,3,2,1,0:T(8,128)(2,1)} %param.14) | copy-start | bytes 1572868
  9.6 36.4 %all-to-all-start = ((bf16[32,32,1024]{2,1,0:T(8,128)(2,1)}), bf16[32,32,1024]{2,1,0:T(8,128)(2,1)S(1)}, u32[]{:S(2)}, u32[]{:S(2)}) async-start(bf16[32,32,1024]{2,1,0:T(8,128)(2,1)} %broadcast_in_dim.348), calls=%async_computation | async-start | bytes 4194304 | tf_op jit(solution)/shard_map/all_to_all | solution.py:48
  17.1 75.4 %reduce-scatter.3.cloned.1.call-start = ((), (), s32[]{:S(2)}) async-start(), calls=%async_computation.6 | async-start | bytes 2359296 | tf_op jit(solution)/shard_map/reduce_scatter | solution.py:110
  19.9 3.7 %collective-permute-start = (f32[1025]{0:T(1024)S(1)}, f32[1025]{0:T(1024)S(1)}, u32[]{:S(2)}, u32[]{:S(2)}) collective-permute-start(f32[1025]{0:T(1024)S(1)} %pad_maximum_fusion.1), channel_id=1, source_target_pairs={{0,1},{1,0},{2,3},{3,2},{4,5},{5,4},{6,7},{7,6},{8,9},{9,8},{10,11... | collective-permute-start | bytes 12308 | tf_op jit(solution)/shard_map/ppermute | solution.py:40
  24.3 5.0 %collective-permute-start.1 = (f32[1025]{0:T(1024)S(1)}, f32[1025]{0:T(1024)S(1)}, u32[]{:S(2)}, u32[]{:S(2)}) collective-permute-start(f32[1025]{0:T(1024)S(1)} %fusion.47), channel_id=1, source_target_pairs={{0,2},{1,3},{2,0},{3,1},{4,6},{5,7},{6,4},{7,5},{8,10},{9,11},{10,... | collective-permute-start | bytes 12308 | tf_op jit(solution)/shard_map/ppermute | solution.py:40
  29.3 7.6 %collective-permute-start.2 = (f32[1025]{0:T(1024)S(1)}, f32[1025]{0:T(1024)S(1)}, u32[]{:S(2)}, u32[]{:S(2)}) collective-permute-start(f32[1025]{0:T(1024)S(1)} %add.159), channel_id=1, source_target_pairs={{0,4},{1,5},{2,6},{3,7},{4,0},{5,1},{6,2},{7,3},{8,12},{9,13},{10,... | collective-permute-start | bytes 12308 | tf_op jit(solution)/shard_map/ppermute | solution.py:40
  46.0 6.0 %copy-start = (bf16[32,32,1024]{2,1,0:T(8,128)(2,1)}, bf16[32,32,1024]{2,1,0:T(8,128)(2,1)S(1)}, u32[]{:S(2)}) copy-start(bf16[32,32,1024]{2,1,0:T(8,128)(2,1)S(1)} %all-to-all-done) | copy-start | bytes 6291460
  52.1 82.8 %all-gather.5.cloned.1.call-start = ((), (), s32[]{:S(2)}) async-start(), calls=%async_computation.7 | async-start | bytes 2359296 | tf_op jit(solution)/shard_map/all_gather | solution.py:116
  53.3 1.4 collective-permute-start.3
  55.8 3.7 %collective-permute-start.4 = (f32[1]{0:T(128)}, f32[1]{0:T(128)}, u32[]{:S(2)}, u32[]{:S(2)}) collective-permute-start(f32[1]{0:T(128)} %add.163), channel_id=1, source_target_pairs={{0,16},{8,24},{16,0},{24,8},{32,48},{40,56},{48,32},{56,40},{64,80... | collective-permute-start | bytes 20 | tf_op jit(solution)/shard_map/ppermute | solution.py:40
  60.1 5.2 %collective-permute-start.5 = (f32[1]{0:T(128)}, f32[1]{0:T(128)}, u32[]{:S(2)}, u32[]{:S(2)}) collective-permute-start(f32[1]{0:T(128)} %add.164), channel_id=1, source_target_pairs={{0,32},{8,40},{16,48},{24,56},{32,0},{40,8},{48,16},{56,24},{64,96... | collective-permute-start | bytes 20 | tf_op jit(solution)/shard_map/ppermute | solution.py:40
  65.9 3.7 %collective-permute-start.6 = (f32[1]{0:T(128)}, f32[1]{0:T(128)}, u32[]{:S(2)}, u32[]{:S(2)}) collective-permute-start(f32[1]{0:T(128)} %add.165), channel_id=1, source_target_pairs={{0,64},{8,72},{16,80},{24,88},{32,96},{40,104},{48,112},{56,120},{... | collective-permute-start | bytes 20 | tf_op jit(solution)/shard_map/ppermute | solution.py:40
  70.2 5.2 %collective-permute-start.7 = (f32[1]{0:T(128)}, f32[1]{0:T(128)}, u32[]{:S(2)}, u32[]{:S(2)}) collective-permute-start(f32[1]{0:T(128)} %add.166), channel_id=1, source_target_pairs={{0,128},{8,136},{16,144},{24,152},{32,160},{40,168},{48,176},{56,1... | collective-permute-start | bytes 20 | tf_op jit(solution)/shard_map/ppermute | solution.py:40
  94.4 154.1 %reduce-scatter.5.cloned.1.call-start = ((), (), s32[]{:S(2)}) async-start(), calls=%async_computation.8 | async-start | bytes 2359296 | tf_op jit(solution)/shard_map/reduce_scatter | solution.py:126
  95.2 43.6 %copy-start.3 = (bf16[8,128,8,128]{3,2,1,0:T(8,128)(2,1)}, bf16[8,128,8,128]{3,2,1,0:T(8,128)(2,1)S(1)}, u32[]{:S(2)}) copy-start(bf16[8,128,8,128]{3,2,1,0:T(8,128)(2,1)S(1)} %select_add_fusion) | copy-start | bytes 6291460
  173.8 0.8 copy-start.9
  174.6 32.3 %copy-start.8 = (bf16[32,1024]{1,0:T(8,128)(2,1)}, bf16[32,1024]{1,0:T(8,128)(2,1)S(1)}, u32[]{:S(2)}) copy-start(bf16[32,1024]{1,0:T(8,128)(2,1)S(1)} %reduce_sum.68) | copy-start | bytes 196612
  174.9 32.0 %copy-start.4 = (bf16[8,128,8,128]{3,2,1,0:T(8,128)(2,1)S(1)}, bf16[8,128,8,128]{3,2,1,0:T(8,128)(2,1)}, u32[]{:S(2)}) copy-start(bf16[8,128,8,128]{3,2,1,0:T(8,128)(2,1)} %copy-done.3) | copy-start | bytes 6291460
  210.7 83.0 %all-gather.7.cloned.1.call-start = ((), (), s32[]{:S(2)}) async-start(), calls=%async_computation.9 | async-start | bytes 2506752 | tf_op jit(solution)/shard_map/all_gather | solution.py:137
  296.5 2.2 copy-start.2
  298.4 2.7 copy-start.1
  303.1 41.7 %all-to-all-start.3 = ((bf16[32,33,1024]{2,1,0:T(8,128)(2,1)}), bf16[32,33,1024]{2,1,0:T(8,128)(2,1)S(1)}, u32[]{:S(2)}, u32[]{:S(2)}) async-start(bf16[32,33,1024]{2,1,0:T(8,128)(2,1)} %pad_maximum_fusion), calls=%async_computation.5 | async-start | bytes 5242880 | tf_op jit(solution)/shard_map/all_to_all | solution.py:151
Sparse Core Ops, SparseCore 0:
  52.2 40.2 reduce-scatter.2
  94.8 40.0 all-gather.4
  210.8 37.6 reduce-scatter.4
  253.4 40.3 all-gather.6

commit v7 on v6

--- a/solution.py
+++ b/solution.py
@@ -1,7 +1,9 @@
 import jax
 import jax.numpy as jnp
 from jax import lax
-from jax.sharding import PartitionSpec as P
+from jax.sharding import Mesh, PartitionSpec as P
+
+WIDE = ("chip", "core")
 
 
 def activate(value):
@@ -33,8 +35,17 @@
     return picked
 
 
+def group_size(axis):
+    if isinstance(axis, tuple):
+        size = 1
+        for name in axis:
+            size *= lax.axis_size(name)
+        return size
+    return lax.axis_size(axis)
+
+
 def butterfly_sum(value, axis):
-    size = lax.axis_size(axis)
+    size = group_size(axis)
     step = 1
     while step < size:
         value = value + lax.ppermute(value, axis, [(i, i ^ step) for i in range(size)])
@@ -42,17 +53,28 @@
     return value
 
 
-def gather_rows(value, axis):
-    size = lax.axis_size(axis)
-    spread = jnp.broadcast_to(value[None], (size,) + value.shape)
-    gathered = lax.all_to_all(spread, axis, 0, 0, tiled=False)
-    return gathered.reshape((size * value.shape[0],) + value.shape[1:])
-
-
-def sum_rows(value, axis):
-    size = lax.axis_size(axis)
-    parts = value.reshape((size, value.shape[0] // size) + value.shape[1:])
-    received = lax.all_to_all(parts, axis, 0, 0, tiled=False)
+def gather_rows(value):
+    chips = lax.axis_size("chip")
+    spread = jnp.broadcast_to(value[None], (chips,) + value.shape)
+    mine = lax.all_to_all(spread, "chip", 0, 0, tiled=False)
+    other = lax.ppermute(mine, "core", [(0, 1), (1, 0)])
+    first = lax.axis_index("core") == 0
+    pair = jnp.where(first, jnp.stack([mine, other], 1), jnp.stack([other, mine], 1))
+    return pair.reshape((-1,) + value.shape[1:])
+
+
+def pair_rows(value):
+    chips = lax.axis_size("chip")
+    parts = value.reshape((chips, 2, -1) + value.shape[1:])
+    first = lax.axis_index("core") == 0
+    keep = jnp.where(first, parts[:, 0], parts[:, 1])
+    give = jnp.where(first, parts[:, 1], parts[:, 0])
+    got = lax.ppermute(give, "core", [(0, 1), (1, 0)])
+    return (keep.astype(jnp.float32) + got.astype(jnp.float32)).astype(jnp.bfloat16)
+
+
+def sum_rows(value):
+    received = lax.all_to_all(pair_rows(value), "chip", 0, 0, tiled=False)
     return jnp.sum(received.astype(jnp.float32), axis=0)
 
 
@@ -91,14 +113,14 @@
     image_part = jnp.einsum(
         "jsk,jskn->jn", chosen, tiles_in.astype(jnp.float32), precision=lax.Precision.HIGHEST
     )
-    x_full = gather_rows(tokens, "wide")
+    x_full = gather_rows(tokens)
     image_and_norm = butterfly_sum(
         jnp.concatenate([image_part.reshape(-1), jnp.sum(probe_vector * probe_vector)[None]]), "blk"
     )
     x_full, image_and_norm = lax.optimization_barrier((x_full, image_and_norm))
     image = image_and_norm[:-1].reshape(image_part.shape)
     norm_probe = image_and_norm[-1]
-    norm_image = butterfly_sum(jnp.sum(image * image)[None], "wide")[0]
+    norm_image = butterfly_sum(jnp.sum(image * image)[None], WIDE)[0]
     spectral = jnp.sqrt(norm_image / norm_probe)
 
     w1 = spread_tiles(tiles_in, row_index, feature_blocks).reshape(features, hidden_width)
@@ -116,9 +138,9 @@
     active_full = lax.all_gather(active_own, "blk", axis=0, tiled=True)
 
     out_part = jnp.dot(active_full, w2, preferred_element_type=jnp.float32)
-    outputs = sum_rows(out_part.astype(jnp.bfloat16), "wide").astype(jnp.bfloat16)
+    outputs = sum_rows(out_part.astype(jnp.bfloat16)).astype(jnp.bfloat16)
     residual = (outputs.astype(jnp.float32) - target.astype(jnp.float32)).astype(jnp.bfloat16)
-    error_full = gather_rows(residual, "wide")
+    error_full = gather_rows(residual)
 
     back_part = lax.dot_general(
         error_full, w2, (((1,), (1,)), ((), ())), preferred_element_type=jnp.float32
@@ -143,13 +165,13 @@
     in_part = lax.dot_general(
         slope_full, w1, (((1,), (1,)), ((), ())), preferred_element_type=jnp.float32
     )
-    size = lax.axis_size("wide")
-    in_rows = in_part.astype(jnp.bfloat16).reshape(size, -1, features)
-    extra = jnp.zeros((size, 1, features), jnp.bfloat16).at[:, 0, :3].set(
-        split_three(curvature_blk)[None]
+    in_rows = pair_rows(in_part.astype(jnp.bfloat16))
+    curvature_chip = curvature_blk + lax.ppermute(curvature_blk, "core", [(0, 1), (1, 0)])
+    extra = jnp.zeros((in_rows.shape[0], 1, features), jnp.bfloat16).at[:, 0, :3].set(
+        split_three(curvature_chip)[None]
     )
     received = lax.all_to_all(
-        jnp.concatenate([in_rows, extra], axis=1), "wide", 0, 0, tiled=False
+        jnp.concatenate([in_rows, extra], axis=1), "chip", 0, 0, tiled=False
     )
     token_grad = (
         jnp.sum(received[:, :-1].astype(jnp.float32), axis=0) / spectral
@@ -167,19 +189,21 @@
 
 
 def solution(mesh):
+    wide, blk = mesh.shape["wide"], mesh.shape["blk"]
+    split = Mesh(mesh.devices.reshape(wide // 2, 2, blk), ("chip", "core", "blk"))
     in_specs = (
-        P("wide", "blk"),
-        P("wide", "blk"),
+        P(WIDE, "blk"),
+        P(WIDE, "blk"),
         P("blk"),
-        P("wide", "blk", None, None, None),
-        P("wide", "blk", None, None, None),
-        P("wide", "blk", None),
-        P("wide", "blk"),
+        P(WIDE, "blk", None, None, None),
+        P(WIDE, "blk", None, None, None),
+        P(WIDE, "blk", None),
+        P(WIDE, "blk"),
     )
     out_specs = (
-        P("wide", "blk"),
-        P("wide", "blk"),
-        P("wide", "blk", None, None, None),
-        P("wide", "blk", None, None, None),
-    )
-    return jax.shard_map(body, mesh=mesh, in_specs=in_specs, out_specs=out_specs, check_vma=False)
+        P(WIDE, "blk"),
+        P(WIDE, "blk"),
+        P(WIDE, "blk", None, None, None),
+        P(WIDE, "blk", None, None, None),
+    )
+    return jax.shard_map(body, mesh=split, in_specs=in_specs, out_specs=out_specs, check_vma=False)

time: 360 us -> 338 us (0.939)
  blocking collectives: 67 us -> 43.8 us
  waiting for transfers between devices: 153 us -> 138 us
  local copies, waits for them, and re-layouts: 36 us -> 47.8 us
  other arithmetic: 22.4 us -> 28.8 us
    all_to_all x2, blocking collectives: 67 us -> 43.8 us  [the longest x1 24.3 us: sum_rows(): received = lax.all_to_all(pair_rows(value), 'chip', 0, 0, tiled=False)]
    reduce_scatter x1, waiting for transfers between devices: 11.3 us -> 1.76 us  [body(): lax.psum_scatter(back_part.astype(jnp.bfloat16), 'blk', scatter_dimension...]
    broadcast_in_dim x18, local copies, waits for them, and re-layouts: 13.1 us -> 19.8 us  [pick_tiles(): jnp.where(hit[r][:, :, None, None], by_col[r][:, None], 0.0)]
    ppermute x0 -> x5, waiting for transfers between devices: none -> 6.26 us  [the longest x2 2.66 us: gather_rows(): other = lax.ppermute(mine, 'core', [(0, 1), (1, 0)])]
    all_to_all x2, waiting for transfers between devices: 28.6 us -> 23.3 us  [the longest x1 14.7 us: gather_rows(): mine = lax.all_to_all(spread, 'chip', 0, 0, tiled=False)]
    ppermute x8, waiting for transfers between devices: 17.1 us -> 12.3 us  [butterfly_sum(): lax.ppermute(value, axis, [(i, i ^ step) for i in range(size)])]
    unnamed x29 -> x35, local copies, waits for them, and re-layouts: 1.08 us -> 5.46 us
  transfers between devices with their start and end apart: 14 -> 19, of which waited for: 13 -> 15; matrix products, arithmetic and copies ran while one was open for 13% -> 17% of each run, Pallas kernels for 0% -> 0%
where the time goes in v7:
time: 338 us; the launch traced here: 337 us
  waiting for transfers between devices  138 us (41%)
  local copies, waits for them, and re-layouts  47.8 us (14%)
  blocking collectives  43.8 us (13%)
  starting transfers between devices  32 us (9%)
  other arithmetic  28.8 us (9%)
  matrix products  23.1 us (7%)
  between operations  22.9 us (7%)
    all_gather x1, waiting for transfers between devices, body(): lax.all_gather(with_row(slope_own, split_three(curvature_part)), 'blk', a...  40.6 us
    all_gather x1, waiting for transfers between devices, body(): active_full = lax.all_gather(active_own, 'blk', axis=0, tiled=True)  38.2 us
    all_to_all x1, blocking collectives, sum_rows(): received = lax.all_to_all(pair_rows(value), 'chip', 0, 0, tiled=False)  24.3 us
    broadcast_in_dim x18, local copies, waits for them, and re-layouts, pick_tiles(): jnp.where(hit[r][:, :, None, None], by_col[r][:, None], 0.0)  19.8 us
    all_to_all x1, blocking collectives, gather_rows(): mine = lax.all_to_all(spread, 'chip', 0, 0, tiled=False)  19.5 us
    ppermute x8, starting transfers between devices, butterfly_sum(): lax.ppermute(value, axis, [(i, i ^ step) for i in range(size)])  17 us
    reduce_scatter x1, waiting for transfers between devices, body(): lax.psum_scatter(pre_part.astype(jnp.bfloat16), 'blk', scatter_dimension=...  15.7 us
    all_to_all x1, waiting for transfers between devices, gather_rows(): mine = lax.all_to_all(spread, 'chip', 0, 0, tiled=False)  14.7 us
  transfers between devices with their start and end apart: 19, of which 15 were waited for; matrix products, arithmetic and copies ran while one was open for 17% of the time, Pallas kernels for 0%

profile of v7, /device:TPU:32, one launch (start us, length us, event | category | flops | bytes accessed | tf_op | source)
XLA Modules:
  0.0 336.6 jit_solution(11906209491435661695)
XLA Ops:
  9.2 7.0 %all-to-all-start = ((bf16[16,32,1024]{2,1,0:T(8,128)(2,1)}), bf16[16,32,1024]{2,1,0:T(8,128)(2,1)S(1)}, u32[]{:S(2)}, u32[]{:S(2)}) async-start(bf16[16,32,1024]{2,1,0:T(8,128)(2,1)} %broadcast_in_dim.348), calls=%async_computation | async-start | bytes 2097152 | tf_op jit(solution)/shard_map/all_to_all | solution.py:59
  19.3 14.7 %all-to-all-done = bf16[16,32,1024]{2,1,0:T(8,128)(2,1)S(1)} async-done(((bf16[16,32,1024]{2,1,0:T(8,128)(2,1)}), bf16[16,32,1024]{2,1,0:T(8,128)(2,1)S(1)}, u32[]{:S(2)}, u32[]{:S(2)}) %all-to-all-start) | async-done | bytes 1048608 | tf_op jit(solution)/shard_map/all_to_all | solution.py:59
  35.5 3.4 collective-permute-start.2
  40.5 5.9 %collective-permute-start.3 = (f32[1025]{0:T(1024)S(1)}, f32[1025]{0:T(1024)S(1)}, u32[]{:S(2)}, u32[]{:S(2)}) collective-permute-start(f32[1025]{0:T(1024)S(1)} %add.168), channel_id=1, source_target_pairs={{0,4},{1,5},{2,6},{3,7},{4,0},{5,1},{6,2},{7,3},{8,12},{9,13},{10,... | collective-permute-start | bytes 12308 | tf_op jit(solution)/shard_map/ppermute | solution.py:51
  50.1 3.6 %fusion.10 = bf16[1024,1024]{1,0:T(8,128)(2,1)} fusion(bf16[1024,1024]{1,0:T(8,128)(2,1)S(1)} %bitcast.223, bf16[128,8,8,128]{3,2,1,0:T(8,128)(2,1)S(1)} %bitcast.235), kind=kOutput, calls=%fused_computation.20 | convolution fusion | flops 2148532224 | bytes 6291456 | tf_op jit(solution)/shard_map/dot_general | solution.py:131
  61.8 2.1 collective-permute-start.6
  63.9 2.9 collective-permute-done.6
  69.0 2.2 collective-permute-done.7
  73.9 3.1 collective-permute-done.8
  78.3 15.7 %reduce-scatter.3.cloned.1.call-done = bf16[128,1024]{1,0:T(8,128)(2,1)} async-done(((bf16[1024,1024]{1,0:T(8,128)(2,1)}), bf16[128,1024]{1,0:T(8,128)(2,1)}) %reduce-scatter.3.cloned.1.call-update) | async-done | bytes 262160 | tf_op jit(solution)/shard_map/reduce_scatter | solution.py:132
  98.1 38.2 %all-gather.5.cloned.1.call-done = bf16[1024,1024]{1,0:T(8,128)(2,1)} async-done(((bf16[128,1024]{1,0:T(8,128)(2,1)}), bf16[1024,1024]{1,0:T(8,128)(2,1)}) %all-gather.5.cloned.1.call-update) | async-done | bytes 2097168 | tf_op jit(solution)/shard_map/all_gather | solution.py:138
  136.3 4.5 %fusion.16 = bf16[1024,1024]{1,0:T(8,128)(2,1)S(1)} fusion(bf16[1024,1024]{1,0:T(8,128)(2,1)} %all-gather.5.cloned.1.call-done, bf16[128,8,8,128]{3,2,1,0:T(8,128)(2,1)} %bitcast.238), kind=kOutput, calls=%fused_computation.22 | convolution fusion | flops 2148532224 | bytes 6291456 | tf_op jit(solution)/shard_map/dot_general | solution.py:140
  141.3 2.6 collective-permute-done.9
  144.6 24.3 %all_to_all.20 = bf16[16,32,1024]{2,1,0:T(8,128)(2,1)} all-to-all(bf16[16,32,1024]{2,1,0:T(8,128)(2,1)S(1)} %fusion.9), channel_id=1, replica_groups=mesh['chip'=16,'core'=2,'blk'=8] {'chip'}, dimensions={0} | all-to-all | bytes 2097152 | tf_op jit(solution)/shard_map/all_to_all | solution.py:77
  170.4 19.5 %all_to_all.21 = bf16[16,32,1024]{2,1,0:T(8,128)(2,1)S(1)} all-to-all(bf16[16,32,1024]{2,1,0:T(8,128)(2,1)S(1)} %broadcast_in_dim.372), channel_id=1, replica_groups=mesh['chip'=16,'core'=2,'blk'=8] {'chip'}, dimensions={0} | all-to-all | bytes 2097152 | tf_op jit(solution)/shard_map/all_to_all | solution.py:59
  190.0 2.7 collective-permute-done.10
  195.3 3.7 %fusion.19 = bf16[1024,1024]{1,0:T(8,128)(2,1)} fusion(bf16[1024,1024]{1,0:T(8,128)(2,1)S(1)} %bitcast.227, bf16[128,8,8,128]{3,2,1,0:T(8,128)(2,1)S(1)} %bitcast.239), kind=kOutput, calls=%fused_computation.23 | convolution fusion | flops 2148532224 | bytes 6291456 | tf_op jit(solution)/shard_map/dot_general | solution.py:145
  200.7 4.0 %copy.185 = bf16[1024,1024]{1,0:T(8,128)(2,1)} copy(bf16[1024,1024]{0,1:T(8,128)(2,1)} %bitcast.237) | data formatting | bytes 4194304 | tf_op jit(solution)/shard_map/dot_general | solution.py:151
  204.7 4.0 %copy.184 = bf16[1024,1024]{1,0:T(8,128)(2,1)} copy(bf16[1024,1024]{0,1:T(8,128)(2,1)} %bitcast.228) | data formatting | bytes 4194304 | tf_op jit(solution)/shard_map/dot_general | solution.py:151
  208.6 4.6 %convolution_bitcast_fusion.1 = f32[8,8,128,128]{3,2,1,0:T(8,128)S(1)} fusion(bf16[8,128,1024,1]{2,1,3,0:T(8,128)(2,1)} %bitcast.242, bf16[8,128,1024,1]{2,1,0,3:T(8,128)(2,1)} %bitcast.241), kind=kOutput, calls=%fused_computation.2 | convolution fusion | flops 2147483648 | bytes 8388608 | tf_op jit(solution)/shard_map/dot_general | solution.py:151
  218.6 2.1 copy.168
  220.7 2.1 copy.166
  230.9 3.7 %add_multiply_fusion = f32[8,2,128,128]{3,2,1,0:T(8,128)} fusion(f32[8,2]{1,0:T(8,128)S(1)} %get-tuple-element.78, f32[8,128,128]{2,1,0:T(8,128)S(1)} %copy.172, f32[8,128,128]{2,1,0:T(8,128)} %copy.170, f32[8,128,128]{2,1,0:T(8,128)} %copy.168, f32[8,128,128]{2,1,0:T(8,128)} %copy.166, f32[8,128,128]{2,1,0:T(8,128)} %copy.164, f32[8,128,128]{2,1,0:T(8,128)} %copy.162, ...), kind=kLoop, calls=%fused_computation.35 | loop fusion | flops 4194304 | bytes 5243072 | tf_op jit(solution)/shard_map/mul | solution.py:154
  241.1 40.6 %all-gather.7.cloned.1.call-done = bf16[8,129,1024]{2,1,0:T(8,128)(2,1)} async-done(((bf16[1,129,1024]{2,1,0:T(8,128)(2,1)}), bf16[8,129,1024]{2,1,0:T(8,128)(2,1)}) %all-gather.7.cloned.1.call-update) | async-done | bytes 2113552 | tf_op jit(solution)/shard_map/all_gather | solution.py:159
  283.9 2.4 fusion.13
  293.0 2.2 fusion.8
  296.5 6.8 %all-to-all-start.3 = ((bf16[16,33,1024]{2,1,0:T(8,128)(2,1)}), bf16[16,33,1024]{2,1,0:T(8,128)(2,1)S(1)}, u32[]{:S(2)}, u32[]{:S(2)}) async-start(bf16[16,33,1024]{2,1,0:T(8,128)(2,1)} %pad_maximum_fusion), calls=%async_computation.5 | async-start | bytes 2621440 | tf_op jit(solution)/shard_map/all_to_all | solution.py:173
  303.3 2.6 copy.193
  306.5 4.1 %copy.176 = bf16[1024,1024]{0,1:T(8,128)(2,1)} copy(bf16[1024,1024]{1,0:T(8,128)(2,1)} %bitcast.226) | data formatting | bytes 4194304 | tf_op jit(solution)/shard_map/reshape | solution.py:162
  310.7 4.0 %convolution_bitcast_fusion = f32[8,8,128,128]{3,2,1,0:T(8,128)S(1)} fusion(bf16[8,128,1024,1]{2,1,3,0:T(8,128)(2,1)S(1)} %bitcast.240, bf16[8,128,1024,1]{2,1,0,3:T(8,128)(2,1)} %bitcast.243), kind=kOutput, calls=%fused_computation.1 | convolution fusion | flops 2147483648 | bytes 8388608 | tf_op jit(solution)/shard_map/dot_general | solution.py:181
  316.0 8.6 %all-to-all-done.3 = bf16[16,33,1024]{2,1,0:T(8,128)(2,1)S(1)} async-done(((bf16[16,33,1024]{2,1,0:T(8,128)(2,1)}), bf16[16,33,1024]{2,1,0:T(8,128)(2,1)S(1)}, u32[]{:S(2)}, u32[]{:S(2)}) %all-to-all-start.3) | async-done | bytes 1081376 | tf_op jit(solution)/shard_map/all_to_all | solution.py:173
  326.8 3.3 subtract_bitcast_fusion
  (133 shorter events, 62.7 us)
Async XLA Ops:
  7.2 9.2 %copy-start.13 = (s32[8,1,2]{0,2,1:T(2,128)S(1)}, s32[8,1,2]{0,2,1:T(2,128)}, u32[]{:S(2)}) copy-start(s32[8,1,2]{0,2,1:T(2,128)} %param.16) | copy-start | bytes 196
  7.2 9.3 %copy-start.14 = (s32[8,1]{0,1:T(1,128)S(1)}, s32[8,1]{0,1:T(1,128)}, u32[]{:S(2)}) copy-start(s32[8,1]{0,1:T(1,128)} %param.17) | copy-start | bytes 100
  7.2 9.5 %copy-start.7 = (f32[1024]{0:T(1024)S(1)}, f32[1024]{0:T(1024)}, u32[]{:S(2)}) copy-start(f32[1024]{0:T(1024)} %param.13) | copy-start | bytes 12292
  7.2 10.7 %copy-start.9 = (bf16[8,1,2,128,128]{4,3,2,1,0:T(8,128)(2,1)S(1)}, bf16[8,1,2,128,128]{4,3,2,1,0:T(8,128)(2,1)}, u32[]{:S(2)}) copy-start(bf16[8,1,2,128,128]{4,3,2,1,0:T(8,128)(2,1)} %param.15) | copy-start | bytes 1572868
  7.2 10.7 %copy-start.10 = (bf16[8,1,2,128,128]{4,3,2,1,0:T(8,128)(2,1)S(1)}, bf16[8,1,2,128,128]{4,3,2,1,0:T(8,128)(2,1)}, u32[]{:S(2)}) copy-start(bf16[8,1,2,128,128]{4,3,2,1,0:T(8,128)(2,1)} %param.14) | copy-start | bytes 1572868
  9.2 24.7 %all-to-all-start = ((bf16[16,32,1024]{2,1,0:T(8,128)(2,1)}), bf16[16,32,1024]{2,1,0:T(8,128)(2,1)S(1)}, u32[]{:S(2)}, u32[]{:S(2)}) async-start(bf16[16,32,1024]{2,1,0:T(8,128)(2,1)} %broadcast_in_dim.348), calls=%async_computation | async-start | bytes 2097152 | tf_op jit(solution)/shard_map/all_to_all | solution.py:59
  16.3 77.7 %reduce-scatter.3.cloned.1.call-start = ((), (), s32[]{:S(2)}) async-start(), calls=%async_computation.6 | async-start | bytes 2359296 | tf_op jit(solution)/shard_map/reduce_scatter | solution.py:132
  19.1 15.7 %collective-permute-start.1 = (f32[1025]{0:T(1024)S(1)}, f32[1025]{0:T(1024)S(1)}, u32[]{:S(2)}, u32[]{:S(2)}) collective-permute-start(f32[1025]{0:T(1024)S(1)} %pad_maximum_fusion.1), channel_id=1, source_target_pairs={{0,1},{1,0},{2,3},{3,2},{4,5},{5,4},{6,7},{7,6},{8,9},{9,8},{10,11... | collective-permute-start | bytes 12308 | tf_op jit(solution)/shard_map/ppermute | solution.py:51
  34.0 14.1 %collective-permute-start = (bf16[16,32,1024]{2,1,0:T(8,128)(2,1)S(1)}, bf16[16,32,1024]{2,1,0:T(8,128)(2,1)S(1)}, u32[]{:S(2)}, u32[]{:S(2)}) collective-permute-start(bf16[16,32,1024]{2,1,0:T(8,128)(2,1)S(1)} %all-to-all-done), channel_id=1, source_target_pairs={{0,8},{8,0},{1,9},{9,1},{2,10},{10,2},{3,11},{11,3},{4,12},{12,4},... | collective-permute-start | bytes 3145736 | tf_op jit(solution)/shard_map/ppermute | solution.py:60
  35.5 5.0 %collective-permute-start.2 = (f32[1025]{0:T(1024)S(1)}, f32[1025]{0:T(1024)S(1)}, u32[]{:S(2)}, u32[]{:S(2)}) collective-permute-start(f32[1025]{0:T(1024)S(1)} %fusion.49), channel_id=1, source_target_pairs={{0,2},{1,3},{2,0},{3,1},{4,6},{5,7},{6,4},{7,5},{8,10},{9,11},{10,... | collective-permute-start | bytes 12308 | tf_op jit(solution)/shard_map/ppermute | solution.py:51
  40.5 7.7 %collective-permute-start.3 = (f32[1025]{0:T(1024)S(1)}, f32[1025]{0:T(1024)S(1)}, u32[]{:S(2)}, u32[]{:S(2)}) collective-permute-start(f32[1025]{0:T(1024)S(1)} %add.168), channel_id=1, source_target_pairs={{0,4},{1,5},{2,6},{3,7},{4,0},{5,1},{6,2},{7,3},{8,12},{9,13},{10,... | collective-permute-start | bytes 12308 | tf_op jit(solution)/shard_map/ppermute | solution.py:51
  48.5 1.6 copy-start.3
  53.7 42.5 %copy-start.8 = (bf16[8,128,128]{2,1,0:T(8,128)(2,1)S(1)}, bf16[8,128,128]{2,1,0:T(8,128)(2,1)}, u32[]{:S(2)}) copy-start(bf16[8,128,128]{2,1,0:T(8,128)(2,1)} %get-tuple-element.59) | copy-start | bytes 786436
  53.7 82.6 %all-gather.5.cloned.1.call-start = ((), (), s32[]{:S(2)}) async-start(), calls=%async_computation.7 | async-start | bytes 2359296 | tf_op jit(solution)/shard_map/all_gather | solution.py:138
  55.0 1.2 collective-permute-start.4
  57.5 3.6 %collective-permute-start.5 = (f32[1]{0:T(128)}, f32[1]{0:T(128)}, u32[]{:S(2)}, u32[]{:S(2)}) collective-permute-start(f32[1]{0:T(128)} %add.172), channel_id=1, source_target_pairs={{0,16},{8,24},{16,0},{24,8},{32,48},{40,56},{48,32},{56,40},{64,80... | collective-permute-start | bytes 20 | tf_op jit(solution)/shard_map/ppermute | solution.py:51
  61.8 5.1 %collective-permute-start.6 = (f32[1]{0:T(128)}, f32[1]{0:T(128)}, u32[]{:S(2)}, u32[]{:S(2)}) collective-permute-start(f32[1]{0:T(128)} %add.173), channel_id=1, source_target_pairs={{0,32},{8,40},{16,48},{24,56},{32,0},{40,8},{48,16},{56,24},{64,96... | collective-permute-start | bytes 20 | tf_op jit(solution)/shard_map/ppermute | solution.py:51
  67.6 3.6 %collective-permute-start.7 = (f32[1]{0:T(128)}, f32[1]{0:T(128)}, u32[]{:S(2)}, u32[]{:S(2)}) collective-permute-start(f32[1]{0:T(128)} %add.174), channel_id=1, source_target_pairs={{0,64},{8,72},{16,80},{24,88},{32,96},{40,104},{48,112},{56,120},{... | collective-permute-start | bytes 20 | tf_op jit(solution)/shard_map/ppermute | solution.py:51
  71.9 5.1 %collective-permute-start.8 = (f32[1]{0:T(128)}, f32[1]{0:T(128)}, u32[]{:S(2)}, u32[]{:S(2)}) collective-permute-start(f32[1]{0:T(128)} %add.175), channel_id=1, source_target_pairs={{0,128},{8,136},{16,144},{24,152},{32,160},{40,168},{48,176},{56,1... | collective-permute-start | bytes 20 | tf_op jit(solution)/shard_map/ppermute | solution.py:51
  95.9 140.4 %reduce-scatter.5.cloned.1.call-start = ((), (), s32[]{:S(2)}) async-start(), calls=%async_computation.8 | async-start | bytes 2359296 | tf_op jit(solution)/shard_map/reduce_scatter | solution.py:148
  141.0 2.9 collective-permute-start.9
  144.6 25.7 %copy-start.12 = (bf16[32,1024]{1,0:T(8,128)(2,1)S(1)}, bf16[32,1024]{1,0:T(8,128)(2,1)}, u32[]{:S(2)}) copy-start(bf16[32,1024]{1,0:T(8,128)(2,1)} %param.12) | copy-start | bytes 196612
  170.3 22.7 %copy-start.11 = (bf16[32,1024]{1,0:T(8,128)(2,1)}, bf16[32,1024]{1,0:T(8,128)(2,1)S(1)}, u32[]{:S(2)}) copy-start(bf16[32,1024]{1,0:T(8,128)(2,1)S(1)} %reduce_sum.68) | copy-start | bytes 196612
  190.0 2.7 collective-permute-start.10
  193.0 2.3 copy-start.5
  199.0 82.7 %all-gather.7.cloned.1.call-start = ((), (), s32[]{:S(2)}) async-start(), calls=%async_computation.9 | async-start | bytes 2506752 | tf_op jit(solution)/shard_map/all_gather | solution.py:159
  281.7 2.2 copy-start.4
  283.6 2.7 copy-start
  288.7 4.3 %collective-permute-start.11 = (bf16[16,32,1024]{2,1,0:T(8,128)(2,1)}, bf16[16,32,1024]{2,1,0:T(8,128)(2,1)S(1)}, u32[]{:S(2)}, u32[]{:S(2)}) collective-permute-start(bf16[16,32,1024]{2,1,0:T(8,128)(2,1)} %select_bitcast_fusion), channel_id=1, source_target_pairs={{0,8},{8,0},{1,9},{9,1},{2,10},{10,2},{3,11},{11,3},{4,12},{12,4},... | collective-permute-start | bytes 3145736 | tf_op jit(solution)/shard_map/ppermute | solution.py:72
  290.2 1.5 collective-permute-start.12
  296.5 28.1 %all-to-all-start.3 = ((bf16[16,33,1024]{2,1,0:T(8,128)(2,1)}), bf16[16,33,1024]{2,1,0:T(8,128)(2,1)S(1)}, u32[]{:S(2)}, u32[]{:S(2)}) async-start(bf16[16,33,1024]{2,1,0:T(8,128)(2,1)} %pad_maximum_fusion), calls=%async_computation.5 | async-start | bytes 2621440 | tf_op jit(solution)/shard_map/all_to_all | solution.py:173
  306.5 4.1 %copy-start.6 = (bf16[1024,1024]{1,0:T(8,128)(2,1)S(1)}, bf16[1024,1024]{1,0:T(8,128)(2,1)}, u32[]{:S(2)}) copy-start(bf16[1024,1024]{1,0:T(8,128)(2,1)} %copy.193) | copy-start | bytes 6291460
  (2 other events, 2.7 us)
Sparse Core Ops, SparseCore 0:
  53.8 40.1 reduce-scatter.2
  96.4 39.9 all-gather.4
  199.1 37.1 reduce-scatter.4
  241.2 40.4 all-gather.6

commit v8 on v7

--- a/solution.py
+++ b/solution.py
@@ -117,7 +117,6 @@
     image_and_norm = butterfly_sum(
         jnp.concatenate([image_part.reshape(-1), jnp.sum(probe_vector * probe_vector)[None]]), "blk"
     )
-    x_full, image_and_norm = lax.optimization_barrier((x_full, image_and_norm))
     image = image_and_norm[:-1].reshape(image_part.shape)
     norm_probe = image_and_norm[-1]
     norm_image = butterfly_sum(jnp.sum(image * image)[None], WIDE)[0]

time: 338 us -> 330 us (0.976)
  waiting for transfers between devices: 138 us -> 132 us
    reduce_scatter x1, waiting for transfers between devices: 15.7 us -> 0.02 us  [body(): lax.psum_scatter(pre_part.astype(jnp.bfloat16), 'blk', scatter_dimension=...]
    ppermute x8, waiting for transfers between devices: 12.3 us -> 18.3 us  [butterfly_sum(): lax.ppermute(value, axis, [(i, i ^ step) for i in range(size)])]
  transfers between devices with their start and end apart: 19 -> 19, of which waited for: 15 -> 17; matrix products, arithmetic and copies ran while one was open for 17% -> 17% of each run, Pallas kernels for 0% -> 0%
where the time goes in v8:
time: 330 us; the launch traced here: 329 us
  waiting for transfers between devices  132 us (40%)
  local copies, waits for them, and re-layouts  46.2 us (14%)
  blocking collectives  43.8 us (13%)
  starting transfers between devices  31.8 us (10%)
  other arithmetic  29 us (9%)
  matrix products  23.1 us (7%)
  between operations  22.8 us (7%)
    all_gather x1, waiting for transfers between devices, body(): lax.all_gather(with_row(slope_own, split_three(curvature_part)), 'blk', a...  40.5 us
    all_gather x1, waiting for transfers between devices, body(): active_full = lax.all_gather(active_own, 'blk', axis=0, tiled=True)  37.2 us
    all_to_all x1, blocking collectives, sum_rows(): received = lax.all_to_all(pair_rows(value), 'chip', 0, 0, tiled=False)  24.3 us
    broadcast_in_dim x18, local copies, waits for them, and re-layouts, pick_tiles(): jnp.where(hit[r][:, :, None, None], by_col[r][:, None], 0.0)  19.8 us
    all_to_all x1, blocking collectives, gather_rows(): mine = lax.all_to_all(spread, 'chip', 0, 0, tiled=False)  19.5 us
    ppermute x8, waiting for transfers between devices, butterfly_sum(): lax.ppermute(value, axis, [(i, i ^ step) for i in range(size)])  18.3 us
    all_to_all x1, waiting for transfers between devices, gather_rows(): mine = lax.all_to_all(spread, 'chip', 0, 0, tiled=False)  17.6 us
    ppermute x8, starting transfers between devices, butterfly_sum(): lax.ppermute(value, axis, [(i, i ^ step) for i in range(size)])  16.8 us
  transfers between devices with their start and end apart: 19, of which 17 were waited for; matrix products, arithmetic and copies ran while one was open for 17% of the time, Pallas kernels for 0%

profile of v8, /device:TPU:32, one launch (start us, length us, event | category | flops | bytes accessed | tf_op | source)
XLA Modules:
  0.0 328.5 jit_solution(1199556183973200832)
XLA Ops:
  9.2 7.0 %all-to-all-start = ((bf16[16,32,1024]{2,1,0:T(8,128)(2,1)}), bf16[16,32,1024]{2,1,0:T(8,128)(2,1)S(1)}, u32[]{:S(2)}, u32[]{:S(2)}) async-start(bf16[16,32,1024]{2,1,0:T(8,128)(2,1)} %broadcast_in_dim.348), calls=%async_computation | async-start | bytes 2097152 | tf_op jit(solution)/shard_map/all_to_all | solution.py:59
  16.4 17.6 %all-to-all-done = bf16[16,32,1024]{2,1,0:T(8,128)(2,1)S(1)} async-done(((bf16[16,32,1024]{2,1,0:T(8,128)(2,1)}), bf16[16,32,1024]{2,1,0:T(8,128)(2,1)S(1)}, u32[]{:S(2)}, u32[]{:S(2)}) %all-to-all-start) | async-done | bytes 1048608 | tf_op jit(solution)/shard_map/all_to_all | solution.py:59
  38.8 3.6 %fusion.10 = bf16[1024,1024]{1,0:T(8,128)(2,1)} fusion(bf16[1024,1024]{1,0:T(8,128)(2,1)S(1)} %bitcast.224, bf16[128,8,8,128]{3,2,1,0:T(8,128)(2,1)S(1)} %bitcast.236), kind=kOutput, calls=%fused_computation.20 | convolution fusion | flops 2148532224 | bytes 6291456 | tf_op jit(solution)/shard_map/dot_general | solution.py:130
  45.6 3.5 %collective-permute-done.1 = f32[1025]{0:T(1024)S(1)} collective-permute-done((f32[1025]{0:T(1024)S(1)}, f32[1025]{0:T(1024)S(1)}, u32[]{:S(2)}, u32[]{:S(2)}) %collective-permute-start.1) | collective-permute-done | bytes 4132 | tf_op jit(solution)/shard_map/ppermute | solution.py:51
  49.8 3.4 %collective-permute-start.2 = (f32[1025]{0:T(1024)S(1)}, f32[1025]{0:T(1024)S(1)}, u32[]{:S(2)}, u32[]{:S(2)}) collective-permute-start(f32[1025]{0:T(1024)S(1)} %fusion.49), channel_id=1, source_target_pairs={{0,2},{1,3},{2,0},{3,1},{4,6},{5,7},{6,4},{7,5},{8,10},{9,11},{10,... | collective-permute-start | bytes 12308 | tf_op jit(solution)/shard_map/ppermute | solution.py:51
  54.9 6.0 %collective-permute-start.3 = (f32[1025]{0:T(1024)S(1)}, f32[1025]{0:T(1024)S(1)}, u32[]{:S(2)}, u32[]{:S(2)}) collective-permute-start(f32[1025]{0:T(1024)S(1)} %add.173), channel_id=1, source_target_pairs={{0,4},{1,5},{2,6},{3,7},{4,0},{5,1},{6,2},{7,3},{8,12},{9,13},{10,... | collective-permute-start | bytes 12308 | tf_op jit(solution)/shard_map/ppermute | solution.py:51
  70.6 2.1 collective-permute-start.6
  72.6 3.0 collective-permute-done.6
  77.7 2.2 collective-permute-done.7
  82.5 3.2 collective-permute-done.8
  91.2 37.2 %all-gather.5.cloned.1.call-done = bf16[1024,1024]{1,0:T(8,128)(2,1)} async-done(((bf16[128,1024]{1,0:T(8,128)(2,1)}), bf16[1024,1024]{1,0:T(8,128)(2,1)}) %all-gather.5.cloned.1.call-update) | async-done | bytes 2097168 | tf_op jit(solution)/shard_map/all_gather | solution.py:137
  128.3 4.5 %fusion.16 = bf16[1024,1024]{1,0:T(8,128)(2,1)S(1)} fusion(bf16[1024,1024]{1,0:T(8,128)(2,1)} %all-gather.5.cloned.1.call-done, bf16[128,8,8,128]{3,2,1,0:T(8,128)(2,1)} %bitcast.239), kind=kOutput, calls=%fused_computation.22 | convolution fusion | flops 2148532224 | bytes 6291456 | tf_op jit(solution)/shard_map/dot_general | solution.py:139
  133.3 2.6 collective-permute-done.9
  136.6 24.3 %all_to_all.20 = bf16[16,32,1024]{2,1,0:T(8,128)(2,1)} all-to-all(bf16[16,32,1024]{2,1,0:T(8,128)(2,1)S(1)} %fusion.9), channel_id=1, replica_groups=mesh['chip'=16,'core'=2,'blk'=8] {'chip'}, dimensions={0} | all-to-all | bytes 2097152 | tf_op jit(solution)/shard_map/all_to_all | solution.py:77
  162.4 19.5 %all_to_all.21 = bf16[16,32,1024]{2,1,0:T(8,128)(2,1)S(1)} all-to-all(bf16[16,32,1024]{2,1,0:T(8,128)(2,1)S(1)} %broadcast_in_dim.372), channel_id=1, replica_groups=mesh['chip'=16,'core'=2,'blk'=8] {'chip'}, dimensions={0} | all-to-all | bytes 2097152 | tf_op jit(solution)/shard_map/all_to_all | solution.py:59
  181.9 2.7 collective-permute-done.10
  187.3 3.7 %fusion.19 = bf16[1024,1024]{1,0:T(8,128)(2,1)} fusion(bf16[1024,1024]{1,0:T(8,128)(2,1)S(1)} %bitcast.228, bf16[128,8,8,128]{3,2,1,0:T(8,128)(2,1)S(1)} %bitcast.240), kind=kOutput, calls=%fused_computation.23 | convolution fusion | flops 2148532224 | bytes 6291456 | tf_op jit(solution)/shard_map/dot_general | solution.py:144
  192.7 4.0 %copy.185 = bf16[1024,1024]{1,0:T(8,128)(2,1)} copy(bf16[1024,1024]{0,1:T(8,128)(2,1)} %bitcast.238) | data formatting | bytes 4194304 | tf_op jit(solution)/shard_map/dot_general | solution.py:150
  196.7 4.0 %copy.184 = bf16[1024,1024]{1,0:T(8,128)(2,1)} copy(bf16[1024,1024]{0,1:T(8,128)(2,1)} %bitcast.229) | data formatting | bytes 4194304 | tf_op jit(solution)/shard_map/dot_general | solution.py:150
  200.6 4.6 %convolution_bitcast_fusion.1 = f32[8,8,128,128]{3,2,1,0:T(8,128)S(1)} fusion(bf16[8,128,1024,1]{2,1,3,0:T(8,128)(2,1)} %bitcast.243, bf16[8,128,1024,1]{2,1,0,3:T(8,128)(2,1)} %bitcast.242), kind=kOutput, calls=%fused_computation.2 | convolution fusion | flops 2147483648 | bytes 8388608 | tf_op jit(solution)/shard_map/dot_general | solution.py:150
  210.6 2.1 copy.168
  212.6 2.1 copy.166
  222.9 3.7 %add_multiply_fusion = f32[8,2,128,128]{3,2,1,0:T(8,128)} fusion(f32[8,2]{1,0:T(8,128)S(1)} %get-tuple-element.74, f32[8,128,128]{2,1,0:T(8,128)S(1)} %copy.172, f32[8,128,128]{2,1,0:T(8,128)} %copy.170, f32[8,128,128]{2,1,0:T(8,128)} %copy.168, f32[8,128,128]{2,1,0:T(8,128)} %copy.166, f32[8,128,128]{2,1,0:T(8,128)} %copy.164, f32[8,128,128]{2,1,0:T(8,128)} %copy.162, ...), kind=kLoop, calls=%fused_computation.35 | loop fusion | flops 4194304 | bytes 5243072 | tf_op jit(solution)/shard_map/mul | solution.py:153
  233.0 40.5 %all-gather.7.cloned.1.call-done = bf16[8,129,1024]{2,1,0:T(8,128)(2,1)} async-done(((bf16[1,129,1024]{2,1,0:T(8,128)(2,1)}), bf16[8,129,1024]{2,1,0:T(8,128)(2,1)}) %all-gather.7.cloned.1.call-update) | async-done | bytes 2113552 | tf_op jit(solution)/shard_map/all_gather | solution.py:158
  275.8 2.4 fusion.13
  284.9 2.2 fusion.8
  288.4 6.8 %all-to-all-start.3 = ((bf16[16,33,1024]{2,1,0:T(8,128)(2,1)}), bf16[16,33,1024]{2,1,0:T(8,128)(2,1)S(1)}, u32[]{:S(2)}, u32[]{:S(2)}) async-start(bf16[16,33,1024]{2,1,0:T(8,128)(2,1)} %pad_maximum_fusion), calls=%async_computation.5 | async-start | bytes 2621440 | tf_op jit(solution)/shard_map/all_to_all | solution.py:172
  295.2 2.6 copy.193
  298.4 4.1 %copy.176 = bf16[1024,1024]{0,1:T(8,128)(2,1)} copy(bf16[1024,1024]{1,0:T(8,128)(2,1)} %bitcast.227) | data formatting | bytes 4194304 | tf_op jit(solution)/shard_map/reshape | solution.py:161
  302.6 4.0 %convolution_bitcast_fusion = f32[8,8,128,128]{3,2,1,0:T(8,128)S(1)} fusion(bf16[8,128,1024,1]{2,1,3,0:T(8,128)(2,1)S(1)} %bitcast.241, bf16[8,128,1024,1]{2,1,0,3:T(8,128)(2,1)} %bitcast.244), kind=kOutput, calls=%fused_computation.1 | convolution fusion | flops 2147483648 | bytes 8388608 | tf_op jit(solution)/shard_map/dot_general | solution.py:180
  307.9 8.6 %all-to-all-done.3 = bf16[16,33,1024]{2,1,0:T(8,128)(2,1)S(1)} async-done(((bf16[16,33,1024]{2,1,0:T(8,128)(2,1)}), bf16[16,33,1024]{2,1,0:T(8,128)(2,1)S(1)}, u32[]{:S(2)}, u32[]{:S(2)}) %all-to-all-start.3) | async-done | bytes 1081376 | tf_op jit(solution)/shard_map/all_to_all | solution.py:172
  318.8 3.3 subtract_bitcast_fusion
  (131 shorter events, 65.0 us)
Async XLA Ops:
  7.2 9.1 %copy-start.13 = (s32[8,1]{0,1:T(1,128)S(1)}, s32[8,1]{0,1:T(1,128)}, u32[]{:S(2)}) copy-start(s32[8,1]{0,1:T(1,128)} %param.17) | copy-start | bytes 100
  7.2 26.8 %copy-start.8 = (bf16[8,1,2,128,128]{4,3,2,1,0:T(8,128)(2,1)S(1)}, bf16[8,1,2,128,128]{4,3,2,1,0:T(8,128)(2,1)}, u32[]{:S(2)}) copy-start(bf16[8,1,2,128,128]{4,3,2,1,0:T(8,128)(2,1)} %param.15) | copy-start | bytes 1572868
  7.2 26.8 %copy-start.9 = (bf16[8,1,2,128,128]{4,3,2,1,0:T(8,128)(2,1)S(1)}, bf16[8,1,2,128,128]{4,3,2,1,0:T(8,128)(2,1)}, u32[]{:S(2)}) copy-start(bf16[8,1,2,128,128]{4,3,2,1,0:T(8,128)(2,1)} %param.14) | copy-start | bytes 1572868
  9.2 24.7 %all-to-all-start = ((bf16[16,32,1024]{2,1,0:T(8,128)(2,1)}), bf16[16,32,1024]{2,1,0:T(8,128)(2,1)S(1)}, u32[]{:S(2)}, u32[]{:S(2)}) async-start(bf16[16,32,1024]{2,1,0:T(8,128)(2,1)} %broadcast_in_dim.348), calls=%async_computation | async-start | bytes 2097152 | tf_op jit(solution)/shard_map/all_to_all | solution.py:59
  16.3 70.8 %reduce-scatter.3.cloned.1.call-start = ((), (), s32[]{:S(2)}) async-start(), calls=%async_computation.6 | async-start | bytes 2359296 | tf_op jit(solution)/shard_map/reduce_scatter | solution.py:131
  34.0 2.8 collective-permute-start
  35.2 3.6 %copy-start.3 = (bf16[8,128,8,128]{3,2,1,0:T(8,128)(2,1)}, bf16[8,128,8,128]{3,2,1,0:T(8,128)(2,1)S(1)}, u32[]{:S(2)}) copy-start(bf16[8,128,8,128]{3,2,1,0:T(8,128)(2,1)S(1)} %select_add_fusion.1) | copy-start | bytes 6291460
  42.5 0.7 copy-start.7
  42.5 85.8 %all-gather.5.cloned.1.call-start = ((), (), s32[]{:S(2)}) async-start(), calls=%async_computation.7 | async-start | bytes 2359296 | tf_op jit(solution)/shard_map/all_gather | solution.py:137
  45.4 3.7 %collective-permute-start.1 = (f32[1025]{0:T(1024)S(1)}, f32[1025]{0:T(1024)S(1)}, u32[]{:S(2)}, u32[]{:S(2)}) collective-permute-start(f32[1025]{0:T(1024)S(1)} %pad_maximum_fusion.1), channel_id=1, source_target_pairs={{0,1},{1,0},{2,3},{3,2},{4,5},{5,4},{6,7},{7,6},{8,9},{9,8},{10,11... | collective-permute-start | bytes 12308 | tf_op jit(solution)/shard_map/ppermute | solution.py:51
  49.8 5.1 %collective-permute-start.2 = (f32[1025]{0:T(1024)S(1)}, f32[1025]{0:T(1024)S(1)}, u32[]{:S(2)}, u32[]{:S(2)}) collective-permute-start(f32[1025]{0:T(1024)S(1)} %fusion.49), channel_id=1, source_target_pairs={{0,2},{1,3},{2,0},{3,1},{4,6},{5,7},{6,4},{7,5},{8,10},{9,11},{10,... | collective-permute-start | bytes 12308 | tf_op jit(solution)/shard_map/ppermute | solution.py:51
  54.9 7.7 %collective-permute-start.3 = (f32[1025]{0:T(1024)S(1)}, f32[1025]{0:T(1024)S(1)}, u32[]{:S(2)}, u32[]{:S(2)}) collective-permute-start(f32[1025]{0:T(1024)S(1)} %add.173), channel_id=1, source_target_pairs={{0,4},{1,5},{2,6},{3,7},{4,0},{5,1},{6,2},{7,3},{8,12},{9,13},{10,... | collective-permute-start | bytes 12308 | tf_op jit(solution)/shard_map/ppermute | solution.py:51
  63.7 1.2 collective-permute-start.4
  66.3 3.6 %collective-permute-start.5 = (f32[1]{0:T(128)}, f32[1]{0:T(128)}, u32[]{:S(2)}, u32[]{:S(2)}) collective-permute-start(f32[1]{0:T(128)} %add.175), channel_id=1, source_target_pairs={{0,16},{8,24},{16,0},{24,8},{32,48},{40,56},{48,32},{56,40},{64,80... | collective-permute-start | bytes 20 | tf_op jit(solution)/shard_map/ppermute | solution.py:51
  70.6 5.1 %collective-permute-start.6 = (f32[1]{0:T(128)}, f32[1]{0:T(128)}, u32[]{:S(2)}, u32[]{:S(2)}) collective-permute-start(f32[1]{0:T(128)} %add.176), channel_id=1, source_target_pairs={{0,32},{8,40},{16,48},{24,56},{32,0},{40,8},{48,16},{56,24},{64,96... | collective-permute-start | bytes 20 | tf_op jit(solution)/shard_map/ppermute | solution.py:51
  76.3 3.6 %collective-permute-start.7 = (f32[1]{0:T(128)}, f32[1]{0:T(128)}, u32[]{:S(2)}, u32[]{:S(2)}) collective-permute-start(f32[1]{0:T(128)} %add.177), channel_id=1, source_target_pairs={{0,64},{8,72},{16,80},{24,88},{32,96},{40,104},{48,112},{56,120},{... | collective-permute-start | bytes 20 | tf_op jit(solution)/shard_map/ppermute | solution.py:51
  80.6 5.1 %collective-permute-start.8 = (f32[1]{0:T(128)}, f32[1]{0:T(128)}, u32[]{:S(2)}, u32[]{:S(2)}) collective-permute-start(f32[1]{0:T(128)} %add.178), channel_id=1, source_target_pairs={{0,128},{8,136},{16,144},{24,152},{32,160},{40,168},{48,176},{56,1... | collective-permute-start | bytes 20 | tf_op jit(solution)/shard_map/ppermute | solution.py:51
  89.0 139.2 %reduce-scatter.5.cloned.1.call-start = ((), (), s32[]{:S(2)}) async-start(), calls=%async_computation.8 | async-start | bytes 2359296 | tf_op jit(solution)/shard_map/reduce_scatter | solution.py:147
  133.0 2.9 collective-permute-start.9
  136.6 25.7 %copy-start.11 = (bf16[32,1024]{1,0:T(8,128)(2,1)S(1)}, bf16[32,1024]{1,0:T(8,128)(2,1)}, u32[]{:S(2)}) copy-start(bf16[32,1024]{1,0:T(8,128)(2,1)} %param.12) | copy-start | bytes 196612
  162.3 22.7 %copy-start.10 = (bf16[32,1024]{1,0:T(8,128)(2,1)}, bf16[32,1024]{1,0:T(8,128)(2,1)S(1)}, u32[]{:S(2)}) copy-start(bf16[32,1024]{1,0:T(8,128)(2,1)S(1)} %reduce_sum.68) | copy-start | bytes 196612
  181.9 2.7 collective-permute-start.10
  185.0 2.3 copy-start.5
  185.2 1.4 copy-start.1
  191.0 82.6 %all-gather.7.cloned.1.call-start = ((), (), s32[]{:S(2)}) async-start(), calls=%async_computation.9 | async-start | bytes 2506752 | tf_op jit(solution)/shard_map/all_gather | solution.py:158
  273.6 2.2 copy-start.4
  275.5 2.7 copy-start
  278.2 1.3 copy-start.2
  280.6 4.3 %collective-permute-start.11 = (bf16[16,32,1024]{2,1,0:T(8,128)(2,1)}, bf16[16,32,1024]{2,1,0:T(8,128)(2,1)S(1)}, u32[]{:S(2)}, u32[]{:S(2)}) collective-permute-start(bf16[16,32,1024]{2,1,0:T(8,128)(2,1)} %select_bitcast_fusion), channel_id=1, source_target_pairs={{0,8},{8,0},{1,9},{9,1},{2,10},{10,2},{3,11},{11,3},{4,12},{12,4},... | collective-permute-start | bytes 3145736 | tf_op jit(solution)/shard_map/ppermute | solution.py:72
  282.0 1.6 collective-permute-start.12
  288.4 28.2 %all-to-all-start.3 = ((bf16[16,33,1024]{2,1,0:T(8,128)(2,1)}), bf16[16,33,1024]{2,1,0:T(8,128)(2,1)S(1)}, u32[]{:S(2)}, u32[]{:S(2)}) async-start(bf16[16,33,1024]{2,1,0:T(8,128)(2,1)} %pad_maximum_fusion), calls=%async_computation.5 | async-start | bytes 2621440 | tf_op jit(solution)/shard_map/all_to_all | solution.py:172
  298.4 4.2 %copy-start.6 = (bf16[1024,1024]{1,0:T(8,128)(2,1)S(1)}, bf16[1024,1024]{1,0:T(8,128)(2,1)}, u32[]{:S(2)}) copy-start(bf16[1024,1024]{1,0:T(8,128)(2,1)} %copy.193) | copy-start | bytes 6291460
  (1 other events, 0.7 us)
Sparse Core Ops, SparseCore 0:
  42.6 40.6 reduce-scatter.2
  89.1 39.1 all-gather.4
  191.1 37.1 reduce-scatter.4
  233.2 40.3 all-gather.6

commit v9 on v8

--- a/solution.py
+++ b/solution.py
@@ -29,10 +29,8 @@
     rows = lax.broadcasted_iota(jnp.int32, (feature_blocks,) + row_index.shape, 0)
     hit = rows == row_index[None]
     by_col = jnp.transpose(dense, (0, 2, 1, 3))
-    picked = jnp.zeros(row_index.shape + dense.shape[1:2] + dense.shape[3:4], dense.dtype)
-    for r in range(feature_blocks):
-        picked = picked + jnp.where(hit[r][:, :, None, None], by_col[r][:, None], 0.0)
-    return picked
+    chosen = jnp.where(hit[:, :, :, None, None], by_col[:, :, None], 0.0)
+    return jnp.sum(chosen, axis=0)
 
 
 def group_size(axis):

time: 330 us -> 328 us (level)
  waiting for transfers between devices: 132 us -> 152 us
  local copies, waits for them, and re-layouts: 46.2 us -> 27.5 us
    reduce_scatter x1, waiting for transfers between devices: 1.71 us -> 21.9 us  [body(): lax.psum_scatter(back_part.astype(jnp.bfloat16), 'blk', scatter_dimension...]
    broadcast_in_dim x18 -> x0, local copies, waits for them, and re-layouts: 19.8 us -> none  [pick_tiles(): jnp.where(hit[r][:, :, None, None], by_col[r][:, None], 0.0)]
    unnamed x33 -> x34, local copies, waits for them, and re-layouts: 4.62 us -> 7.14 us
  transfers between devices with their start and end apart: 19 -> 19, of which waited for: 17 -> 17; matrix products, arithmetic and copies ran while one was open for 17% -> 11% of each run, Pallas kernels for 0% -> 0%
where the time goes in v9:
time: 328 us; the launch traced here: 327 us
  waiting for transfers between devices  152 us (46%)
  blocking collectives  43.8 us (13%)
  starting transfers between devices  31.6 us (10%)
  local copies, waits for them, and re-layouts  27.5 us (8%)
  other arithmetic  26.5 us (8%)
  matrix products  23.8 us (7%)
  between operations  22.2 us (7%)
    all_gather x1, waiting for transfers between devices, body(): lax.all_gather(with_row(slope_own, split_three(curvature_part)), 'blk', a...  40.6 us
    all_gather x1, waiting for transfers between devices, body(): active_full = lax.all_gather(active_own, 'blk', axis=0, tiled=True)  37.1 us
    all_to_all x1, blocking collectives, sum_rows(): received = lax.all_to_all(pair_rows(value), 'chip', 0, 0, tiled=False)  24.3 us
    reduce_scatter x1, waiting for transfers between devices, body(): lax.psum_scatter(back_part.astype(jnp.bfloat16), 'blk', scatter_dimension...  21.9 us
    all_to_all x1, blocking collectives, gather_rows(): mine = lax.all_to_all(spread, 'chip', 0, 0, tiled=False)  19.5 us
    ppermute x8, waiting for transfers between devices, butterfly_sum(): lax.ppermute(value, axis, [(i, i ^ step) for i in range(size)])  19.1 us
    all_to_all x1, waiting for transfers between devices, gather_rows(): mine = lax.all_to_all(spread, 'chip', 0, 0, tiled=False)  17.6 us
    ppermute x8, starting transfers between devices, butterfly_sum(): lax.ppermute(value, axis, [(i, i ^ step) for i in range(size)])  16.8 us
  transfers between devices with their start and end apart: 19, of which 17 were waited for; matrix products, arithmetic and copies ran while one was open for 11% of the time, Pallas kernels for 0%

profile of v9, /device:TPU:32, one launch (start us, length us, event | category | flops | bytes accessed | tf_op | source)
XLA Modules:
  0.0 326.9 jit_solution(12987056981566215361)
XLA Ops:
  7.2 2.0 broadcast_in_dim.148
  9.2 7.0 %all-to-all-start = ((bf16[16,32,1024]{2,1,0:T(8,128)(2,1)}), bf16[16,32,1024]{2,1,0:T(8,128)(2,1)S(1)}, u32[]{:S(2)}, u32[]{:S(2)}) async-start(bf16[16,32,1024]{2,1,0:T(8,128)(2,1)} %broadcast_in_dim.148), calls=%async_computation | async-start | bytes 2097152 | tf_op jit(solution)/shard_map/all_to_all | solution.py:57
  16.4 17.6 %all-to-all-done = bf16[16,32,1024]{2,1,0:T(8,128)(2,1)S(1)} async-done(((bf16[16,32,1024]{2,1,0:T(8,128)(2,1)}), bf16[16,32,1024]{2,1,0:T(8,128)(2,1)S(1)}, u32[]{:S(2)}, u32[]{:S(2)}) %all-to-all-start) | async-done | bytes 1048608 | tf_op jit(solution)/shard_map/all_to_all | solution.py:57
  38.9 3.7 %fusion.10 = bf16[1024,1024]{1,0:T(8,128)(2,1)} fusion(bf16[1024,1024]{1,0:T(8,128)(2,1)S(1)} %bitcast.172, bf16[128,8,8,128]{3,2,1,0:T(8,128)(2,1)S(1)} %bitcast.185), kind=kOutput, calls=%fused_computation.22 | convolution fusion | flops 2148532224 | bytes 6291456 | tf_op jit(solution)/shard_map/dot_general | solution.py:128
  45.7 3.5 %collective-permute-done.1 = f32[1025]{0:T(1024)S(1)} collective-permute-done((f32[1025]{0:T(1024)S(1)}, f32[1025]{0:T(1024)S(1)}, u32[]{:S(2)}, u32[]{:S(2)}) %collective-permute-start.1) | collective-permute-done | bytes 4132 | tf_op jit(solution)/shard_map/ppermute | solution.py:49
  49.9 3.4 %collective-permute-start.2 = (f32[1025]{0:T(1024)S(1)}, f32[1025]{0:T(1024)S(1)}, u32[]{:S(2)}, u32[]{:S(2)}) collective-permute-start(f32[1025]{0:T(1024)S(1)} %fusion.49), channel_id=1, source_target_pairs={{0,2},{1,3},{2,0},{3,1},{4,6},{5,7},{6,4},{7,5},{8,10},{9,11},{10,... | collective-permute-start | bytes 12308 | tf_op jit(solution)/shard_map/ppermute | solution.py:49
  55.0 6.0 %collective-permute-start.3 = (f32[1025]{0:T(1024)S(1)}, f32[1025]{0:T(1024)S(1)}, u32[]{:S(2)}, u32[]{:S(2)}) collective-permute-start(f32[1025]{0:T(1024)S(1)} %add.124), channel_id=1, source_target_pairs={{0,4},{1,5},{2,6},{3,7},{4,0},{5,1},{6,2},{7,3},{8,12},{9,13},{10,... | collective-permute-start | bytes 12308 | tf_op jit(solution)/shard_map/ppermute | solution.py:49
  70.7 2.0 collective-permute-start.6
  72.7 3.2 collective-permute-done.6
  77.9 2.3 collective-permute-done.7
  82.7 3.3 %collective-permute-done.8 = f32[1]{0:T(128)} collective-permute-done((f32[1]{0:T(128)}, f32[1]{0:T(128)}, u32[]{:S(2)}, u32[]{:S(2)}) %collective-permute-start.8) | collective-permute-done | bytes 36 | tf_op jit(solution)/shard_map/ppermute | solution.py:49
  89.4 2.0 select_add_fusion
  91.4 37.1 %all-gather.5.cloned.1.call-done = bf16[1024,1024]{1,0:T(8,128)(2,1)} async-done(((bf16[128,1024]{1,0:T(8,128)(2,1)}), bf16[1024,1024]{1,0:T(8,128)(2,1)}) %all-gather.5.cloned.1.call-update) | async-done | bytes 2097168 | tf_op jit(solution)/shard_map/all_gather | solution.py:135
  128.5 4.5 %fusion.16 = bf16[1024,1024]{1,0:T(8,128)(2,1)S(1)} fusion(bf16[1024,1024]{1,0:T(8,128)(2,1)} %all-gather.5.cloned.1.call-done, bf16[128,8,8,128]{3,2,1,0:T(8,128)(2,1)} %bitcast.188), kind=kOutput, calls=%fused_computation.24 | convolution fusion | flops 2148532224 | bytes 6291456 | tf_op jit(solution)/shard_map/dot_general | solution.py:137
  133.4 2.6 collective-permute-done.9
  136.7 24.3 %all_to_all.20 = bf16[16,32,1024]{2,1,0:T(8,128)(2,1)} all-to-all(bf16[16,32,1024]{2,1,0:T(8,128)(2,1)S(1)} %fusion.9), channel_id=1, replica_groups=mesh['chip'=16,'core'=2,'blk'=8] {'chip'}, dimensions={0} | all-to-all | bytes 2097152 | tf_op jit(solution)/shard_map/all_to_all | solution.py:75
  162.6 19.5 %all_to_all.21 = bf16[16,32,1024]{2,1,0:T(8,128)(2,1)S(1)} all-to-all(bf16[16,32,1024]{2,1,0:T(8,128)(2,1)S(1)} %broadcast_in_dim.172), channel_id=1, replica_groups=mesh['chip'=16,'core'=2,'blk'=8] {'chip'}, dimensions={0} | all-to-all | bytes 2097152 | tf_op jit(solution)/shard_map/all_to_all | solution.py:57
  182.1 2.7 collective-permute-done.10
  187.4 3.7 %fusion.19 = bf16[1024,1024]{1,0:T(8,128)(2,1)} fusion(bf16[1024,1024]{1,0:T(8,128)(2,1)S(1)} %bitcast.178, bf16[128,8,8,128]{3,2,1,0:T(8,128)(2,1)S(1)} %bitcast.189), kind=kOutput, calls=%fused_computation.25 | convolution fusion | flops 2148532224 | bytes 6291456 | tf_op jit(solution)/shard_map/dot_general | solution.py:142
  192.0 4.0 %copy.117 = bf16[1024,1024]{1,0:T(8,128)(2,1)} copy(bf16[1024,1024]{0,1:T(8,128)(2,1)} %bitcast.187) | data formatting | bytes 4194304 | tf_op jit(solution)/shard_map/dot_general | solution.py:148
  195.9 4.0 %copy.116 = bf16[1024,1024]{1,0:T(8,128)(2,1)} copy(bf16[1024,1024]{0,1:T(8,128)(2,1)} %bitcast.179) | data formatting | bytes 4194304 | tf_op jit(solution)/shard_map/dot_general | solution.py:148
  199.9 4.6 %convolution_bitcast_fusion.1 = f32[8,8,128,128]{3,2,1,0:T(8,128)S(1)} fusion(bf16[8,128,1024,1]{2,1,3,0:T(8,128)(2,1)} %bitcast.192, bf16[8,128,1024,1]{2,1,0,3:T(8,128)(2,1)} %bitcast.191), kind=kOutput, calls=%fused_computation.4 | convolution fusion | flops 2147483648 | bytes 8388608 | tf_op jit(solution)/shard_map/dot_general | solution.py:148
  206.6 21.9 %reduce-scatter.5.cloned.1.call-done = bf16[128,1024]{1,0:T(8,128)(2,1)} async-done(((bf16[1024,1024]{1,0:T(8,128)(2,1)}), bf16[128,1024]{1,0:T(8,128)(2,1)}) %reduce-scatter.5.cloned.1.call-update) | async-done | bytes 262160 | tf_op jit(solution)/shard_map/reduce_scatter | solution.py:145
  233.2 40.6 %all-gather.7.cloned.1.call-done = bf16[8,129,1024]{2,1,0:T(8,128)(2,1)} async-done(((bf16[1,129,1024]{2,1,0:T(8,128)(2,1)}), bf16[8,129,1024]{2,1,0:T(8,128)(2,1)}) %all-gather.7.cloned.1.call-update) | async-done | bytes 2113552 | tf_op jit(solution)/shard_map/all_gather | solution.py:156
  276.0 2.4 fusion.13
  285.2 2.2 fusion.8
  288.6 6.8 %all-to-all-start.3 = ((bf16[16,33,1024]{2,1,0:T(8,128)(2,1)}), bf16[16,33,1024]{2,1,0:T(8,128)(2,1)S(1)}, u32[]{:S(2)}, u32[]{:S(2)}) async-start(bf16[16,33,1024]{2,1,0:T(8,128)(2,1)} %pad_maximum_fusion), calls=%async_computation.5 | async-start | bytes 2621440 | tf_op jit(solution)/shard_map/all_to_all | solution.py:170
  295.4 2.6 copy.118
  298.7 2.5 copy.111
  301.3 2.5 copy.107
  303.8 4.6 %convolution_bitcast_fusion = f32[8,8,128,128]{3,2,1,0:T(8,128)S(1)} fusion(bf16[8,128,1024,1]{2,1,3,0:T(8,128)(2,1)} %bitcast.190, bf16[8,128,1024,1]{2,1,0,3:T(8,128)(2,1)} %bitcast.193), kind=kOutput, calls=%fused_computation.3 | convolution fusion | flops 2147483648 | bytes 8388608 | tf_op jit(solution)/shard_map/dot_general | solution.py:178
  309.4 7.4 %all-to-all-done.3 = bf16[16,33,1024]{2,1,0:T(8,128)(2,1)S(1)} async-done(((bf16[16,33,1024]{2,1,0:T(8,128)(2,1)}), bf16[16,33,1024]{2,1,0:T(8,128)(2,1)S(1)}, u32[]{:S(2)}, u32[]{:S(2)}) %all-to-all-start.3) | async-done | bytes 1081376 | tf_op jit(solution)/shard_map/all_to_all | solution.py:170
  (116 shorter events, 48.3 us)
Async XLA Ops:
  7.2 9.1 %copy-start.13 = (s32[8,1]{0,1:T(1,128)S(1)}, s32[8,1]{0,1:T(1,128)}, u32[]{:S(2)}) copy-start(s32[8,1]{0,1:T(1,128)} %param.17) | copy-start | bytes 100
  7.2 26.8 %copy-start.8 = (bf16[8,1,2,128,128]{4,3,2,1,0:T(8,128)(2,1)S(1)}, bf16[8,1,2,128,128]{4,3,2,1,0:T(8,128)(2,1)}, u32[]{:S(2)}) copy-start(bf16[8,1,2,128,128]{4,3,2,1,0:T(8,128)(2,1)} %param.15) | copy-start | bytes 1572868
  7.2 26.8 %copy-start.9 = (bf16[8,1,2,128,128]{4,3,2,1,0:T(8,128)(2,1)S(1)}, bf16[8,1,2,128,128]{4,3,2,1,0:T(8,128)(2,1)}, u32[]{:S(2)}) copy-start(bf16[8,1,2,128,128]{4,3,2,1,0:T(8,128)(2,1)} %param.14) | copy-start | bytes 1572868
  9.2 24.7 %all-to-all-start = ((bf16[16,32,1024]{2,1,0:T(8,128)(2,1)}), bf16[16,32,1024]{2,1,0:T(8,128)(2,1)S(1)}, u32[]{:S(2)}, u32[]{:S(2)}) async-start(bf16[16,32,1024]{2,1,0:T(8,128)(2,1)} %broadcast_in_dim.148), calls=%async_computation | async-start | bytes 2097152 | tf_op jit(solution)/shard_map/all_to_all | solution.py:57
  16.3 71.0 %reduce-scatter.3.cloned.1.call-start = ((), (), s32[]{:S(2)}) async-start(), calls=%async_computation.6 | async-start | bytes 2359296 | tf_op jit(solution)/shard_map/reduce_scatter | solution.py:129
  34.0 2.8 collective-permute-start
  35.2 3.7 %copy-start.4 = (bf16[8,128,8,128]{3,2,1,0:T(8,128)(2,1)}, bf16[8,128,8,128]{3,2,1,0:T(8,128)(2,1)S(1)}, u32[]{:S(2)}) copy-start(bf16[8,128,8,128]{3,2,1,0:T(8,128)(2,1)S(1)} %select_add_fusion.1) | copy-start | bytes 6291460
  42.5 0.7 copy-start.7
  42.6 85.9 %all-gather.5.cloned.1.call-start = ((), (), s32[]{:S(2)}) async-start(), calls=%async_computation.7 | async-start | bytes 2359296 | tf_op jit(solution)/shard_map/all_gather | solution.py:135
  45.5 3.7 %collective-permute-start.1 = (f32[1025]{0:T(1024)S(1)}, f32[1025]{0:T(1024)S(1)}, u32[]{:S(2)}, u32[]{:S(2)}) collective-permute-start(f32[1025]{0:T(1024)S(1)} %pad_maximum_fusion.1), channel_id=1, source_target_pairs={{0,1},{1,0},{2,3},{3,2},{4,5},{5,4},{6,7},{7,6},{8,9},{9,8},{10,11... | collective-permute-start | bytes 12308 | tf_op jit(solution)/shard_map/ppermute | solution.py:49
  49.9 5.1 %collective-permute-start.2 = (f32[1025]{0:T(1024)S(1)}, f32[1025]{0:T(1024)S(1)}, u32[]{:S(2)}, u32[]{:S(2)}) collective-permute-start(f32[1025]{0:T(1024)S(1)} %fusion.49), channel_id=1, source_target_pairs={{0,2},{1,3},{2,0},{3,1},{4,6},{5,7},{6,4},{7,5},{8,10},{9,11},{10,... | collective-permute-start | bytes 12308 | tf_op jit(solution)/shard_map/ppermute | solution.py:49
  55.0 7.7 %collective-permute-start.3 = (f32[1025]{0:T(1024)S(1)}, f32[1025]{0:T(1024)S(1)}, u32[]{:S(2)}, u32[]{:S(2)}) collective-permute-start(f32[1025]{0:T(1024)S(1)} %add.124), channel_id=1, source_target_pairs={{0,4},{1,5},{2,6},{3,7},{4,0},{5,1},{6,2},{7,3},{8,12},{9,13},{10,... | collective-permute-start | bytes 12308 | tf_op jit(solution)/shard_map/ppermute | solution.py:49
  63.8 1.4 collective-permute-start.4
  66.4 3.7 %collective-permute-start.5 = (f32[1]{0:T(128)}, f32[1]{0:T(128)}, u32[]{:S(2)}, u32[]{:S(2)}) collective-permute-start(f32[1]{0:T(128)} %add.126), channel_id=1, source_target_pairs={{0,16},{8,24},{16,0},{24,8},{32,48},{40,56},{48,32},{56,40},{64,80... | collective-permute-start | bytes 20 | tf_op jit(solution)/shard_map/ppermute | solution.py:49
  70.7 5.2 %collective-permute-start.6 = (f32[1]{0:T(128)}, f32[1]{0:T(128)}, u32[]{:S(2)}, u32[]{:S(2)}) collective-permute-start(f32[1]{0:T(128)} %add.127), channel_id=1, source_target_pairs={{0,32},{8,40},{16,48},{24,56},{32,0},{40,8},{48,16},{56,24},{64,96... | collective-permute-start | bytes 20 | tf_op jit(solution)/shard_map/ppermute | solution.py:49
  76.5 3.7 %collective-permute-start.7 = (f32[1]{0:T(128)}, f32[1]{0:T(128)}, u32[]{:S(2)}, u32[]{:S(2)}) collective-permute-start(f32[1]{0:T(128)} %add.128), channel_id=1, source_target_pairs={{0,64},{8,72},{16,80},{24,88},{32,96},{40,104},{48,112},{56,120},{... | collective-permute-start | bytes 20 | tf_op jit(solution)/shard_map/ppermute | solution.py:49
  80.8 5.2 %collective-permute-start.8 = (f32[1]{0:T(128)}, f32[1]{0:T(128)}, u32[]{:S(2)}, u32[]{:S(2)}) collective-permute-start(f32[1]{0:T(128)} %add.129), channel_id=1, source_target_pairs={{0,128},{8,136},{16,144},{24,152},{32,160},{40,168},{48,176},{56,1... | collective-permute-start | bytes 20 | tf_op jit(solution)/shard_map/ppermute | solution.py:49
  89.2 139.3 %reduce-scatter.5.cloned.1.call-start = ((), (), s32[]{:S(2)}) async-start(), calls=%async_computation.8 | async-start | bytes 2359296 | tf_op jit(solution)/shard_map/reduce_scatter | solution.py:145
  133.1 2.9 collective-permute-start.9
  136.7 25.7 %copy-start.11 = (bf16[32,1024]{1,0:T(8,128)(2,1)S(1)}, bf16[32,1024]{1,0:T(8,128)(2,1)}, u32[]{:S(2)}) copy-start(bf16[32,1024]{1,0:T(8,128)(2,1)} %param.12) | copy-start | bytes 196612
  162.4 22.7 %copy-start.10 = (bf16[32,1024]{1,0:T(8,128)(2,1)}, bf16[32,1024]{1,0:T(8,128)(2,1)S(1)}, u32[]{:S(2)}) copy-start(bf16[32,1024]{1,0:T(8,128)(2,1)S(1)} %reduce_sum.86) | copy-start | bytes 196612
  182.1 2.7 collective-permute-start.10
  185.1 2.3 copy-start.6
  185.3 1.4 copy-start.3
  191.2 82.6 %all-gather.7.cloned.1.call-start = ((), (), s32[]{:S(2)}) async-start(), calls=%async_computation.9 | async-start | bytes 2506752 | tf_op jit(solution)/shard_map/all_gather | solution.py:156
  273.8 2.2 copy-start.5
  275.7 2.7 copy-start
  278.4 1.3 copy-start.2
  280.8 4.3 %collective-permute-start.11 = (bf16[16,32,1024]{2,1,0:T(8,128)(2,1)}, bf16[16,32,1024]{2,1,0:T(8,128)(2,1)S(1)}, u32[]{:S(2)}, u32[]{:S(2)}) collective-permute-start(bf16[16,32,1024]{2,1,0:T(8,128)(2,1)} %select_bitcast_fusion), channel_id=1, source_target_pairs={{0,8},{8,0},{1,9},{9,1},{2,10},{10,2},{3,11},{11,3},{4,12},{12,4},... | collective-permute-start | bytes 3145736 | tf_op jit(solution)/shard_map/ppermute | solution.py:70
  282.3 1.6 collective-permute-start.12
  288.6 28.2 %all-to-all-start.3 = ((bf16[16,33,1024]{2,1,0:T(8,128)(2,1)}), bf16[16,33,1024]{2,1,0:T(8,128)(2,1)S(1)}, u32[]{:S(2)}, u32[]{:S(2)}) async-start(bf16[16,33,1024]{2,1,0:T(8,128)(2,1)} %pad_maximum_fusion), calls=%async_computation.5 | async-start | bytes 2621440 | tf_op jit(solution)/shard_map/all_to_all | solution.py:170
  298.0 3.3 copy-start.1
  (1 other events, 0.7 us)
Sparse Core Ops, SparseCore 0:
  42.7 40.7 reduce-scatter.2
  89.3 39.1 all-gather.4
  191.3 37.1 reduce-scatter.4
  233.4 40.4 all-gather.6

commit v10 on v9

--- a/solution.py
+++ b/solution.py
@@ -57,7 +57,7 @@
     mine = lax.all_to_all(spread, "chip", 0, 0, tiled=False)
     other = lax.ppermute(mine, "core", [(0, 1), (1, 0)])
     first = lax.axis_index("core") == 0
-    pair = jnp.where(first, jnp.stack([mine, other], 1), jnp.stack([other, mine], 1))
+    pair = jnp.stack([jnp.where(first, mine, other), jnp.where(first, other, mine)], 1)
     return pair.reshape((-1,) + value.shape[1:])
 
 

time: 328 us -> 327 us (level)
  transfers between devices with their start and end apart: 19 -> 19, of which waited for: 17 -> 17; matrix products, arithmetic and copies ran while one was open for 11% -> 12% of each run, Pallas kernels for 0% -> 0%
where the time goes in v10:
time: 327 us; the launch traced here: 326 us
  waiting for transfers between devices  151 us (46%)
  blocking collectives  43.8 us (13%)
  starting transfers between devices  31.5 us (10%)
  local copies, waits for them, and re-layouts  27.3 us (8%)
  other arithmetic  26.2 us (8%)
  matrix products  23.8 us (7%)
  between operations  22.8 us (7%)
    all_gather x1, waiting for transfers between devices, body(): lax.all_gather(with_row(slope_own, split_three(curvature_part)), 'blk', a...  40.7 us
    all_gather x1, waiting for transfers between devices, body(): active_full = lax.all_gather(active_own, 'blk', axis=0, tiled=True)  37.1 us
    all_to_all x1, blocking collectives, sum_rows(): received = lax.all_to_all(pair_rows(value), 'chip', 0, 0, tiled=False)  24.3 us
    reduce_scatter x1, waiting for transfers between devices, body(): lax.psum_scatter(back_part.astype(jnp.bfloat16), 'blk', scatter_dimension...  21.7 us
    all_to_all x1, blocking collectives, gather_rows(): mine = lax.all_to_all(spread, 'chip', 0, 0, tiled=False)  19.5 us
    ppermute x8, waiting for transfers between devices, butterfly_sum(): lax.ppermute(value, axis, [(i, i ^ step) for i in range(size)])  18.4 us
    all_to_all x1, waiting for transfers between devices, gather_rows(): mine = lax.all_to_all(spread, 'chip', 0, 0, tiled=False)  17.6 us
    ppermute x8, starting transfers between devices, butterfly_sum(): lax.ppermute(value, axis, [(i, i ^ step) for i in range(size)])  16.7 us
  transfers between devices with their start and end apart: 19, of which 17 were waited for; matrix products, arithmetic and copies ran while one was open for 12% of the time, Pallas kernels for 0%

profile of v10, /device:TPU:32, one launch (start us, length us, event | category | flops | bytes accessed | tf_op | source)
XLA Modules:
  0.0 326.0 jit_solution(849292486093681003)
XLA Ops:
  7.2 2.0 broadcast_in_dim.148
  9.2 7.0 %all-to-all-start = ((bf16[16,32,1024]{2,1,0:T(8,128)(2,1)}), bf16[16,32,1024]{2,1,0:T(8,128)(2,1)S(1)}, u32[]{:S(2)}, u32[]{:S(2)}) async-start(bf16[16,32,1024]{2,1,0:T(8,128)(2,1)} %broadcast_in_dim.148), calls=%async_computation | async-start | bytes 2097152 | tf_op jit(solution)/shard_map/all_to_all | solution.py:57
  16.4 17.6 %all-to-all-done = bf16[16,32,1024]{2,1,0:T(8,128)(2,1)S(1)} async-done(((bf16[16,32,1024]{2,1,0:T(8,128)(2,1)}), bf16[16,32,1024]{2,1,0:T(8,128)(2,1)S(1)}, u32[]{:S(2)}, u32[]{:S(2)}) %all-to-all-start) | async-done | bytes 1048608 | tf_op jit(solution)/shard_map/all_to_all | solution.py:57
  38.3 3.7 %fusion.10 = bf16[1024,1024]{1,0:T(8,128)(2,1)} fusion(bf16[1024,1024]{1,0:T(8,128)(2,1)S(1)} %bitcast.178, bf16[128,8,8,128]{3,2,1,0:T(8,128)(2,1)S(1)} %bitcast.189), kind=kOutput, calls=%fused_computation.22 | convolution fusion | flops 2148532224 | bytes 6291456 | tf_op jit(solution)/shard_map/dot_general | solution.py:128
  45.1 3.5 %collective-permute-done.1 = f32[1025]{0:T(1024)S(1)} collective-permute-done((f32[1025]{0:T(1024)S(1)}, f32[1025]{0:T(1024)S(1)}, u32[]{:S(2)}, u32[]{:S(2)}) %collective-permute-start.1) | collective-permute-done | bytes 4132 | tf_op jit(solution)/shard_map/ppermute | solution.py:49
  49.3 3.4 %collective-permute-start.2 = (f32[1025]{0:T(1024)S(1)}, f32[1025]{0:T(1024)S(1)}, u32[]{:S(2)}, u32[]{:S(2)}) collective-permute-start(f32[1025]{0:T(1024)S(1)} %fusion.49), channel_id=1, source_target_pairs={{0,2},{1,3},{2,0},{3,1},{4,6},{5,7},{6,4},{7,5},{8,10},{9,11},{10,... | collective-permute-start | bytes 12308 | tf_op jit(solution)/shard_map/ppermute | solution.py:49
  54.4 6.0 %collective-permute-start.3 = (f32[1025]{0:T(1024)S(1)}, f32[1025]{0:T(1024)S(1)}, u32[]{:S(2)}, u32[]{:S(2)}) collective-permute-start(f32[1025]{0:T(1024)S(1)} %add.124), channel_id=1, source_target_pairs={{0,4},{1,5},{2,6},{3,7},{4,0},{5,1},{6,2},{7,3},{8,12},{9,13},{10,... | collective-permute-start | bytes 12308 | tf_op jit(solution)/shard_map/ppermute | solution.py:49
  70.0 2.0 collective-permute-start.6
  72.1 3.0 collective-permute-done.6
  77.1 2.2 collective-permute-done.7
  81.9 3.2 collective-permute-done.8
  88.6 2.0 select_add_fusion
  90.5 37.1 %all-gather.5.cloned.1.call-done = bf16[1024,1024]{1,0:T(8,128)(2,1)} async-done(((bf16[128,1024]{1,0:T(8,128)(2,1)}), bf16[1024,1024]{1,0:T(8,128)(2,1)}) %all-gather.5.cloned.1.call-update) | async-done | bytes 2097168 | tf_op jit(solution)/shard_map/all_gather | solution.py:135
  127.6 4.5 %fusion.16 = bf16[1024,1024]{1,0:T(8,128)(2,1)S(1)} fusion(bf16[1024,1024]{1,0:T(8,128)(2,1)} %all-gather.5.cloned.1.call-done, bf16[128,8,8,128]{3,2,1,0:T(8,128)(2,1)} %bitcast.192), kind=kOutput, calls=%fused_computation.24 | convolution fusion | flops 2148532224 | bytes 6291456 | tf_op jit(solution)/shard_map/dot_general | solution.py:137
  132.6 2.6 collective-permute-done.9
  135.9 24.3 %all_to_all.20 = bf16[16,32,1024]{2,1,0:T(8,128)(2,1)} all-to-all(bf16[16,32,1024]{2,1,0:T(8,128)(2,1)S(1)} %fusion.9), channel_id=1, replica_groups=mesh['chip'=16,'core'=2,'blk'=8] {'chip'}, dimensions={0} | all-to-all | bytes 2097152 | tf_op jit(solution)/shard_map/all_to_all | solution.py:75
  161.7 19.5 %all_to_all.21 = bf16[16,32,1024]{2,1,0:T(8,128)(2,1)S(1)} all-to-all(bf16[16,32,1024]{2,1,0:T(8,128)(2,1)S(1)} %broadcast_in_dim.172), channel_id=1, replica_groups=mesh['chip'=16,'core'=2,'blk'=8] {'chip'}, dimensions={0} | all-to-all | bytes 2097152 | tf_op jit(solution)/shard_map/all_to_all | solution.py:57
  181.2 2.7 collective-permute-done.10
  186.6 3.7 %fusion.19 = bf16[1024,1024]{1,0:T(8,128)(2,1)} fusion(bf16[1024,1024]{1,0:T(8,128)(2,1)S(1)} %bitcast.184, bf16[128,8,8,128]{3,2,1,0:T(8,128)(2,1)S(1)} %bitcast.193), kind=kOutput, calls=%fused_computation.25 | convolution fusion | flops 2148532224 | bytes 6291456 | tf_op jit(solution)/shard_map/dot_general | solution.py:142
  191.2 4.0 %copy.118 = bf16[1024,1024]{1,0:T(8,128)(2,1)} copy(bf16[1024,1024]{0,1:T(8,128)(2,1)} %bitcast.191) | data formatting | bytes 4194304 | tf_op jit(solution)/shard_map/dot_general | solution.py:148
  195.1 4.0 %copy.104 = bf16[1024,1024]{1,0:T(8,128)(2,1)} copy(bf16[1024,1024]{0,1:T(8,128)(2,1)} %bitcast.185) | data formatting | bytes 4194304 | tf_op jit(solution)/shard_map/dot_general | solution.py:148
  199.1 4.6 %convolution_bitcast_fusion.1 = f32[8,8,128,128]{3,2,1,0:T(8,128)S(1)} fusion(bf16[8,128,1024,1]{2,1,3,0:T(8,128)(2,1)} %bitcast.196, bf16[8,128,1024,1]{2,1,0,3:T(8,128)(2,1)} %bitcast.195), kind=kOutput, calls=%fused_computation.4 | convolution fusion | flops 2147483648 | bytes 8388608 | tf_op jit(solution)/shard_map/dot_general | solution.py:148
  205.8 21.7 %reduce-scatter.5.cloned.1.call-done = bf16[128,1024]{1,0:T(8,128)(2,1)} async-done(((bf16[1024,1024]{1,0:T(8,128)(2,1)}), bf16[128,1024]{1,0:T(8,128)(2,1)}) %reduce-scatter.5.cloned.1.call-update) | async-done | bytes 262160 | tf_op jit(solution)/shard_map/reduce_scatter | solution.py:145
  232.3 40.7 %all-gather.7.cloned.1.call-done = bf16[8,129,1024]{2,1,0:T(8,128)(2,1)} async-done(((bf16[1,129,1024]{2,1,0:T(8,128)(2,1)}), bf16[8,129,1024]{2,1,0:T(8,128)(2,1)}) %all-gather.7.cloned.1.call-update) | async-done | bytes 2113552 | tf_op jit(solution)/shard_map/all_gather | solution.py:156
  275.2 2.4 fusion.13
  284.4 2.2 fusion.8
  287.8 6.8 %all-to-all-start.3 = ((bf16[16,33,1024]{2,1,0:T(8,128)(2,1)}), bf16[16,33,1024]{2,1,0:T(8,128)(2,1)S(1)}, u32[]{:S(2)}, u32[]{:S(2)}) async-start(bf16[16,33,1024]{2,1,0:T(8,128)(2,1)} %pad_maximum_fusion.2), calls=%async_computation.5 | async-start | bytes 2621440 | tf_op jit(solution)/shard_map/all_to_all | solution.py:170
  294.6 2.6 copy.109
  298.0 2.5 copy.113
  300.6 2.6 copy.110
  303.1 4.6 %convolution_bitcast_fusion = f32[8,8,128,128]{3,2,1,0:T(8,128)S(1)} fusion(bf16[8,128,1024,1]{2,1,3,0:T(8,128)(2,1)} %bitcast.194, bf16[8,128,1024,1]{2,1,0,3:T(8,128)(2,1)} %bitcast.197), kind=kOutput, calls=%fused_computation.3 | convolution fusion | flops 2147483648 | bytes 8388608 | tf_op jit(solution)/shard_map/dot_general | solution.py:178
  308.7 7.3 %all-to-all-done.3 = bf16[16,33,1024]{2,1,0:T(8,128)(2,1)S(1)} async-done(((bf16[16,33,1024]{2,1,0:T(8,128)(2,1)}), bf16[16,33,1024]{2,1,0:T(8,128)(2,1)S(1)}, u32[]{:S(2)}, u32[]{:S(2)}) %all-to-all-start.3) | async-done | bytes 1081376 | tf_op jit(solution)/shard_map/all_to_all | solution.py:170
  (117 shorter events, 47.4 us)
Async XLA Ops:
  7.2 9.1 %copy-start.13 = (s32[8,1]{0,1:T(1,128)S(1)}, s32[8,1]{0,1:T(1,128)}, u32[]{:S(2)}) copy-start(s32[8,1]{0,1:T(1,128)} %param.17) | copy-start | bytes 100
  7.2 26.8 %copy-start.8 = (bf16[8,1,2,128,128]{4,3,2,1,0:T(8,128)(2,1)S(1)}, bf16[8,1,2,128,128]{4,3,2,1,0:T(8,128)(2,1)}, u32[]{:S(2)}) copy-start(bf16[8,1,2,128,128]{4,3,2,1,0:T(8,128)(2,1)} %param.15) | copy-start | bytes 1572868
  7.2 26.8 %copy-start.9 = (bf16[8,1,2,128,128]{4,3,2,1,0:T(8,128)(2,1)S(1)}, bf16[8,1,2,128,128]{4,3,2,1,0:T(8,128)(2,1)}, u32[]{:S(2)}) copy-start(bf16[8,1,2,128,128]{4,3,2,1,0:T(8,128)(2,1)} %param.14) | copy-start | bytes 1572868
  9.2 24.7 %all-to-all-start = ((bf16[16,32,1024]{2,1,0:T(8,128)(2,1)}), bf16[16,32,1024]{2,1,0:T(8,128)(2,1)S(1)}, u32[]{:S(2)}, u32[]{:S(2)}) async-start(bf16[16,32,1024]{2,1,0:T(8,128)(2,1)} %broadcast_in_dim.148), calls=%async_computation | async-start | bytes 2097152 | tf_op jit(solution)/shard_map/all_to_all | solution.py:57
  16.3 70.2 %reduce-scatter.3.cloned.1.call-start = ((), (), s32[]{:S(2)}) async-start(), calls=%async_computation.6 | async-start | bytes 2359296 | tf_op jit(solution)/shard_map/reduce_scatter | solution.py:129
  34.0 2.8 collective-permute-start
  35.2 3.1 copy-start.4
  42.0 0.7 copy-start.7
  42.0 85.6 %all-gather.5.cloned.1.call-start = ((), (), s32[]{:S(2)}) async-start(), calls=%async_computation.7 | async-start | bytes 2359296 | tf_op jit(solution)/shard_map/all_gather | solution.py:135
  44.9 3.7 %collective-permute-start.1 = (f32[1025]{0:T(1024)S(1)}, f32[1025]{0:T(1024)S(1)}, u32[]{:S(2)}, u32[]{:S(2)}) collective-permute-start(f32[1025]{0:T(1024)S(1)} %pad_maximum_fusion.3), channel_id=1, source_target_pairs={{0,1},{1,0},{2,3},{3,2},{4,5},{5,4},{6,7},{7,6},{8,9},{9,8},{10,11... | collective-permute-start | bytes 12308 | tf_op jit(solution)/shard_map/ppermute | solution.py:49
  49.3 5.1 %collective-permute-start.2 = (f32[1025]{0:T(1024)S(1)}, f32[1025]{0:T(1024)S(1)}, u32[]{:S(2)}, u32[]{:S(2)}) collective-permute-start(f32[1025]{0:T(1024)S(1)} %fusion.49), channel_id=1, source_target_pairs={{0,2},{1,3},{2,0},{3,1},{4,6},{5,7},{6,4},{7,5},{8,10},{9,11},{10,... | collective-permute-start | bytes 12308 | tf_op jit(solution)/shard_map/ppermute | solution.py:49
  54.4 7.7 %collective-permute-start.3 = (f32[1025]{0:T(1024)S(1)}, f32[1025]{0:T(1024)S(1)}, u32[]{:S(2)}, u32[]{:S(2)}) collective-permute-start(f32[1025]{0:T(1024)S(1)} %add.124), channel_id=1, source_target_pairs={{0,4},{1,5},{2,6},{3,7},{4,0},{5,1},{6,2},{7,3},{8,12},{9,13},{10,... | collective-permute-start | bytes 12308 | tf_op jit(solution)/shard_map/ppermute | solution.py:49
  63.3 1.2 collective-permute-start.4
  65.8 3.6 %collective-permute-start.5 = (f32[1]{0:T(128)}, f32[1]{0:T(128)}, u32[]{:S(2)}, u32[]{:S(2)}) collective-permute-start(f32[1]{0:T(128)} %add.126), channel_id=1, source_target_pairs={{0,16},{8,24},{16,0},{24,8},{32,48},{40,56},{48,32},{56,40},{64,80... | collective-permute-start | bytes 20 | tf_op jit(solution)/shard_map/ppermute | solution.py:49
  70.0 5.1 %collective-permute-start.6 = (f32[1]{0:T(128)}, f32[1]{0:T(128)}, u32[]{:S(2)}, u32[]{:S(2)}) collective-permute-start(f32[1]{0:T(128)} %add.127), channel_id=1, source_target_pairs={{0,32},{8,40},{16,48},{24,56},{32,0},{40,8},{48,16},{56,24},{64,96... | collective-permute-start | bytes 20 | tf_op jit(solution)/shard_map/ppermute | solution.py:49
  75.8 3.6 %collective-permute-start.7 = (f32[1]{0:T(128)}, f32[1]{0:T(128)}, u32[]{:S(2)}, u32[]{:S(2)}) collective-permute-start(f32[1]{0:T(128)} %add.128), channel_id=1, source_target_pairs={{0,64},{8,72},{16,80},{24,88},{32,96},{40,104},{48,112},{56,120},{... | collective-permute-start | bytes 20 | tf_op jit(solution)/shard_map/ppermute | solution.py:49
  80.0 5.1 %collective-permute-start.8 = (f32[1]{0:T(128)}, f32[1]{0:T(128)}, u32[]{:S(2)}, u32[]{:S(2)}) collective-permute-start(f32[1]{0:T(128)} %add.129), channel_id=1, source_target_pairs={{0,128},{8,136},{16,144},{24,152},{32,160},{40,168},{48,176},{56,1... | collective-permute-start | bytes 20 | tf_op jit(solution)/shard_map/ppermute | solution.py:49
  88.3 139.2 %reduce-scatter.5.cloned.1.call-start = ((), (), s32[]{:S(2)}) async-start(), calls=%async_computation.8 | async-start | bytes 2359296 | tf_op jit(solution)/shard_map/reduce_scatter | solution.py:145
  132.3 2.9 collective-permute-start.9
  135.9 25.7 %copy-start.11 = (bf16[32,1024]{1,0:T(8,128)(2,1)S(1)}, bf16[32,1024]{1,0:T(8,128)(2,1)}, u32[]{:S(2)}) copy-start(bf16[32,1024]{1,0:T(8,128)(2,1)} %param.12) | copy-start | bytes 196612
  161.6 22.5 %copy-start.10 = (bf16[32,1024]{1,0:T(8,128)(2,1)}, bf16[32,1024]{1,0:T(8,128)(2,1)S(1)}, u32[]{:S(2)}) copy-start(bf16[32,1024]{1,0:T(8,128)(2,1)S(1)} %reduce_sum.86) | copy-start | bytes 196612
  181.2 2.7 collective-permute-start.10
  184.3 2.3 copy-start.6
  184.5 1.4 copy-start.3
  190.4 82.7 %all-gather.7.cloned.1.call-start = ((), (), s32[]{:S(2)}) async-start(), calls=%async_computation.9 | async-start | bytes 2506752 | tf_op jit(solution)/shard_map/all_gather | solution.py:156
  273.0 2.2 copy-start.5
  274.9 2.7 copy-start
  277.6 1.3 copy-start.2
  280.0 4.3 %collective-permute-start.11 = (bf16[16,32,1024]{2,1,0:T(8,128)(2,1)}, bf16[16,32,1024]{2,1,0:T(8,128)(2,1)S(1)}, u32[]{:S(2)}, u32[]{:S(2)}) collective-permute-start(bf16[16,32,1024]{2,1,0:T(8,128)(2,1)} %select_bitcast_fusion), channel_id=1, source_target_pairs={{0,8},{8,0},{1,9},{9,1},{2,10},{10,2},{3,11},{11,3},{4,12},{12,4},... | collective-permute-start | bytes 3145736 | tf_op jit(solution)/shard_map/ppermute | solution.py:70
  281.5 1.5 collective-permute-start.12
  287.8 28.1 %all-to-all-start.3 = ((bf16[16,33,1024]{2,1,0:T(8,128)(2,1)}), bf16[16,33,1024]{2,1,0:T(8,128)(2,1)S(1)}, u32[]{:S(2)}, u32[]{:S(2)}) async-start(bf16[16,33,1024]{2,1,0:T(8,128)(2,1)} %pad_maximum_fusion.2), calls=%async_computation.5 | async-start | bytes 2621440 | tf_op jit(solution)/shard_map/all_to_all | solution.py:170
  297.2 3.3 %copy-start.1 = (bf16[8,128,1024]{2,1,0:T(8,128)(2,1)S(1)}, bf16[8,128,1024]{2,1,0:T(8,128)(2,1)}, u32[]{:S(2)}) copy-start(bf16[8,128,1024]{2,1,0:T(8,128)(2,1)} %copy-done) | copy-start | bytes 6291460
  (1 other events, 0.7 us)
Sparse Core Ops, SparseCore 0:
  42.1 40.6 reduce-scatter.2
  88.5 39.1 all-gather.4
  190.5 36.9 reduce-scatter.4
  232.4 40.5 all-gather.6

commit v11 on v10

--- a/solution.py
+++ b/solution.py
@@ -61,18 +61,21 @@
     return pair.reshape((-1,) + value.shape[1:])
 
 
-def pair_rows(value):
+def pair_rows(left, product):
     chips = lax.axis_size("chip")
-    parts = value.reshape((chips, 2, -1) + value.shape[1:])
+    parts = left.reshape((chips, 2, -1) + left.shape[1:])
     first = lax.axis_index("core") == 0
-    keep = jnp.where(first, parts[:, 0], parts[:, 1])
-    give = jnp.where(first, parts[:, 1], parts[:, 0])
+    keep_in = jnp.where(first, parts[:, 0], parts[:, 1]).reshape((-1,) + left.shape[1:])
+    give_in = jnp.where(first, parts[:, 1], parts[:, 0]).reshape((-1,) + left.shape[1:])
+    give = product(give_in).astype(jnp.bfloat16)
     got = lax.ppermute(give, "core", [(0, 1), (1, 0)])
-    return (keep.astype(jnp.float32) + got.astype(jnp.float32)).astype(jnp.bfloat16)
-
-
-def sum_rows(value):
-    received = lax.all_to_all(pair_rows(value), "chip", 0, 0, tiled=False)
+    keep = product(keep_in).astype(jnp.bfloat16)
+    pair = keep.astype(jnp.float32) + got.astype(jnp.float32)
+    return pair.astype(jnp.bfloat16).reshape((chips, -1) + pair.shape[1:])
+
+
+def sum_rows(left, product):
+    received = lax.all_to_all(pair_rows(left, product), "chip", 0, 0, tiled=False)
     return jnp.sum(received.astype(jnp.float32), axis=0)
 
 
@@ -134,8 +137,9 @@
     active_own = activate(hidden_own).astype(jnp.bfloat16)
     active_full = lax.all_gather(active_own, "blk", axis=0, tiled=True)
 
-    out_part = jnp.dot(active_full, w2, preferred_element_type=jnp.float32)
-    outputs = sum_rows(out_part.astype(jnp.bfloat16)).astype(jnp.bfloat16)
+    outputs = sum_rows(
+        active_full, lambda rows: jnp.dot(rows, w2, preferred_element_type=jnp.float32)
+    ).astype(jnp.bfloat16)
     residual = (outputs.astype(jnp.float32) - target.astype(jnp.float32)).astype(jnp.bfloat16)
     error_full = gather_rows(residual)
 
@@ -159,10 +163,12 @@
     slope_full = slope_rows[:, :-1].reshape(-1, slope_own.shape[1])
     curvature_blk = jnp.sum(join_three(slope_rows[:, -1, :3]))
 
-    in_part = lax.dot_general(
-        slope_full, w1, (((1,), (1,)), ((), ())), preferred_element_type=jnp.float32
-    )
-    in_rows = pair_rows(in_part.astype(jnp.bfloat16))
+    in_rows = pair_rows(
+        slope_full,
+        lambda rows: lax.dot_general(
+            rows, w1, (((1,), (1,)), ((), ())), preferred_element_type=jnp.float32
+        ),
+    )
     curvature_chip = curvature_blk + lax.ppermute(curvature_blk, "core", [(0, 1), (1, 0)])
     extra = jnp.zeros((in_rows.shape[0], 1, features), jnp.bfloat16).at[:, 0, :3].set(
         split_three(curvature_chip)[None]

time: 327 us -> 326 us (level)
  other arithmetic: 26.2 us -> 21.4 us
    dot_general x2 -> x4, matrix products: 6.91 us -> 7.91 us  [the longest x2 5.4 us: body(): lax.dot_general(rows, w1, (((1,), (1,)), ((), ())), preferred_element_typ...]
  transfers between devices with their start and end apart: 19 -> 19, of which waited for: 17 -> 16; matrix products, arithmetic and copies ran while one was open for 12% -> 12% of each run, Pallas kernels for 0% -> 0%
where the time goes in v11:
time: 326 us; the launch traced here: 324 us
  waiting for transfers between devices  151 us (46%)
  blocking collectives  43.7 us (13%)
  starting transfers between devices  31.9 us (10%)
  local copies, waits for them, and re-layouts  30 us (9%)
  matrix products  24.2 us (7%)
  between operations  22.7 us (7%)
  other arithmetic  21.4 us (7%)
    all_gather x1, waiting for transfers between devices, body(): lax.all_gather(with_row(slope_own, split_three(curvature_part)), 'blk', a...  40.6 us
    all_gather x1, waiting for transfers between devices, body(): active_full = lax.all_gather(active_own, 'blk', axis=0, tiled=True)  38.5 us
    all_to_all x1, blocking collectives, sum_rows(): lax.all_to_all(pair_rows(left, product), 'chip', 0, 0, tiled=False)  24.1 us
    reduce_scatter x1, waiting for transfers between devices, body(): lax.psum_scatter(back_part.astype(jnp.bfloat16), 'blk', scatter_dimension...  23 us
    all_to_all x1, blocking collectives, gather_rows(): mine = lax.all_to_all(spread, 'chip', 0, 0, tiled=False)  19.5 us
    ppermute x8, waiting for transfers between devices, butterfly_sum(): lax.ppermute(value, axis, [(i, i ^ step) for i in range(size)])  18.7 us
    all_to_all x1, waiting for transfers between devices, gather_rows(): mine = lax.all_to_all(spread, 'chip', 0, 0, tiled=False)  17.6 us
    ppermute x8, starting transfers between devices, butterfly_sum(): lax.ppermute(value, axis, [(i, i ^ step) for i in range(size)])  17.1 us
  transfers between devices with their start and end apart: 19, of which 16 were waited for; matrix products, arithmetic and copies ran while one was open for 12% of the time, Pallas kernels for 0%

profile of v11, /device:TPU:32, one launch (start us, length us, event | category | flops | bytes accessed | tf_op | source)
XLA Modules:
  0.0 324.5 jit_solution(9153554988454920634)
XLA Ops:
  7.2 1.9 broadcast_in_dim.148
  9.1 7.0 %all-to-all-start = ((bf16[16,32,1024]{2,1,0:T(8,128)(2,1)}), bf16[16,32,1024]{2,1,0:T(8,128)(2,1)S(1)}, u32[]{:S(2)}, u32[]{:S(2)}) async-start(bf16[16,32,1024]{2,1,0:T(8,128)(2,1)} %broadcast_in_dim.148), calls=%async_computation | async-start | bytes 2097152 | tf_op jit(solution)/shard_map/all_to_all | solution.py:57
  16.3 17.6 %all-to-all-done = bf16[16,32,1024]{2,1,0:T(8,128)(2,1)S(1)} async-done(((bf16[16,32,1024]{2,1,0:T(8,128)(2,1)}), bf16[16,32,1024]{2,1,0:T(8,128)(2,1)S(1)}, u32[]{:S(2)}, u32[]{:S(2)}) %all-to-all-start) | async-done | bytes 1048608 | tf_op jit(solution)/shard_map/all_to_all | solution.py:57
  38.8 3.7 %fusion.12 = bf16[1024,1024]{1,0:T(8,128)(2,1)} fusion(bf16[1024,1024]{1,0:T(8,128)(2,1)S(1)} %bitcast.166, bf16[128,8,8,128]{3,2,1,0:T(8,128)(2,1)S(1)} %bitcast.173), kind=kOutput, calls=%fused_computation.24 | convolution fusion | flops 2148532224 | bytes 6291456 | tf_op jit(solution)/shard_map/dot_general | solution.py:131
  45.6 3.5 %collective-permute-done.1 = f32[1025]{0:T(1024)S(1)} collective-permute-done((f32[1025]{0:T(1024)S(1)}, f32[1025]{0:T(1024)S(1)}, u32[]{:S(2)}, u32[]{:S(2)}) %collective-permute-start.1) | collective-permute-done | bytes 4132 | tf_op jit(solution)/shard_map/ppermute | solution.py:49
  49.8 3.4 %collective-permute-start.2 = (f32[1025]{0:T(1024)S(1)}, f32[1025]{0:T(1024)S(1)}, u32[]{:S(2)}, u32[]{:S(2)}) collective-permute-start(f32[1025]{0:T(1024)S(1)} %fusion.63), channel_id=1, source_target_pairs={{0,2},{1,3},{2,0},{3,1},{4,6},{5,7},{6,4},{7,5},{8,10},{9,11},{10,... | collective-permute-start | bytes 12308 | tf_op jit(solution)/shard_map/ppermute | solution.py:49
  54.8 6.0 %collective-permute-start.3 = (f32[1025]{0:T(1024)S(1)}, f32[1025]{0:T(1024)S(1)}, u32[]{:S(2)}, u32[]{:S(2)}) collective-permute-start(f32[1025]{0:T(1024)S(1)} %add.135), channel_id=1, source_target_pairs={{0,4},{1,5},{2,6},{3,7},{4,0},{5,1},{6,2},{7,3},{8,12},{9,13},{10,... | collective-permute-start | bytes 12308 | tf_op jit(solution)/shard_map/ppermute | solution.py:49
  66.3 2.0 collective-permute-start.5
  70.7 2.1 collective-permute-start.6
  72.8 3.1 collective-permute-done.6
  78.0 2.3 collective-permute-done.7
  80.9 2.0 collective-permute-start.8
  82.9 3.3 %collective-permute-done.8 = f32[1]{0:T(128)} collective-permute-done((f32[1]{0:T(128)}, f32[1]{0:T(128)}, u32[]{:S(2)}, u32[]{:S(2)}) %collective-permute-start.8) | collective-permute-done | bytes 36 | tf_op jit(solution)/shard_map/ppermute | solution.py:49
  90.4 38.5 %all-gather.5.cloned.1.call-done = bf16[1024,1024]{1,0:T(8,128)(2,1)} async-done(((bf16[128,1024]{1,0:T(8,128)(2,1)}), bf16[1024,1024]{1,0:T(8,128)(2,1)}) %all-gather.5.cloned.1.call-update) | async-done | bytes 2097168 | tf_op jit(solution)/shard_map/all_gather | solution.py:138
  132.1 2.6 collective-permute-done.9
  136.0 24.1 %all_to_all.20 = bf16[16,32,1024]{2,1,0:T(8,128)(2,1)S(1)} all-to-all(bf16[16,32,1024]{2,1,0:T(8,128)(2,1)S(1)} %bitcast.189), channel_id=1, replica_groups=mesh['chip'=16,'core'=2,'blk'=8] {'chip'}, dimensions={0} | all-to-all | bytes 2097152 | tf_op jit(solution)/shard_map/all_to_all | solution.py:78
  160.6 19.5 %all_to_all.21 = bf16[16,32,1024]{2,1,0:T(8,128)(2,1)S(1)} all-to-all(bf16[16,32,1024]{2,1,0:T(8,128)(2,1)S(1)} %broadcast_in_dim.172), channel_id=1, replica_groups=mesh['chip'=16,'core'=2,'blk'=8] {'chip'}, dimensions={0} | all-to-all | bytes 2097152 | tf_op jit(solution)/shard_map/all_to_all | solution.py:57
  180.1 2.7 collective-permute-done.10
  185.4 3.7 %fusion.15 = bf16[1024,1024]{1,0:T(8,128)(2,1)} fusion(bf16[1024,1024]{1,0:T(8,128)(2,1)S(1)} %bitcast.170, bf16[128,8,8,128]{3,2,1,0:T(8,128)(2,1)S(1)} %bitcast.178), kind=kOutput, calls=%fused_computation.25 | convolution fusion | flops 2148532224 | bytes 6291456 | tf_op jit(solution)/shard_map/dot_general | solution.py:146
  190.8 2.6 copy.100
  193.3 4.1 %copy.88 = bf16[1024,1024]{1,0:T(8,128)(2,1)} copy(bf16[1024,1024]{0,1:T(8,128)(2,1)} %bitcast.171) | data formatting | bytes 4194304 | tf_op jit(solution)/shard_map/dot_general | solution.py:152
  197.5 4.0 %convolution_bitcast_fusion.1 = f32[8,8,128,128]{3,2,1,0:T(8,128)S(1)} fusion(bf16[8,128,1024,1]{2,1,3,0:T(8,128)(2,1)} %bitcast.181, bf16[8,128,1024,1]{2,1,0,3:T(8,128)(2,1)S(1)} %bitcast.180), kind=kOutput, calls=%fused_computation.4 | convolution fusion | flops 2147483648 | bytes 8388608 | tf_op jit(solution)/shard_map/dot_general | solution.py:152
  203.5 23.0 %reduce-scatter.5.cloned.1.call-done = bf16[128,1024]{1,0:T(8,128)(2,1)} async-done(((bf16[1024,1024]{1,0:T(8,128)(2,1)}), bf16[128,1024]{1,0:T(8,128)(2,1)}) %reduce-scatter.5.cloned.1.call-update) | async-done | bytes 262160 | tf_op jit(solution)/shard_map/reduce_scatter | solution.py:149
  231.3 40.6 %all-gather.7.cloned.1.call-done = bf16[8,129,1024]{2,1,0:T(8,128)(2,1)} async-done(((bf16[1,129,1024]{2,1,0:T(8,128)(2,1)}), bf16[8,129,1024]{2,1,0:T(8,128)(2,1)}) %all-gather.7.cloned.1.call-update) | async-done | bytes 2113552 | tf_op jit(solution)/shard_map/all_gather | solution.py:160
  275.4 2.3 fusion.27
  282.0 3.1 add_convert_fusion
  286.4 6.8 %all-to-all-start.3 = ((bf16[16,33,1024]{2,1,0:T(8,128)(2,1)}), bf16[16,33,1024]{2,1,0:T(8,128)(2,1)S(1)}, u32[]{:S(2)}, u32[]{:S(2)}) async-start(bf16[16,33,1024]{2,1,0:T(8,128)(2,1)} %pad_maximum_fusion.2), calls=%async_computation.5 | async-start | bytes 2621440 | tf_op jit(solution)/shard_map/all_to_all | solution.py:176
  293.2 4.0 %copy.91 = bf16[1024,1024]{1,0:T(8,128)(2,1)} copy(bf16[1024,1024]{0,1:T(8,128)(2,1)} %bitcast.167) | data formatting | bytes 4194304 | tf_op jit(solution)/shard_map/dot_general | solution.py:184
  297.9 2.5 copy.95
  300.4 2.6 copy.92
  303.0 4.6 %convolution_bitcast_fusion = f32[8,8,128,128]{3,2,1,0:T(8,128)S(1)} fusion(bf16[8,128,1024,1]{2,1,3,0:T(8,128)(2,1)} %bitcast.179, bf16[8,128,1024,1]{2,1,0,3:T(8,128)(2,1)} %bitcast.182), kind=kOutput, calls=%fused_computation.3 | convolution fusion | flops 2147483648 | bytes 8388608 | tf_op jit(solution)/shard_map/dot_general | solution.py:184
  308.6 5.8 %all-to-all-done.3 = bf16[16,33,1024]{2,1,0:T(8,128)(2,1)S(1)} async-done(((bf16[16,33,1024]{2,1,0:T(8,128)(2,1)}), bf16[16,33,1024]{2,1,0:T(8,128)(2,1)S(1)}, u32[]{:S(2)}, u32[]{:S(2)}) %all-to-all-start.3) | async-done | bytes 1081376 | tf_op jit(solution)/shard_map/all_to_all | solution.py:176
  (117 shorter events, 46.6 us)
Async XLA Ops:
  7.2 9.0 %copy-start.13 = (s32[8,1]{0,1:T(1,128)S(1)}, s32[8,1]{0,1:T(1,128)}, u32[]{:S(2)}) copy-start(s32[8,1]{0,1:T(1,128)} %param.17) | copy-start | bytes 100
  9.1 24.7 %all-to-all-start = ((bf16[16,32,1024]{2,1,0:T(8,128)(2,1)}), bf16[16,32,1024]{2,1,0:T(8,128)(2,1)S(1)}, u32[]{:S(2)}, u32[]{:S(2)}) async-start(bf16[16,32,1024]{2,1,0:T(8,128)(2,1)} %broadcast_in_dim.148), calls=%async_computation | async-start | bytes 2097152 | tf_op jit(solution)/shard_map/all_to_all | solution.py:57
  16.2 71.4 %reduce-scatter.3.cloned.1.call-start = ((), (), s32[]{:S(2)}) async-start(), calls=%async_computation.6 | async-start | bytes 2359296 | tf_op jit(solution)/shard_map/reduce_scatter | solution.py:132
  33.9 3.0 collective-permute-start
  35.2 1.2 copy-start.12
  36.8 1.3 copy-start.3
  37.2 1.6 copy-start
  42.5 47.3 %copy-start.9 = (bf16[8,128,128]{2,1,0:T(8,128)(2,1)S(1)}, bf16[8,128,128]{2,1,0:T(8,128)(2,1)}, u32[]{:S(2)}) copy-start(bf16[8,128,128]{2,1,0:T(8,128)(2,1)} %get-tuple-element.63) | copy-start | bytes 786436
  42.5 86.4 %all-gather.5.cloned.1.call-start = ((), (), s32[]{:S(2)}) async-start(), calls=%async_computation.7 | async-start | bytes 2359296 | tf_op jit(solution)/shard_map/all_gather | solution.py:138
  45.4 3.7 %collective-permute-start.1 = (f32[1025]{0:T(1024)S(1)}, f32[1025]{0:T(1024)S(1)}, u32[]{:S(2)}, u32[]{:S(2)}) collective-permute-start(f32[1025]{0:T(1024)S(1)} %pad_maximum_fusion.3), channel_id=1, source_target_pairs={{0,1},{1,0},{2,3},{3,2},{4,5},{5,4},{6,7},{7,6},{8,9},{9,8},{10,11... | collective-permute-start | bytes 12308 | tf_op jit(solution)/shard_map/ppermute | solution.py:49
  49.8 5.0 %collective-permute-start.2 = (f32[1025]{0:T(1024)S(1)}, f32[1025]{0:T(1024)S(1)}, u32[]{:S(2)}, u32[]{:S(2)}) collective-permute-start(f32[1025]{0:T(1024)S(1)} %fusion.63), channel_id=1, source_target_pairs={{0,2},{1,3},{2,0},{3,1},{4,6},{5,7},{6,4},{7,5},{8,10},{9,11},{10,... | collective-permute-start | bytes 12308 | tf_op jit(solution)/shard_map/ppermute | solution.py:49
  54.8 7.7 %collective-permute-start.3 = (f32[1025]{0:T(1024)S(1)}, f32[1025]{0:T(1024)S(1)}, u32[]{:S(2)}, u32[]{:S(2)}) collective-permute-start(f32[1025]{0:T(1024)S(1)} %add.135), channel_id=1, source_target_pairs={{0,4},{1,5},{2,6},{3,7},{4,0},{5,1},{6,2},{7,3},{8,12},{9,13},{10,... | collective-permute-start | bytes 12308 | tf_op jit(solution)/shard_map/ppermute | solution.py:49
  63.7 1.4 collective-permute-start.4
  66.3 3.7 %collective-permute-start.5 = (f32[1]{0:T(128)}, f32[1]{0:T(128)}, u32[]{:S(2)}, u32[]{:S(2)}) collective-permute-start(f32[1]{0:T(128)} %add.137), channel_id=1, source_target_pairs={{0,16},{8,24},{16,0},{24,8},{32,48},{40,56},{48,32},{56,40},{64,80... | collective-permute-start | bytes 20 | tf_op jit(solution)/shard_map/ppermute | solution.py:49
  70.7 5.2 %collective-permute-start.6 = (f32[1]{0:T(128)}, f32[1]{0:T(128)}, u32[]{:S(2)}, u32[]{:S(2)}) collective-permute-start(f32[1]{0:T(128)} %add.138), channel_id=1, source_target_pairs={{0,32},{8,40},{16,48},{24,56},{32,0},{40,8},{48,16},{56,24},{64,96... | collective-permute-start | bytes 20 | tf_op jit(solution)/shard_map/ppermute | solution.py:49
  76.6 3.7 %collective-permute-start.7 = (f32[1]{0:T(128)}, f32[1]{0:T(128)}, u32[]{:S(2)}, u32[]{:S(2)}) collective-permute-start(f32[1]{0:T(128)} %add.139), channel_id=1, source_target_pairs={{0,64},{8,72},{16,80},{24,88},{32,96},{40,104},{48,112},{56,120},{... | collective-permute-start | bytes 20 | tf_op jit(solution)/shard_map/ppermute | solution.py:49
  80.9 5.2 %collective-permute-start.8 = (f32[1]{0:T(128)}, f32[1]{0:T(128)}, u32[]{:S(2)}, u32[]{:S(2)}) collective-permute-start(f32[1]{0:T(128)} %add.140), channel_id=1, source_target_pairs={{0,128},{8,136},{16,144},{24,152},{32,160},{40,168},{48,176},{56,1... | collective-permute-start | bytes 20 | tf_op jit(solution)/shard_map/ppermute | solution.py:49
  89.5 137.0 %reduce-scatter.5.cloned.1.call-start = ((), (), s32[]{:S(2)}) async-start(), calls=%async_computation.8 | async-start | bytes 2359296 | tf_op jit(solution)/shard_map/reduce_scatter | solution.py:149
  90.4 44.4 %copy-start.5 = (bf16[8,128,8,128]{3,2,1,0:T(8,128)(2,1)}, bf16[8,128,8,128]{3,2,1,0:T(8,128)(2,1)S(1)}, u32[]{:S(2)}) copy-start(bf16[8,128,8,128]{3,2,1,0:T(8,128)(2,1)S(1)} %select_add_fusion) | copy-start | bytes 6291460
  131.8 2.9 collective-permute-start.9
  136.0 24.4 %copy-start.11 = (bf16[32,1024]{1,0:T(8,128)(2,1)S(1)}, bf16[32,1024]{1,0:T(8,128)(2,1)}, u32[]{:S(2)}) copy-start(bf16[32,1024]{1,0:T(8,128)(2,1)} %param.12) | copy-start | bytes 196612
  160.4 22.5 %copy-start.10 = (bf16[32,1024]{1,0:T(8,128)(2,1)}, bf16[32,1024]{1,0:T(8,128)(2,1)S(1)}, u32[]{:S(2)}) copy-start(bf16[32,1024]{1,0:T(8,128)(2,1)S(1)} %reduce_sum.86) | copy-start | bytes 196612
  180.1 2.7 collective-permute-start.10
  183.1 2.3 copy-start.6
  183.4 1.4 copy-start.2
  189.2 1.6 copy-start.1
  189.2 82.7 %all-gather.7.cloned.1.call-start = ((), (), s32[]{:S(2)}) async-start(), calls=%async_computation.9 | async-start | bytes 2506752 | tf_op jit(solution)/shard_map/all_gather | solution.py:160
  193.3 4.1 %copy-start.7 = (bf16[1024,1024]{1,0:T(8,128)(2,1)S(1)}, bf16[1024,1024]{1,0:T(8,128)(2,1)}, u32[]{:S(2)}) copy-start(bf16[1024,1024]{1,0:T(8,128)(2,1)} %copy.100) | copy-start | bytes 6291460
  273.8 1.6 copy-start.4
  277.6 4.4 %collective-permute-start.11 = (bf16[512,1024]{1,0:T(8,128)(2,1)}, bf16[512,1024]{1,0:T(8,128)(2,1)}, u32[]{:S(2)}, u32[]{:S(2)}) collective-permute-start(bf16[512,1024]{1,0:T(8,128)(2,1)} %fusion.27), channel_id=1, source_target_pairs={{0,8},{8,0},{1,9},{9,1},{2,10},{10,2},{3,11},{11,3},{4,12},{12,4},... | collective-permute-start | bytes 3145736 | tf_op jit(solution)/shard_map/ppermute | solution.py:71
  279.1 1.6 collective-permute-start.12
  286.4 28.0 %all-to-all-start.3 = ((bf16[16,33,1024]{2,1,0:T(8,128)(2,1)}), bf16[16,33,1024]{2,1,0:T(8,128)(2,1)S(1)}, u32[]{:S(2)}, u32[]{:S(2)}) async-start(bf16[16,33,1024]{2,1,0:T(8,128)(2,1)} %pad_maximum_fusion.2), calls=%async_computation.5 | async-start | bytes 2621440 | tf_op jit(solution)/shard_map/all_to_all | solution.py:176
  (1 other events, 0.7 us)
Sparse Core Ops, SparseCore 0:
  42.6 40.4 reduce-scatter.2
  89.6 39.2 all-gather.4
  189.3 37.1 reduce-scatter.4
  231.4 40.4 all-gather.6

commit v12 on v11

--- a/solution.py
+++ b/solution.py
@@ -59,6 +59,20 @@
     first = lax.axis_index("core") == 0
     pair = jnp.stack([jnp.where(first, mine, other), jnp.where(first, other, mine)], 1)
     return pair.reshape((-1,) + value.shape[1:])
+
+
+def gather_halves(value):
+    chips = lax.axis_size("chip")
+    spread = jnp.broadcast_to(value[None], (chips,) + value.shape)
+    mine = lax.all_to_all(spread, "chip", 0, 0, tiled=False)
+    other = lax.ppermute(mine, "core", [(0, 1), (1, 0)])
+    return mine, other
+
+
+def order_pair(mine, other):
+    first = lax.axis_index("core") == 0
+    pair = jnp.stack([jnp.where(first, mine, other), jnp.where(first, other, mine)], 1)
+    return pair.reshape((-1,) + mine.shape[2:])
 
 
 def pair_rows(left, product):
@@ -114,7 +128,8 @@
     image_part = jnp.einsum(
         "jsk,jskn->jn", chosen, tiles_in.astype(jnp.float32), precision=lax.Precision.HIGHEST
     )
-    x_full = gather_rows(tokens)
+    x_mine, x_other = gather_halves(tokens)
+    x_full = order_pair(x_mine, x_other)
     image_and_norm = butterfly_sum(
         jnp.concatenate([image_part.reshape(-1), jnp.sum(probe_vector * probe_vector)[None]]), "blk"
     )
@@ -128,7 +143,9 @@
         spread_tiles(tiles_out, row_index, feature_blocks), (2, 1, 0, 3)
     ).reshape(hidden_width, features)
 
-    pre_part = jnp.dot(x_full, w1, preferred_element_type=jnp.float32)
+    pre_mine = jnp.dot(x_mine, w1, preferred_element_type=jnp.float32)
+    pre_other = jnp.dot(x_other, w1, preferred_element_type=jnp.float32)
+    pre_part = order_pair(pre_mine, pre_other)
     pre_own = lax.psum_scatter(
         pre_part.astype(jnp.bfloat16), "blk", scatter_dimension=0, tiled=True
     ).astype(jnp.float32)

time: 326 us -> 331 us (1.015)
  waiting for transfers between devices: 151 us -> 147 us
  other arithmetic: 21.4 us -> 24.9 us
    another operation x2 -> x5, other arithmetic: 1.36 us -> 6.42 us  [the longest x3 5.06 us: order_pair(): jnp.stack([jnp.where(first, mine, other), jnp.where(first, other, mine)], 1)]
    unnamed x34 -> x36, local copies, waits for them, and re-layouts: 9.01 us -> 7.25 us
  transfers between devices with their start and end apart: 19 -> 19, of which waited for: 16 -> 16; matrix products, arithmetic and copies ran while one was open for 12% -> 14% of each run, Pallas kernels for 0% -> 0%
where the time goes in v12:
time: 331 us; the launch traced here: 330 us
  waiting for transfers between devices  147 us (44%)
  blocking collectives  43.7 us (13%)
  local copies, waits for them, and re-layouts  33.2 us (10%)
  starting transfers between devices  32.2 us (10%)
  matrix products  26.2 us (8%)
  other arithmetic  24.9 us (8%)
  between operations  22.7 us (7%)
    all_gather x1, waiting for transfers between devices, body(): lax.all_gather(with_row(slope_own, split_three(curvature_part)), 'blk', a...  40.7 us
    all_gather x1, waiting for transfers between devices, body(): active_full = lax.all_gather(active_own, 'blk', axis=0, tiled=True)  38.3 us
    all_to_all x1, blocking collectives, sum_rows(): lax.all_to_all(pair_rows(left, product), 'chip', 0, 0, tiled=False)  24.1 us
    reduce_scatter x1, waiting for transfers between devices, body(): lax.psum_scatter(back_part.astype(jnp.bfloat16), 'blk', scatter_dimension...  22.8 us
    all_to_all x1, blocking collectives, gather_rows(): mine = lax.all_to_all(spread, 'chip', 0, 0, tiled=False)  19.5 us
    ppermute x8, waiting for transfers between devices, butterfly_sum(): lax.ppermute(value, axis, [(i, i ^ step) for i in range(size)])  17.8 us
    all_to_all x1, waiting for transfers between devices, gather_halves(): mine = lax.all_to_all(spread, 'chip', 0, 0, tiled=False)  17.4 us
    ppermute x8, starting transfers between devices, butterfly_sum(): lax.ppermute(value, axis, [(i, i ^ step) for i in range(size)])  17.2 us
  transfers between devices with their start and end apart: 19, of which 16 were waited for; matrix products, arithmetic and copies ran while one was open for 14% of the time, Pallas kernels for 0%

profile of v12, /device:TPU:32, one launch (start us, length us, event | category | flops | bytes accessed | tf_op | source)
XLA Modules:
  0.0 329.9 jit_solution(6769953846279835779)
XLA Ops:
  9.2 7.1 %all-to-all-start = ((bf16[16,32,1024]{2,1,0:T(8,128)(2,1)}), bf16[16,32,1024]{2,1,0:T(8,128)(2,1)}, u32[]{:S(2)}, u32[]{:S(2)}) async-start(bf16[16,32,1024]{2,1,0:T(8,128)(2,1)} %broadcast_in_dim.159), calls=%async_computation | async-start | bytes 2097152 | tf_op jit(solution)/shard_map/all_to_all | solution.py:67
  16.7 17.4 %all-to-all-done = bf16[16,32,1024]{2,1,0:T(8,128)(2,1)} async-done(((bf16[16,32,1024]{2,1,0:T(8,128)(2,1)}), bf16[16,32,1024]{2,1,0:T(8,128)(2,1)}, u32[]{:S(2)}, u32[]{:S(2)}) %all-to-all-start) | async-done | bytes 1048608 | tf_op jit(solution)/shard_map/all_to_all | solution.py:67
  34.8 2.6 reshape.343
  37.5 3.3 fusion.61
  40.8 2.5 fusion.34
  48.1 3.5 %collective-permute-done.1 = f32[1025]{0:T(1024)S(1)} collective-permute-done((f32[1025]{0:T(1024)S(1)}, f32[1025]{0:T(1024)S(1)}, u32[]{:S(2)}, u32[]{:S(2)}) %collective-permute-start.1) | collective-permute-done | bytes 4132 | tf_op jit(solution)/shard_map/ppermute | solution.py:49
  52.3 3.4 %collective-permute-start.2 = (f32[1025]{0:T(1024)S(1)}, f32[1025]{0:T(1024)S(1)}, u32[]{:S(2)}, u32[]{:S(2)}) collective-permute-start(f32[1025]{0:T(1024)S(1)} %fusion.59), channel_id=1, source_target_pairs={{0,2},{1,3},{2,0},{3,1},{4,6},{5,7},{6,4},{7,5},{8,10},{9,11},{10,... | collective-permute-start | bytes 12308 | tf_op jit(solution)/shard_map/ppermute | solution.py:49
  57.3 6.0 %collective-permute-start.3 = (f32[1025]{0:T(1024)S(1)}, f32[1025]{0:T(1024)S(1)}, u32[]{:S(2)}, u32[]{:S(2)}) collective-permute-start(f32[1025]{0:T(1024)S(1)} %add.132), channel_id=1, source_target_pairs={{0,4},{1,5},{2,6},{3,7},{4,0},{5,1},{6,2},{7,3},{8,12},{9,13},{10,... | collective-permute-start | bytes 12308 | tf_op jit(solution)/shard_map/ppermute | solution.py:49
  72.9 2.1 collective-permute-start.6
  75.1 2.9 collective-permute-done.6
  80.1 2.2 collective-permute-done.7
  84.9 3.1 collective-permute-done.8
  92.4 38.3 %all-gather.5.cloned.1.call-done = bf16[1024,1024]{1,0:T(8,128)(2,1)} async-done(((bf16[128,1024]{1,0:T(8,128)(2,1)}), bf16[1024,1024]{1,0:T(8,128)(2,1)}) %all-gather.5.cloned.1.call-update) | async-done | bytes 2097168 | tf_op jit(solution)/shard_map/all_gather | solution.py:155
  133.7 2.6 collective-permute-done.9
  137.7 24.1 %all_to_all.20 = bf16[16,32,1024]{2,1,0:T(8,128)(2,1)S(1)} all-to-all(bf16[16,32,1024]{2,1,0:T(8,128)(2,1)S(1)} %bitcast.196), channel_id=1, replica_groups=mesh['chip'=16,'core'=2,'blk'=8] {'chip'}, dimensions={0} | all-to-all | bytes 2097152 | tf_op jit(solution)/shard_map/all_to_all | solution.py:92
  162.2 19.5 %all_to_all.21 = bf16[16,32,1024]{2,1,0:T(8,128)(2,1)S(1)} all-to-all(bf16[16,32,1024]{2,1,0:T(8,128)(2,1)S(1)} %broadcast_in_dim.172), channel_id=1, replica_groups=mesh['chip'=16,'core'=2,'blk'=8] {'chip'}, dimensions={0} | all-to-all | bytes 2097152 | tf_op jit(solution)/shard_map/all_to_all | solution.py:57
  181.7 2.7 collective-permute-done.10
  184.4 3.1 select_bitcast_fusion.1
  190.0 3.7 %fusion.10 = bf16[1024,1024]{1,0:T(8,128)(2,1)} fusion(bf16[1024,1024]{1,0:T(8,128)(2,1)S(1)} %bitcast.179, bf16[128,8,8,128]{3,2,1,0:T(8,128)(2,1)S(1)} %bitcast.185), kind=kOutput, calls=%fused_computation.25 | convolution fusion | flops 2148532224 | bytes 6291456 | tf_op jit(solution)/shard_map/dot_general | solution.py:163
  195.3 2.7 copy.100
  198.0 4.1 %copy.87 = bf16[1024,1024]{1,0:T(8,128)(2,1)} copy(bf16[1024,1024]{0,1:T(8,128)(2,1)} %bitcast.180) | data formatting | bytes 4194304 | tf_op jit(solution)/shard_map/dot_general | solution.py:169
  202.1 4.0 %convolution_bitcast_fusion.1 = f32[8,8,128,128]{3,2,1,0:T(8,128)S(1)} fusion(bf16[8,128,1024,1]{2,1,3,0:T(8,128)(2,1)} %bitcast.188, bf16[8,128,1024,1]{2,1,0,3:T(8,128)(2,1)S(1)} %bitcast.187), kind=kOutput, calls=%fused_computation.4 | convolution fusion | flops 2147483648 | bytes 8388608 | tf_op jit(solution)/shard_map/dot_general | solution.py:169
  208.2 22.8 %reduce-scatter.5.cloned.1.call-done = bf16[128,1024]{1,0:T(8,128)(2,1)} async-done(((bf16[1024,1024]{1,0:T(8,128)(2,1)}), bf16[128,1024]{1,0:T(8,128)(2,1)}) %reduce-scatter.5.cloned.1.call-update) | async-done | bytes 262160 | tf_op jit(solution)/shard_map/reduce_scatter | solution.py:166
  235.8 40.7 %all-gather.7.cloned.1.call-done = bf16[8,129,1024]{2,1,0:T(8,128)(2,1)} async-done(((bf16[1,129,1024]{2,1,0:T(8,128)(2,1)}), bf16[8,129,1024]{2,1,0:T(8,128)(2,1)}) %all-gather.7.cloned.1.call-update) | async-done | bytes 2113552 | tf_op jit(solution)/shard_map/all_gather | solution.py:177
  279.9 2.2 fusion.27
  287.2 3.1 add_convert_fusion
  291.6 6.8 %all-to-all-start.3 = ((bf16[16,33,1024]{2,1,0:T(8,128)(2,1)}), bf16[16,33,1024]{2,1,0:T(8,128)(2,1)S(1)}, u32[]{:S(2)}, u32[]{:S(2)}) async-start(bf16[16,33,1024]{2,1,0:T(8,128)(2,1)} %pad_maximum_fusion.3), calls=%async_computation.5 | async-start | bytes 2621440 | tf_op jit(solution)/shard_map/all_to_all | solution.py:193
  301.7 4.0 %copy.91 = bf16[1024,1024]{1,0:T(8,128)(2,1)} copy(bf16[1024,1024]{0,1:T(8,128)(2,1)} %bitcast.181) | data formatting | bytes 4194304 | tf_op jit(solution)/shard_map/dot_general | solution.py:201
  305.6 2.5 copy.95
  308.2 2.6 copy.92
  310.7 4.6 %convolution_bitcast_fusion = f32[8,8,128,128]{3,2,1,0:T(8,128)S(1)} fusion(bf16[8,128,1024,1]{2,1,3,0:T(8,128)(2,1)} %bitcast.186, bf16[8,128,1024,1]{2,1,0,3:T(8,128)(2,1)} %bitcast.189), kind=kOutput, calls=%fused_computation.3 | convolution fusion | flops 2147483648 | bytes 8388608 | tf_op jit(solution)/shard_map/dot_general | solution.py:201
  316.3 3.5 %all-to-all-done.3 = bf16[16,33,1024]{2,1,0:T(8,128)(2,1)S(1)} async-done(((bf16[16,33,1024]{2,1,0:T(8,128)(2,1)}), bf16[16,33,1024]{2,1,0:T(8,128)(2,1)S(1)}, u32[]{:S(2)}, u32[]{:S(2)}) %all-to-all-start.3) | async-done | bytes 1081376 | tf_op jit(solution)/shard_map/all_to_all | solution.py:193
  (124 shorter events, 53.3 us)
Async XLA Ops:
  7.2 9.2 %copy-start.13 = (s32[8,1,2]{0,2,1:T(2,128)S(1)}, s32[8,1,2]{0,2,1:T(2,128)}, u32[]{:S(2)}) copy-start(s32[8,1,2]{0,2,1:T(2,128)} %param.16) | copy-start | bytes 196
  7.2 9.2 %copy-start.14 = (s32[8,1]{0,1:T(1,128)S(1)}, s32[8,1]{0,1:T(1,128)}, u32[]{:S(2)}) copy-start(s32[8,1]{0,1:T(1,128)} %param.17) | copy-start | bytes 100
  7.2 9.3 %copy-start.9 = (bf16[8,1,2,128,128]{4,3,2,1,0:T(8,128)(2,1)S(1)}, bf16[8,1,2,128,128]{4,3,2,1,0:T(8,128)(2,1)}, u32[]{:S(2)}) copy-start(bf16[8,1,2,128,128]{4,3,2,1,0:T(8,128)(2,1)} %param.15) | copy-start | bytes 1572868
  7.2 9.3 %copy-start.10 = (bf16[8,1,2,128,128]{4,3,2,1,0:T(8,128)(2,1)S(1)}, bf16[8,1,2,128,128]{4,3,2,1,0:T(8,128)(2,1)}, u32[]{:S(2)}) copy-start(bf16[8,1,2,128,128]{4,3,2,1,0:T(8,128)(2,1)} %param.14) | copy-start | bytes 1572868
  9.2 24.8 %all-to-all-start = ((bf16[16,32,1024]{2,1,0:T(8,128)(2,1)}), bf16[16,32,1024]{2,1,0:T(8,128)(2,1)}, u32[]{:S(2)}, u32[]{:S(2)}) async-start(bf16[16,32,1024]{2,1,0:T(8,128)(2,1)} %broadcast_in_dim.159), calls=%async_computation | async-start | bytes 2097152 | tf_op jit(solution)/shard_map/all_to_all | solution.py:67
  16.3 73.0 %reduce-scatter.3.cloned.1.call-start = ((), (), s32[]{:S(2)}) async-start(), calls=%async_computation.6 | async-start | bytes 2359296 | tf_op jit(solution)/shard_map/reduce_scatter | solution.py:149
  34.1 6.7 %collective-permute-start = (bf16[16,32,1024]{2,1,0:T(8,128)(2,1)}, bf16[16,32,1024]{2,1,0:T(8,128)(2,1)}, u32[]{:S(2)}, u32[]{:S(2)}) collective-permute-start(bf16[16,32,1024]{2,1,0:T(8,128)(2,1)} %all-to-all-done), channel_id=1, source_target_pairs={{0,8},{8,0},{1,9},{9,1},{2,10},{10,2},{3,11},{11,3},{4,12},{12,4},... | collective-permute-start | bytes 3145736 | tf_op jit(solution)/shard_map/ppermute | solution.py:68
  34.8 2.7 copy-start
  37.5 3.3 copy-start.6
  45.0 85.7 %all-gather.5.cloned.1.call-start = ((), (), s32[]{:S(2)}) async-start(), calls=%async_computation.7 | async-start | bytes 2359296 | tf_op jit(solution)/shard_map/all_gather | solution.py:155
  47.9 3.7 %collective-permute-start.1 = (f32[1025]{0:T(1024)S(1)}, f32[1025]{0:T(1024)S(1)}, u32[]{:S(2)}, u32[]{:S(2)}) collective-permute-start(f32[1025]{0:T(1024)S(1)} %pad_maximum_fusion.4), channel_id=1, source_target_pairs={{0,1},{1,0},{2,3},{3,2},{4,5},{5,4},{6,7},{7,6},{8,9},{9,8},{10,11... | collective-permute-start | bytes 12308 | tf_op jit(solution)/shard_map/ppermute | solution.py:49
  52.3 5.0 %collective-permute-start.2 = (f32[1025]{0:T(1024)S(1)}, f32[1025]{0:T(1024)S(1)}, u32[]{:S(2)}, u32[]{:S(2)}) collective-permute-start(f32[1025]{0:T(1024)S(1)} %fusion.59), channel_id=1, source_target_pairs={{0,2},{1,3},{2,0},{3,1},{4,6},{5,7},{6,4},{7,5},{8,10},{9,11},{10,... | collective-permute-start | bytes 12308 | tf_op jit(solution)/shard_map/ppermute | solution.py:49
  57.3 7.7 %collective-permute-start.3 = (f32[1025]{0:T(1024)S(1)}, f32[1025]{0:T(1024)S(1)}, u32[]{:S(2)}, u32[]{:S(2)}) collective-permute-start(f32[1025]{0:T(1024)S(1)} %add.132), channel_id=1, source_target_pairs={{0,4},{1,5},{2,6},{3,7},{4,0},{5,1},{6,2},{7,3},{8,12},{9,13},{10,... | collective-permute-start | bytes 12308 | tf_op jit(solution)/shard_map/ppermute | solution.py:49
  66.1 1.2 collective-permute-start.4
  68.6 3.6 %collective-permute-start.5 = (f32[1]{0:T(128)}, f32[1]{0:T(128)}, u32[]{:S(2)}, u32[]{:S(2)}) collective-permute-start(f32[1]{0:T(128)} %add.134), channel_id=1, source_target_pairs={{0,16},{8,24},{16,0},{24,8},{32,48},{40,56},{48,32},{56,40},{64,80... | collective-permute-start | bytes 20 | tf_op jit(solution)/shard_map/ppermute | solution.py:49
  72.9 5.1 %collective-permute-start.6 = (f32[1]{0:T(128)}, f32[1]{0:T(128)}, u32[]{:S(2)}, u32[]{:S(2)}) collective-permute-start(f32[1]{0:T(128)} %add.135), channel_id=1, source_target_pairs={{0,32},{8,40},{16,48},{24,56},{32,0},{40,8},{48,16},{56,24},{64,96... | collective-permute-start | bytes 20 | tf_op jit(solution)/shard_map/ppermute | solution.py:49
  78.7 3.6 %collective-permute-start.7 = (f32[1]{0:T(128)}, f32[1]{0:T(128)}, u32[]{:S(2)}, u32[]{:S(2)}) collective-permute-start(f32[1]{0:T(128)} %add.136), channel_id=1, source_target_pairs={{0,64},{8,72},{16,80},{24,88},{32,96},{40,104},{48,112},{56,120},{... | collective-permute-start | bytes 20 | tf_op jit(solution)/shard_map/ppermute | solution.py:49
  82.9 5.1 %collective-permute-start.8 = (f32[1]{0:T(128)}, f32[1]{0:T(128)}, u32[]{:S(2)}, u32[]{:S(2)}) collective-permute-start(f32[1]{0:T(128)} %add.137), channel_id=1, source_target_pairs={{0,128},{8,136},{16,144},{24,152},{32,160},{40,168},{48,176},{56,1... | collective-permute-start | bytes 20 | tf_op jit(solution)/shard_map/ppermute | solution.py:49
  91.3 139.7 %reduce-scatter.5.cloned.1.call-start = ((), (), s32[]{:S(2)}) async-start(), calls=%async_computation.8 | async-start | bytes 2359296 | tf_op jit(solution)/shard_map/reduce_scatter | solution.py:166
  92.4 44.0 %copy-start.4 = (bf16[8,128,8,128]{3,2,1,0:T(8,128)(2,1)}, bf16[8,128,8,128]{3,2,1,0:T(8,128)(2,1)S(1)}, u32[]{:S(2)}) copy-start(bf16[8,128,8,128]{3,2,1,0:T(8,128)(2,1)S(1)} %select_add_fusion) | copy-start | bytes 6291460
  133.6 2.7 collective-permute-start.9
  137.7 24.4 %copy-start.12 = (bf16[32,1024]{1,0:T(8,128)(2,1)S(1)}, bf16[32,1024]{1,0:T(8,128)(2,1)}, u32[]{:S(2)}) copy-start(bf16[32,1024]{1,0:T(8,128)(2,1)} %param.12) | copy-start | bytes 196612
  162.0 25.5 %copy-start.11 = (bf16[32,1024]{1,0:T(8,128)(2,1)}, bf16[32,1024]{1,0:T(8,128)(2,1)S(1)}, u32[]{:S(2)}) copy-start(bf16[32,1024]{1,0:T(8,128)(2,1)S(1)} %reduce_sum.86) | copy-start | bytes 196612
  181.7 2.7 collective-permute-start.10
  187.7 2.3 copy-start.5
  193.7 1.6 copy-start.2
  193.8 82.7 %all-gather.7.cloned.1.call-start = ((), (), s32[]{:S(2)}) async-start(), calls=%async_computation.9 | async-start | bytes 2506752 | tf_op jit(solution)/shard_map/all_gather | solution.py:177
  198.0 4.1 %copy-start.7 = (bf16[1024,1024]{1,0:T(8,128)(2,1)S(1)}, bf16[1024,1024]{1,0:T(8,128)(2,1)}, u32[]{:S(2)}) copy-start(bf16[1024,1024]{1,0:T(8,128)(2,1)} %copy.100) | copy-start | bytes 6291460
  278.3 1.6 copy-start.1
  282.2 5.0 %collective-permute-start.11 = (bf16[512,1024]{1,0:T(8,128)(2,1)}, bf16[512,1024]{1,0:T(8,128)(2,1)}, u32[]{:S(2)}, u32[]{:S(2)}) collective-permute-start(bf16[512,1024]{1,0:T(8,128)(2,1)} %fusion.27), channel_id=1, source_target_pairs={{0,8},{8,0},{1,9},{9,1},{2,10},{10,2},{3,11},{11,3},{4,12},{12,4},... | collective-permute-start | bytes 3145736 | tf_op jit(solution)/shard_map/ppermute | solution.py:85
  284.2 1.6 collective-permute-start.12
  291.6 28.2 %all-to-all-start.3 = ((bf16[16,33,1024]{2,1,0:T(8,128)(2,1)}), bf16[16,33,1024]{2,1,0:T(8,128)(2,1)S(1)}, u32[]{:S(2)}, u32[]{:S(2)}) async-start(bf16[16,33,1024]{2,1,0:T(8,128)(2,1)} %pad_maximum_fusion.3), calls=%async_computation.5 | async-start | bytes 2621440 | tf_op jit(solution)/shard_map/all_to_all | solution.py:193
  (2 other events, 2.1 us)
Sparse Core Ops, SparseCore 0:
  45.1 40.3 reduce-scatter.2
  91.4 39.2 all-gather.4
  193.9 37.0 reduce-scatter.4
  235.9 40.5 all-gather.6
